TPU v7x, 256 devices: a whole 4x4x8 slice. The times are simulated.
256 devices in a mesh: freq: 32 (over x, y, core), beam: 8 (over z).
Axes of the slice: x: 4, y: 4, z: 8, core: 2. Of those that a mesh axis runs over, the one named last changes fastest.
Arguments:
- block_samples: bfloat16 [8, 2048, 256], P('beam', 'freq'), may hold values from -6 to 6
- tail_samples: bfloat16 [8, 2048, 2048], P('beam', 'freq'), may hold values from -6 to 6
- tail_blocks: int32 [8], P('beam'), may hold values from 1 to 16, as said below
- dm_limit: int32 [8], P('beam'), may hold values from 256 to 2048, as said below
Outputs:
- peak_snr: float32 [8, 7, 2048], P('beam', None, 'freq')
- excess_snr: float32 [8, 7, 2048], P('beam', None, 'freq')
Inputs may be any that keep to these rules, and one draw needn't show every extreme that they name: `tail_blocks`: some beam has a full tail in every draw. `dm_limit`: some beam searches all trials in every draw.
All inputs are finite; a program needn't handle non-finite values.
Results may differ from a plain program's by a relative error of at most 0.0003.
Values sent between devices are 32-bit elements; how exact they have to be, the bound alone decides.
No kernel may reach another device: no remote copies, remote signals or barrier semaphores. Data moves between devices by JAX's collectives and lax.ppermute only.
A program may use at most 64 MiB of HBM per device.

v0:
```python
import jax
import jax.numpy as jnp
import numpy as np
from jax import lax
from jax.experimental import pallas as pl
from jax.experimental.pallas import tpu as pltpu
from jax.sharding import PartitionSpec as P

WIDTHS = 7


def partner_2(block, axis, stride):
    count = lax.axis_size(axis)
    route = []
    for low in range(count):
        high = low | 1 << stride
        if high != low and high < count:
            route += [(low, high), (high, low)]
    return lax.ppermute(block, axis, route)


def skew_rows(series, step_size, base_shift, pad_width):
    dims_of = series.shape
    rows_count = dims_of[-2]
    length_now = dims_of[-1]
    flattened = series.reshape((-1, rows_count, length_now))
    padded = jnp.pad(flattened, ((0, 0), (0, 0), (pad_width, 0)))
    row_width = length_now + pad_width
    lined_up = padded.reshape((flattened.shape[0], rows_count * row_width))
    lined_up = jnp.pad(lined_up, ((0, 0), (0, pad_width)))
    window = lax.dynamic_slice_in_dim(
        lined_up, pad_width - base_shift, rows_count * (row_width - step_size), axis=1
    )
    moved_rows = window.reshape((flattened.shape[0], rows_count, row_width - step_size))[
        :, :, :length_now
    ]
    return moved_rows.reshape(dims_of)


def tree_section(series, offset, reach_max):
    upper_rows = series[..., 0::2, :, :]
    odd_rows = series[..., 1::2, :, :]
    even_moved = skew_rows(odd_rows, 1, (offset + 1) // 2, reach_max)
    odd_moved = skew_rows(odd_rows, 1, (offset + 2) // 2, reach_max)
    joined_rows = jnp.stack([upper_rows + even_moved, upper_rows + odd_moved], axis=-2)
    dims_of = upper_rows.shape
    return joined_rows.reshape(dims_of[:-2] + (2 * dims_of[-2], dims_of[-1]))


def peak_ratios(series, tail_len):
    searched = series[..., tail_len:]
    average = jnp.mean(searched, axis=-1, keepdims=True)
    deviation = jnp.sqrt(jnp.mean((searched - average) ** 2, axis=-1, keepdims=True) + 1e-05)
    reach_back = 2 ** (WIDTHS - 1)
    boxcar = series[..., tail_len - reach_back :]
    results = []
    for width_bit in range(WIDTHS):
        width_now = 2**width_bit
        if width_bit > 0:
            half_width = width_now // 2
            pad_spec = [(0, 0)] * (series.ndim - 1) + [(half_width, 0)]
            boxcar = boxcar + jnp.pad(boxcar[..., :-half_width], pad_spec)
        ratio = (boxcar[..., reach_back:] - width_now * average) / (
            jnp.sqrt(jnp.float32(width_now)) * deviation
        )
        results.append(jnp.max(ratio, axis=-1))
    return jnp.stack(results, axis=-2)


def shift_in(row_block, amount, lanes, rows_vary):
    if rows_vary:
        moved = pltpu.roll(row_block, amount, 1, stride=1, stride_axis=0)
        limit = lax.broadcasted_iota(jnp.int32, row_block.shape, 0) + amount
    else:
        moved = pltpu.roll(row_block, amount, 1)
        limit = amount
    return jnp.where(lanes >= limit, moved, jnp.float32(0.0))


def tree_in_place(buf, subbands, trials, first_trial):
    length = buf.shape[1]
    while subbands > 1:
        half = subbands // 2
        lanes = lax.broadcasted_iota(jnp.int32, (half, length), 1)
        for k in range(trials):
            top = k * subbands
            upper = buf[top : top + half, :]
            lower = buf[top + half : top + subbands, :]
            buf[top : top + half, :] = upper + shift_in(lower, first_trial + k, lanes, False)
            buf[top + half : top + subbands, :] = upper + shift_in(
                lower, first_trial + k + 1, lanes, False
            )
        subbands = half
        trials = 2 * trials
        first_trial = 2 * first_trial


def bit_reversed(count):
    bits = count.bit_length() - 1
    return np.array([int(format(i, f"0{bits}b")[::-1], 2) for i in range(count)], np.int32)


def local_tree(joined):
    beams_dev, rows, length = joined.shape

    def body(x_ref, o_ref):
        o_ref[...] = x_ref[...]
        tree_in_place(o_ref, rows, 1, 0)

    spec = pl.BlockSpec((None, rows, length), lambda b: (b, 0, 0))
    return pl.pallas_call(
        body,
        grid=(beams_dev,),
        in_specs=[spec],
        out_specs=spec,
        out_shape=jax.ShapeDtypeStruct(joined.shape, jnp.float32),
    )(joined)


def merge_tree(parts, first_trial):
    beams_dev, subbands, trials, length = parts.shape
    rows = subbands * trials
    order = bit_reversed(subbands)
    laid = jnp.swapaxes(parts[:, order], 1, 2).reshape(beams_dev, rows, length)

    def body(off_ref, x_ref, o_ref):
        o_ref[...] = x_ref[...]
        tree_in_place(o_ref, subbands, trials, off_ref[0])

    spec = pl.BlockSpec((None, rows, length), lambda b: (b, 0, 0))
    return pl.pallas_call(
        body,
        grid=(beams_dev,),
        in_specs=[pl.BlockSpec(memory_space=pltpu.SMEM), spec],
        out_specs=spec,
        out_shape=jax.ShapeDtypeStruct((beams_dev, rows, length), jnp.float32),
    )(jnp.reshape(first_trial, (1,)).astype(jnp.int32), laid)


def local(block_samples, tail_samples, tail_blocks, dm_limit):
    beams_dev, local_chan, block_len = block_samples.shape
    tail_len = tail_samples.shape[2]
    valid_mask = (
        jnp.arange(tail_len, dtype=jnp.int32)[None, None, :]
        >= tail_len - 128 * tail_blocks[:, None, None]
    )
    joined = jnp.concatenate(
        [
            jnp.where(valid_mask, tail_samples.astype(jnp.float32), jnp.float32(0.0)),
            block_samples.astype(jnp.float32),
        ],
        axis=-1,
    )
    joined = joined[:, bit_reversed(local_chan)]
    series = local_tree(joined)[:, None]
    devices = lax.axis_size("freq")
    position = lax.axis_index("freq")
    series = lax.all_to_all(series, "freq", split_axis=2, concat_axis=1, tiled=True)
    per_dev = series.shape[2]
    dm_rows = merge_tree(series, position * per_dev)
    scores = peak_ratios(dm_rows, tail_len)
    out_rows = scores.shape[-1]
    trial_ids = position * out_rows + jnp.arange(out_rows, dtype=jnp.int32)
    peak_snr = jnp.where(
        trial_ids[None, None, :] < dm_limit[:, None, None], scores, jnp.float32(0.0)
    )
    beam_total = lax.psum(jnp.sum(peak_snr, axis=0), "beam")
    excess_snr = peak_snr - beam_total[None] / (beams_dev * lax.axis_size("beam"))
    return (peak_snr, excess_snr)


def solution(mesh):
    return jax.shard_map(
        local,
        mesh=mesh,
        in_specs=(P("beam", "freq", None), P("beam", "freq", None), P("beam"), P("beam")),
        out_specs=(P("beam", None, "freq"), P("beam", None, "freq")),
        check_vma=False,
    )
```

profile of v0, /device:TPU:8, one launch (start us, length us, event | category | flops | bytes accessed | tf_op | source)
XLA Modules:
  0.0 68.2 jit_solution(6408857761636337353)
XLA Ops:
  1.3 0.0 copy-start.1
  1.3 0.8 %convert_element_type.19 = f32[1,64,256]{2,1,0:T(8,128)S(1)} convert(bf16[1,64,256]{2,1,0:T(8,128)(2,1)} %param.8) | non-fusion elementwise | flops 16384 | bytes 98304 | tf_op jit(solution)/shard_map/convert_element_type | solution.py:150
  2.1 0.0 copy-done.1
  2.1 1.0 %convert_select_fusion = f32[1,64,2048]{2,1,0:T(8,128)S(1)} fusion(bf16[1,64,2048]{2,1,0:T(8,128)(2,1)} %param.9, pred[2048]{0:T(1024)(128)(4,1)S(1)} %iota_compare_fusion), kind=kLoop, calls=%fused_computation.3 | loop fusion | flops 262144 | bytes 788480 | tf_op jit(solution)/shard_map/jit(_where)/select_n | solution.py:149
  3.1 1.6 %gather_fusion = f32[64,2304]{1,0:T(8,128)} fusion(f32[64,2304]{1,0:T(8,128)S(1)} %maximum_bitcast_fusion, s32[1024]{0:T(1024)S(1)} %pad_clamp_fusion.1), kind=kCustom, calls=%fused_computation | custom fusion | bytes 1179904 | tf_op jit(solution)/shard_map/gather | solution.py:154
  4.7 4.4 %shard_map.95 = f32[1,64,2304]{2,1,0:T(8,128)} custom-call(f32[1,64,2304]{2,1,0:T(8,128)} %bitcast.36), custom_call_target="tpu_custom_call" | custom-call | tf_op jit(solution)/shard_map/pallas_call | solution.py:111
  9.1 2.5 %copy.15 = f32[1,1,64,2304]{3,1,0,2:T(1,128)} copy(f32[1,1,64,2304]{3,2,1,0:T(8,128)} %bitcast.35) | data formatting | bytes 1179648 | tf_op jit(solution)/shard_map/broadcast_in_dim | solution.py:155
  11.6 7.5 %all-to-all-start = ((f32[1,1,64,2304]{3,1,0,2:T(1,128)}), f32[1,1,64,2304]{3,1,0,2:T(1,128)S(1)}, u32[]{:S(2)}, u32[]{:S(2)}) async-start(f32[1,1,64,2304]{3,1,0,2:T(1,128)} %copy.15), calls=%async_computation | async-start | bytes 1179648 | tf_op jit(solution)/shard_map/all_to_all | solution.py:158
  19.8 0.0 copy-start
  19.8 0.6 copy-done
  20.4 9.4 %all-to-all-done = f32[1,1,64,2304]{3,1,0,2:T(1,128)S(1)} async-done(((f32[1,1,64,2304]{3,1,0,2:T(1,128)}), f32[1,1,64,2304]{3,1,0,2:T(1,128)S(1)}, u32[]{:S(2)}, u32[]{:S(2)}) %all-to-all-start) | async-done | bytes 589856 | tf_op jit(solution)/shard_map/all_to_all | solution.py:158
  29.9 1.4 %reduce.9 = f32[64,2304]{1,0:T(8,128)S(1)} reduce(f32[1,1,64,2304]{3,1,0,2:T(1,128)S(1)} %all-to-all-done, f32[]{:T(128)} %constant.91), dimensions={0,1}, to_apply=%all_to_all.4.reduce_sub_computation | reduce | bytes 1179652 | tf_op jit(solution)/shard_map/all_to_all | solution.py:158
  31.3 0.3 reshape.336
  31.6 1.2 %gather_fusion.1 = f32[32,2,2304]{2,1,0:T(2,128)S(1)} fusion(f32[32,2,2304]{2,1,0:T(2,128)S(1)} %reshape.336, s32[1024]{0:T(1024)S(1)} %pad_clamp_fusion), kind=kCustom, calls=%fused_computation.1 | custom fusion | bytes 1179776 | tf_op jit(solution)/shard_map/gather | solution.py:124
  32.8 0.8 %copy.16 = f32[1,2,32,2304]{3,2,1,0:T(8,128)} copy(f32[1,2,32,2304]{3,1,2,0:T(2,128)S(1)} %bitcast.33) | data formatting | bytes 1179648 | tf_op jit(solution)/shard_map/transpose | solution.py:124
  33.6 7.2 %shard_map.96 = f32[1,64,2304]{2,1,0:T(8,128)} custom-call(s32[1]{0:T(128)} %bitcast.1.off_ref, f32[1,64,2304]{2,1,0:T(8,128)} %bitcast.34), custom_call_target="tpu_custom_call" | custom-call | tf_op jit(solution)/shard_map/pallas_call | solution.py:131
  40.9 1.0 %slice.65 = f32[1,64,319]{2,1,0:T(8,128)S(1)} slice(f32[1,64,2304]{2,1,0:T(8,128)} %shard_map.96), slice={[0:1], [0:64], [1984:2303]} | slice | bytes 163328 | tf_op jit(solution)/shard_map/slice | solution.py:62
  41.9 0.9 %slice_reduce_fusion = f32[64]{0:T(128)S(1)} fusion(f32[1,64,2304]{2,1,0:T(8,128)} %shard_map.96), kind=kLoop, calls=%fused_computation.30 | loop fusion | flops 16320 | bytes 65792 | tf_op jit(solution)/shard_map/reduce_sum | solution.py:52
  42.8 1.0 %slice_add_fusion = f32[1,64,320]{2,1,0:T(8,128)S(1)} fusion(f32[1,64,2304]{2,1,0:T(8,128)} %shard_map.96, f32[1,64,319]{2,1,0:T(8,128)S(1)} %slice.65), kind=kLoop, calls=%fused_computation.4 | loop fusion | flops 20480 | bytes 245504 | tf_op jit(solution)/shard_map/add | solution.py:62
  43.8 0.1 pad_add_fusion.3
  43.9 0.1 pad_add_fusion.2
  44.0 0.1 pad_add_fusion.1
  44.1 0.1 pad_add_fusion
  44.2 1.0 %multiply_reduce_fusion = f32[64]{0:T(128)S(1)} fusion(f32[1,64,2304]{2,1,0:T(8,128)} %shard_map.96, f32[64]{0:T(128)S(1)} %get-tuple-element.18), kind=kLoop, calls=%fused_computation.21 | loop fusion | flops 49088 | bytes 66048 | tf_op jit(solution)/shard_map/reduce_sum | solution.py:53
  45.3 1.1 %divide_reduce_fusion = (f32[64]{0:T(128)S(1)}, f32[64]{0:T(128)S(1)}) fusion(f32[1,64,2304]{2,1,0:T(8,128)} %shard_map.96, f32[64]{0:T(128)S(1)} %get-tuple-element.11, f32[64]{0:T(128)S(1)} %get-tuple-element.18, f32[64]{0:T(128)S(1)} %get-tuple-element.23, f32[64]{0:T(128)S(1)} %get-tuple-element.17, f32[1,64,320]{2,1,0:T(8,128)S(1)} %slice_add_fusion), kind=kLoop, calls=%fused_computation.22 | loop fusion | flops 98176 | bytes 132608 | tf_op jit(solution)/shard_map/reduce_max | solution.py:66
  46.4 0.2 fusion.8
  46.6 0.3 fusion.11
  47.0 20.0 %psum.7 = f32[7,64]{1,0:T(8,128)S(1)} all-reduce(f32[7,64]{1,0:T(8,128)S(1)} %broadcast_select_fusion), channel_id=1, replica_groups=mesh['freq'=32,'beam'=8] {'beam'}, use_global_device_ids=true, to_apply=%region_9.10 | all-reduce | flops 448 | bytes 3584 | tf_op jit(solution)/shard_map/psum | solution.py:167
  67.0 0.6 copy.18
  67.6 0.6 copy.17
  (13 shorter events, 0.2 us)
Async XLA Ops:
  1.3 0.8 %copy-start.1 = (s32[64]{0:T(128)S(1)}, s32[64]{0:T(128)}, u32[]{:S(2)}) copy-start(s32[64]{0:T(128)} %constant.89) | copy-start | bytes 772
  11.6 18.3 %all-to-all-start = ((f32[1,1,64,2304]{3,1,0,2:T(1,128)}), f32[1,1,64,2304]{3,1,0,2:T(1,128)S(1)}, u32[]{:S(2)}, u32[]{:S(2)}) async-start(f32[1,1,64,2304]{3,1,0,2:T(1,128)} %copy.15), calls=%async_computation | async-start | bytes 1179648 | tf_op jit(solution)/shard_map/all_to_all | solution.py:158
  19.8 0.7 copy-start
where the time goes:
time: 68.8 us; the launch traced here: 68.2 us
  blocking collectives  20 us (29%)
  Pallas kernels  11.6 us (17%)
  waiting for transfers between devices  9.41 us (14%)
  local copies, waits for them, and re-layouts  9.3 us (14%)
  other arithmetic  8.22 us (12%)
  starting transfers between devices  7.54 us (11%)
  between operations  2.1 us (3%)
    psum x1, blocking collectives, local(): beam_total = lax.psum(jnp.sum(peak_snr, axis=0), 'beam')  20 us
    all_to_all x1, waiting for transfers between devices, local(): lax.all_to_all(series, 'freq', split_axis=2, concat_axis=1, tiled=True)  9.41 us
    all_to_all x1, starting transfers between devices, local(): lax.all_to_all(series, 'freq', split_axis=2, concat_axis=1, tiled=True)  7.54 us
    pallas_call x1, Pallas kernels, merge_tree(): pl.pallas_call(body, grid=(beams_dev,), in_specs=[pl.BlockSpec(memory_spa...  7.23 us
    pallas_call x1, Pallas kernels, local_tree(): pl.pallas_call(body, grid=(beams_dev,), in_specs=[spec], out_specs=spec,...  4.36 us
    broadcast_in_dim x1, local copies, waits for them, and re-layouts, local(): series = local_tree(joined)[:, None]  2.48 us
    unnamed x6, local copies, waits for them, and re-layouts  1.81 us
    reduce_max x3, other arithmetic, peak_ratios(): results.append(jnp.max(ratio, axis=-1))  1.61 us
  transfers between devices with their start and end apart: 1, of which 1 were waited for; matrix products, arithmetic and copies ran while one was open for 0% of the time, Pallas kernels for 0%

commit v1 on v0

--- a/solution.py
+++ b/solution.py
@@ -164,7 +164,11 @@
     peak_snr = jnp.where(
         trial_ids[None, None, :] < dm_limit[:, None, None], scores, jnp.float32(0.0)
     )
-    beam_total = lax.psum(jnp.sum(peak_snr, axis=0), "beam")
+    beam_total = jnp.sum(peak_snr, axis=0)
+    beam_count = lax.axis_size("beam")
+    for level_bit in range(beam_count.bit_length() - 1):
+        pairs = [(i, i ^ (1 << level_bit)) for i in range(beam_count)]
+        beam_total = beam_total + lax.ppermute(beam_total, "beam", pairs)
     excess_snr = peak_snr - beam_total[None] / (beams_dev * lax.axis_size("beam"))
     return (peak_snr, excess_snr)
 

time: 68.8 us -> 65.2 us (0.948)
  the two profiles are of different devices: /device:TPU:8 before, /device:TPU:32 now
where the time goes in v1:
time: 65.2 us; the launch traced here: 64.5 us
  starting transfers between devices  16.9 us (26%)
  waiting for transfers between devices  16.4 us (25%)
  Pallas kernels  11.6 us (18%)
  local copies, waits for them, and re-layouts  9.3 us (14%)
  other arithmetic  8.23 us (13%)
  between operations  2.1 us (3%)
    all_to_all x1, waiting for transfers between devices, local(): lax.all_to_all(series, 'freq', split_axis=2, concat_axis=1, tiled=True)  10.3 us
    ppermute x3, starting transfers between devices, local(): beam_total = beam_total + lax.ppermute(beam_total, 'beam', pairs)  9.41 us
    all_to_all x1, starting transfers between devices, local(): lax.all_to_all(series, 'freq', split_axis=2, concat_axis=1, tiled=True)  7.5 us
    pallas_call x1, Pallas kernels, merge_tree(): pl.pallas_call(body, grid=(beams_dev,), in_specs=[pl.BlockSpec(memory_spa...  7.23 us
    ppermute x3, waiting for transfers between devices, local(): beam_total = beam_total + lax.ppermute(beam_total, 'beam', pairs)  6.05 us
    pallas_call x1, Pallas kernels, local_tree(): pl.pallas_call(body, grid=(beams_dev,), in_specs=[spec], out_specs=spec,...  4.36 us
    broadcast_in_dim x1, local copies, waits for them, and re-layouts, local(): series = local_tree(joined)[:, None]  2.48 us
    unnamed x6, local copies, waits for them, and re-layouts  1.81 us
  transfers between devices with their start and end apart: 4, of which 4 were waited for; matrix products, arithmetic and copies ran while one was open for 1% of the time, Pallas kernels for 0%

profile of v1, /device:TPU:32, one launch (start us, length us, event | category | flops | bytes accessed | tf_op | source)
XLA Modules:
  0.0 64.5 jit_solution(686676335406583891)
XLA Ops:
  1.3 0.8 %convert_element_type.19 = f32[1,64,256]{2,1,0:T(8,128)S(1)} convert(bf16[1,64,256]{2,1,0:T(8,128)(2,1)} %param.8) | non-fusion elementwise | flops 16384 | bytes 98304 | tf_op jit(solution)/shard_map/convert_element_type | solution.py:150
  2.1 1.0 %convert_select_fusion = f32[1,64,2048]{2,1,0:T(8,128)S(1)} fusion(bf16[1,64,2048]{2,1,0:T(8,128)(2,1)} %param.9, pred[2048]{0:T(1024)(128)(4,1)S(1)} %iota_compare_fusion), kind=kLoop, calls=%fused_computation.3 | loop fusion | flops 262144 | bytes 788480 | tf_op jit(solution)/shard_map/jit(_where)/select_n | solution.py:149
  3.1 1.6 %gather_fusion = f32[64,2304]{1,0:T(8,128)} fusion(f32[64,2304]{1,0:T(8,128)S(1)} %maximum_bitcast_fusion, s32[1024]{0:T(1024)S(1)} %pad_clamp_fusion.1), kind=kCustom, calls=%fused_computation | custom fusion | bytes 1179904 | tf_op jit(solution)/shard_map/gather | solution.py:154
  4.7 4.4 %shard_map.95 = f32[1,64,2304]{2,1,0:T(8,128)} custom-call(f32[1,64,2304]{2,1,0:T(8,128)} %bitcast.36), custom_call_target="tpu_custom_call" | custom-call | tf_op jit(solution)/shard_map/pallas_call | solution.py:111
  9.1 2.5 %copy.15 = f32[1,1,64,2304]{3,1,0,2:T(1,128)} copy(f32[1,1,64,2304]{3,2,1,0:T(8,128)} %bitcast.35) | data formatting | bytes 1179648 | tf_op jit(solution)/shard_map/broadcast_in_dim | solution.py:155
  11.6 7.5 %all-to-all-start = ((f32[1,1,64,2304]{3,1,0,2:T(1,128)}), f32[1,1,64,2304]{3,1,0,2:T(1,128)S(1)}, u32[]{:S(2)}, u32[]{:S(2)}) async-start(f32[1,1,64,2304]{3,1,0,2:T(1,128)} %copy.15), calls=%async_computation | async-start | bytes 1179648 | tf_op jit(solution)/shard_map/all_to_all | solution.py:158
  19.8 0.6 copy-done
  20.4 10.3 %all-to-all-done = f32[1,1,64,2304]{3,1,0,2:T(1,128)S(1)} async-done(((f32[1,1,64,2304]{3,1,0,2:T(1,128)}), f32[1,1,64,2304]{3,1,0,2:T(1,128)S(1)}, u32[]{:S(2)}, u32[]{:S(2)}) %all-to-all-start) | async-done | bytes 589856 | tf_op jit(solution)/shard_map/all_to_all | solution.py:158
  30.7 1.4 %reduce.9 = f32[64,2304]{1,0:T(8,128)S(1)} reduce(f32[1,1,64,2304]{3,1,0,2:T(1,128)S(1)} %all-to-all-done, f32[]{:T(128)} %constant.91), dimensions={0,1}, to_apply=%all_to_all.4.reduce_sub_computation | reduce | bytes 1179652 | tf_op jit(solution)/shard_map/all_to_all | solution.py:158
  32.1 0.3 reshape.336
  32.5 1.2 %gather_fusion.1 = f32[32,2,2304]{2,1,0:T(2,128)S(1)} fusion(f32[32,2,2304]{2,1,0:T(2,128)S(1)} %reshape.336, s32[1024]{0:T(1024)S(1)} %pad_clamp_fusion), kind=kCustom, calls=%fused_computation.1 | custom fusion | bytes 1179776 | tf_op jit(solution)/shard_map/gather | solution.py:124
  33.7 0.8 %copy.16 = f32[1,2,32,2304]{3,2,1,0:T(8,128)} copy(f32[1,2,32,2304]{3,1,2,0:T(2,128)S(1)} %bitcast.33) | data formatting | bytes 1179648 | tf_op jit(solution)/shard_map/transpose | solution.py:124
  34.5 7.2 %shard_map.96 = f32[1,64,2304]{2,1,0:T(8,128)} custom-call(s32[1]{0:T(128)} %bitcast.1.off_ref, f32[1,64,2304]{2,1,0:T(8,128)} %bitcast.34), custom_call_target="tpu_custom_call" | custom-call | tf_op jit(solution)/shard_map/pallas_call | solution.py:131
  41.7 1.0 %slice.65 = f32[1,64,319]{2,1,0:T(8,128)S(1)} slice(f32[1,64,2304]{2,1,0:T(8,128)} %shard_map.96), slice={[0:1], [0:64], [1984:2303]} | slice | bytes 163328 | tf_op jit(solution)/shard_map/slice | solution.py:62
  42.7 0.9 %slice_reduce_fusion = f32[64]{0:T(128)S(1)} fusion(f32[1,64,2304]{2,1,0:T(8,128)} %shard_map.96), kind=kLoop, calls=%fused_computation.30 | loop fusion | flops 16320 | bytes 65792 | tf_op jit(solution)/shard_map/reduce_sum | solution.py:52
  43.7 1.0 %slice_add_fusion = f32[1,64,320]{2,1,0:T(8,128)S(1)} fusion(f32[1,64,2304]{2,1,0:T(8,128)} %shard_map.96, f32[1,64,319]{2,1,0:T(8,128)S(1)} %slice.65), kind=kLoop, calls=%fused_computation.4 | loop fusion | flops 20480 | bytes 245504 | tf_op jit(solution)/shard_map/add | solution.py:62
  44.7 0.1 pad_add_fusion.3
  44.8 0.1 pad_add_fusion.2
  44.9 0.1 pad_add_fusion.1
  45.0 0.1 pad_add_fusion
  45.1 1.0 %multiply_reduce_fusion = f32[64]{0:T(128)S(1)} fusion(f32[1,64,2304]{2,1,0:T(8,128)} %shard_map.96, f32[64]{0:T(128)S(1)} %get-tuple-element.18), kind=kLoop, calls=%fused_computation.21 | loop fusion | flops 49088 | bytes 66048 | tf_op jit(solution)/shard_map/reduce_sum | solution.py:53
  46.2 1.1 %divide_reduce_fusion = (f32[64]{0:T(128)S(1)}, f32[64]{0:T(128)S(1)}) fusion(f32[1,64,2304]{2,1,0:T(8,128)} %shard_map.96, f32[64]{0:T(128)S(1)} %get-tuple-element.11, f32[64]{0:T(128)S(1)} %get-tuple-element.18, f32[64]{0:T(128)S(1)} %get-tuple-element.23, f32[64]{0:T(128)S(1)} %get-tuple-element.17, f32[1,64,320]{2,1,0:T(8,128)S(1)} %slice_add_fusion), kind=kLoop, calls=%fused_computation.22 | loop fusion | flops 98176 | bytes 132608 | tf_op jit(solution)/shard_map/reduce_max | solution.py:66
  47.2 0.2 fusion.8
  47.5 0.3 fusion.11
  47.8 0.2 collective-permute-start
  48.0 3.5 %collective-permute-done = f32[7,64]{1,0:T(8,128)S(1)} collective-permute-done((f32[7,64]{1,0:T(8,128)S(1)}, f32[7,64]{1,0:T(8,128)S(1)}, u32[]{:S(2)}, u32[]{:S(2)}) %collective-permute-start) | collective-permute-done | bytes 1824 | tf_op jit(solution)/shard_map/ppermute | solution.py:171
  51.5 3.3 %collective-permute-start.1 = (f32[7,64]{1,0:T(8,128)S(1)}, f32[7,64]{1,0:T(8,128)S(1)}, u32[]{:S(2)}, u32[]{:S(2)}) collective-permute-start(f32[7,64]{1,0:T(8,128)S(1)} %fusion.12), channel_id=1, source_target_pairs={{0,2},{1,3},{2,0},{3,1},{4,6},{5,7},{6,4},{7,5},{8,10},{9,11},{10,... | collective-permute-start | bytes 5384 | tf_op jit(solution)/shard_map/ppermute | solution.py:171
  54.8 1.6 %collective-permute-done.1 = f32[7,64]{1,0:T(8,128)S(1)} collective-permute-done((f32[7,64]{1,0:T(8,128)S(1)}, f32[7,64]{1,0:T(8,128)S(1)}, u32[]{:S(2)}, u32[]{:S(2)}) %collective-permute-start.1) | collective-permute-done | bytes 1824 | tf_op jit(solution)/shard_map/ppermute | solution.py:171
  56.4 5.9 %collective-permute-start.2 = (f32[7,64]{1,0:T(8,128)S(1)}, f32[7,64]{1,0:T(8,128)S(1)}, u32[]{:S(2)}, u32[]{:S(2)}) collective-permute-start(f32[7,64]{1,0:T(8,128)S(1)} %add.105), channel_id=1, source_target_pairs={{0,4},{1,5},{2,6},{3,7},{4,0},{5,1},{6,2},{7,3},{8,12},{9,13},{10,... | collective-permute-start | bytes 5384 | tf_op jit(solution)/shard_map/ppermute | solution.py:171
  62.3 0.6 copy.17
  62.9 1.0 %collective-permute-done.2 = f32[7,64]{1,0:T(8,128)S(1)} collective-permute-done((f32[7,64]{1,0:T(8,128)S(1)}, f32[7,64]{1,0:T(8,128)S(1)}, u32[]{:S(2)}, u32[]{:S(2)}) %collective-permute-start.2) | collective-permute-done | bytes 1824 | tf_op jit(solution)/shard_map/ppermute | solution.py:171
  63.9 0.6 copy.18
  (18 shorter events, 0.2 us)
Async XLA Ops:
  1.3 0.8 %copy-start.1 = (s32[64]{0:T(128)S(1)}, s32[64]{0:T(128)}, u32[]{:S(2)}) copy-start(s32[64]{0:T(128)} %constant.89) | copy-start | bytes 772
  11.6 19.1 %all-to-all-start = ((f32[1,1,64,2304]{3,1,0,2:T(1,128)}), f32[1,1,64,2304]{3,1,0,2:T(1,128)S(1)}, u32[]{:S(2)}, u32[]{:S(2)}) async-start(f32[1,1,64,2304]{3,1,0,2:T(1,128)} %copy.15), calls=%async_computation | async-start | bytes 1179648 | tf_op jit(solution)/shard_map/all_to_all | solution.py:158
  19.7 0.7 %copy-start = (s32[32]{0:T(128)S(1)}, s32[32]{0:T(128)}, u32[]{:S(2)}) copy-start(s32[32]{0:T(128)} %constant.90) | copy-start | bytes 388
  47.8 3.7 %collective-permute-start = (f32[7,64]{1,0:T(8,128)S(1)}, f32[7,64]{1,0:T(8,128)S(1)}, u32[]{:S(2)}, u32[]{:S(2)}) collective-permute-start(f32[7,64]{1,0:T(8,128)S(1)} %broadcast_select_fusion), channel_id=1, source_target_pairs={{0,1},{1,0},{2,3},{3,2},{4,5},{5,4},{6,7},{7,6},{8,9},{9,8},{10,11... | collective-permute-start | bytes 5384 | tf_op jit(solution)/shard_map/ppermute | solution.py:171
  51.5 4.9 %collective-permute-start.1 = (f32[7,64]{1,0:T(8,128)S(1)}, f32[7,64]{1,0:T(8,128)S(1)}, u32[]{:S(2)}, u32[]{:S(2)}) collective-permute-start(f32[7,64]{1,0:T(8,128)S(1)} %fusion.12), channel_id=1, source_target_pairs={{0,2},{1,3},{2,0},{3,1},{4,6},{5,7},{6,4},{7,5},{8,10},{9,11},{10,... | collective-permute-start | bytes 5384 | tf_op jit(solution)/shard_map/ppermute | solution.py:171
  56.4 7.5 %collective-permute-start.2 = (f32[7,64]{1,0:T(8,128)S(1)}, f32[7,64]{1,0:T(8,128)S(1)}, u32[]{:S(2)}, u32[]{:S(2)}) collective-permute-start(f32[7,64]{1,0:T(8,128)S(1)} %add.105), channel_id=1, source_target_pairs={{0,4},{1,5},{2,6},{3,7},{4,0},{5,1},{6,2},{7,3},{8,12},{9,13},{10,... | collective-permute-start | bytes 5384 | tf_op jit(solution)/shard_map/ppermute | solution.py:171

commit v2 on v1

--- a/solution.py
+++ b/solution.py
@@ -67,32 +67,62 @@
     return jnp.stack(results, axis=-2)
 
 
-def shift_in(row_block, amount, lanes, rows_vary):
-    if rows_vary:
-        moved = pltpu.roll(row_block, amount, 1, stride=1, stride_axis=0)
-        limit = lax.broadcasted_iota(jnp.int32, row_block.shape, 0) + amount
+def shift_in(row_block, amount, lanes, stride):
+    if stride:
+        moved = pltpu.roll(row_block, amount, 1, stride=stride, stride_axis=0)
+        limit = lax.broadcasted_iota(jnp.int32, row_block.shape, 0) * stride + amount
     else:
         moved = pltpu.roll(row_block, amount, 1)
         limit = amount
     return jnp.where(lanes >= limit, moved, jnp.float32(0.0))
 
 
-def tree_in_place(buf, subbands, trials, first_trial):
+def permute_rows(matrix, rows):
+    return jnp.dot(matrix, rows, precision=lax.Precision.HIGHEST, preferred_element_type=jnp.float32)
+
+
+def tree_in_place(buf, mid_ref, subbands, trials, first_trial, tile):
     length = buf.shape[1]
-    while subbands > 1:
+    while subbands > 1 and subbands // 2 >= tile:
         half = subbands // 2
         lanes = lax.broadcasted_iota(jnp.int32, (half, length), 1)
         for k in range(trials):
             top = k * subbands
             upper = buf[top : top + half, :]
             lower = buf[top + half : top + subbands, :]
-            buf[top : top + half, :] = upper + shift_in(lower, first_trial + k, lanes, False)
+            buf[top : top + half, :] = upper + shift_in(lower, first_trial + k, lanes, 0)
             buf[top + half : top + subbands, :] = upper + shift_in(
-                lower, first_trial + k + 1, lanes, False
+                lower, first_trial + k + 1, lanes, 0
             )
         subbands = half
         trials = 2 * trials
         first_trial = 2 * first_trial
+    buf[...] = permute_rows(mid_ref[...], buf[...])
+    groups, step = 1, 1
+    lanes = lax.broadcasted_iota(jnp.int32, (tile, length), 1)
+    if not isinstance(first_trial, int):
+        order = bit_reversed(subbands)
+        for pos in range(subbands):
+            rows = slice(pos * tile, (pos + 1) * tile)
+            buf[rows, :] = shift_in(buf[rows, :], first_trial * int(order[pos]), lanes, 0)
+        first_trial = 0
+    while subbands > 1:
+        half = subbands // 2
+        for group in range(groups):
+            for pos in range(half):
+                top = (group * subbands + pos) * tile
+                low = (group * subbands + pos + half) * tile
+                upper = buf[top : top + tile, :]
+                lower = buf[low : low + tile, :]
+                buf[top : top + tile, :] = upper + shift_in(lower, first_trial + group, lanes, step)
+                buf[low : low + tile, :] = upper + shift_in(
+                    lower, first_trial + group + 1, lanes, step
+                )
+        subbands = half
+        groups = 2 * groups
+        step = 2 * step
+        first_trial = 2 * first_trial
+    return groups
 
 
 def bit_reversed(count):
@@ -100,59 +130,89 @@
     return np.array([int(format(i, f"0{bits}b")[::-1], 2) for i in range(count)], np.int32)
 
 
-def local_tree(joined):
-    beams_dev, rows, length = joined.shape
-
-    def body(x_ref, o_ref):
-        o_ref[...] = x_ref[...]
-        tree_in_place(o_ref, rows, 1, 0)
-
-    spec = pl.BlockSpec((None, rows, length), lambda b: (b, 0, 0))
+def one_hot(targets):
+    return np.eye(len(targets), dtype=np.float32)[targets]
+
+
+def tables(subbands, trials, tile):
+    rows = subbands * trials
+    order = bit_reversed(subbands)
+    entry = one_hot([order[r % subbands] * trials + r // subbands for r in range(rows)])
+    at_switch = rows // tile
+    mid = one_hot([(r % tile) * at_switch + r // tile for r in range(rows)])
+    groups = rows // tile
+    leave = one_hot([(d % groups) * tile + d // groups for d in range(rows)])
+    return entry, mid, leave
+
+
+TILE = 8
+
+
+def local_tree(tail_samples, block_samples, tail_blocks):
+    beams_dev, rows, tail_len = tail_samples.shape
+    length = tail_len + block_samples.shape[2]
+    entry, mid, leave = tables(rows, 1, TILE)
+
+    def body(count_ref, tail_ref, block_ref, entry_ref, mid_ref, leave_ref, o_ref, buf):
+        beam = pl.program_id(0)
+        lanes = lax.broadcasted_iota(jnp.int32, (rows, tail_len), 1)
+        keep = lanes >= tail_len - 128 * count_ref[beam]
+        buf[:, :tail_len] = jnp.where(keep, tail_ref[...].astype(jnp.float32), jnp.float32(0.0))
+        buf[:, tail_len:] = block_ref[...].astype(jnp.float32)
+        buf[...] = permute_rows(entry_ref[...], buf[...])
+        tree_in_place(buf, mid_ref, rows, 1, 0, TILE)
+        o_ref[...] = permute_rows(leave_ref[...], buf[...])
+
+    table_spec = pl.BlockSpec((rows, rows), lambda b: (0, 0))
     return pl.pallas_call(
         body,
         grid=(beams_dev,),
-        in_specs=[spec],
-        out_specs=spec,
-        out_shape=jax.ShapeDtypeStruct(joined.shape, jnp.float32),
-    )(joined)
+        in_specs=[
+            pl.BlockSpec(memory_space=pltpu.SMEM),
+            pl.BlockSpec((None, rows, tail_len), lambda b: (b, 0, 0)),
+            pl.BlockSpec((None, rows, block_samples.shape[2]), lambda b: (b, 0, 0)),
+            table_spec,
+            table_spec,
+            table_spec,
+        ],
+        out_specs=pl.BlockSpec((None, rows, length), lambda b: (b, 0, 0)),
+        out_shape=jax.ShapeDtypeStruct((beams_dev, rows, length), jnp.float32),
+        scratch_shapes=[pltpu.VMEM((rows, length), jnp.float32)],
+    )(tail_blocks.astype(jnp.int32), tail_samples, block_samples, entry, mid, leave)
 
 
 def merge_tree(parts, first_trial):
     beams_dev, subbands, trials, length = parts.shape
     rows = subbands * trials
-    order = bit_reversed(subbands)
-    laid = jnp.swapaxes(parts[:, order], 1, 2).reshape(beams_dev, rows, length)
-
-    def body(off_ref, x_ref, o_ref):
-        o_ref[...] = x_ref[...]
-        tree_in_place(o_ref, subbands, trials, off_ref[0])
+    entry, mid, leave = tables(subbands, trials, TILE)
+
+    def body(off_ref, x_ref, entry_ref, mid_ref, leave_ref, o_ref, buf):
+        buf[...] = permute_rows(entry_ref[...], x_ref[...])
+        tree_in_place(buf, mid_ref, subbands, trials, off_ref[0], TILE)
+        o_ref[...] = permute_rows(leave_ref[...], buf[...])
 
     spec = pl.BlockSpec((None, rows, length), lambda b: (b, 0, 0))
+    table_spec = pl.BlockSpec((rows, rows), lambda b: (0, 0))
     return pl.pallas_call(
         body,
         grid=(beams_dev,),
-        in_specs=[pl.BlockSpec(memory_space=pltpu.SMEM), spec],
+        in_specs=[pl.BlockSpec(memory_space=pltpu.SMEM), spec, table_spec, table_spec, table_spec],
         out_specs=spec,
         out_shape=jax.ShapeDtypeStruct((beams_dev, rows, length), jnp.float32),
-    )(jnp.reshape(first_trial, (1,)).astype(jnp.int32), laid)
+        scratch_shapes=[pltpu.VMEM((rows, length), jnp.float32)],
+    )(
+        jnp.reshape(first_trial, (1,)).astype(jnp.int32),
+        parts.reshape(beams_dev, rows, length),
+        entry,
+        mid,
+        leave,
+    )
 
 
 def local(block_samples, tail_samples, tail_blocks, dm_limit):
     beams_dev, local_chan, block_len = block_samples.shape
     tail_len = tail_samples.shape[2]
-    valid_mask = (
-        jnp.arange(tail_len, dtype=jnp.int32)[None, None, :]
-        >= tail_len - 128 * tail_blocks[:, None, None]
-    )
-    joined = jnp.concatenate(
-        [
-            jnp.where(valid_mask, tail_samples.astype(jnp.float32), jnp.float32(0.0)),
-            block_samples.astype(jnp.float32),
-        ],
-        axis=-1,
-    )
-    joined = joined[:, bit_reversed(local_chan)]
-    series = local_tree(joined)[:, None]
+    series = local_tree(tail_samples, block_samples, tail_blocks)[:, None]
     devices = lax.axis_size("freq")
     position = lax.axis_index("freq")
     series = lax.all_to_all(series, "freq", split_axis=2, concat_axis=1, tiled=True)

time: 65.2 us -> 57 us (0.87)
  local copies, waits for them, and re-layouts: 9.3 us -> 5.53 us
  other arithmetic: 8.23 us -> 5 us
  Pallas kernels: 11.6 us -> 9.95 us
  waiting for transfers between devices: 16.4 us -> 17.2 us
    gather x2 -> x0, local copies, waits for them, and re-layouts: 2.79 us -> none  [the longest x1 1.6 us: local(): joined = joined[:, bit_reversed(local_chan)]]
    pallas_call x1, Pallas kernels: 7.23 us -> 5.04 us  [merge_tree(): pl.pallas_call(body, grid=(beams_dev,), in_specs=[pl.BlockSpec(memory_spa...]
    all_to_all x1 -> x0, other arithmetic: 1.4 us -> none  [local(): lax.all_to_all(series, 'freq', split_axis=2, concat_axis=1, tiled=True)]
    select_n x1 -> x0, other arithmetic: 1 us -> none  [local(): jnp.where(valid_mask, tail_samples.astype(jnp.float32), jnp.float32(0.0))]
    transpose x1 -> x0, local copies, waits for them, and re-layouts: 0.85 us -> none  [merge_tree(): laid = jnp.swapaxes(parts[:, order], 1, 2).reshape(beams_dev, rows, length)]
    all_to_all x1, waiting for transfers between devices: 10.3 us -> 11.1 us  [local(): lax.all_to_all(series, 'freq', split_axis=2, concat_axis=1, tiled=True)]
    convert_element_type x1 -> x0, other arithmetic: 0.77 us -> none  [local(): block_samples.astype(jnp.float32)]
    unnamed x6 -> x3, local copies, waits for them, and re-layouts: 1.81 us -> 2.02 us
where the time goes in v2:
time: 57 us; the launch traced here: 56.4 us
  waiting for transfers between devices  17.2 us (30%)
  starting transfers between devices  16.7 us (29%)
  Pallas kernels  9.95 us (17%)
  local copies, waits for them, and re-layouts  5.53 us (10%)
  other arithmetic  5 us (9%)
  between operations  2.04 us (4%)
    all_to_all x1, waiting for transfers between devices, local(): lax.all_to_all(series, 'freq', split_axis=2, concat_axis=1, tiled=True)  11.1 us
    ppermute x3, starting transfers between devices, local(): beam_total = beam_total + lax.ppermute(beam_total, 'beam', pairs)  9.4 us
    all_to_all x1, starting transfers between devices, local(): lax.all_to_all(series, 'freq', split_axis=2, concat_axis=1, tiled=True)  7.34 us
    ppermute x3, waiting for transfers between devices, local(): beam_total = beam_total + lax.ppermute(beam_total, 'beam', pairs)  6.06 us
    pallas_call x1, Pallas kernels, merge_tree(): pl.pallas_call(body, grid=(beams_dev,), in_specs=[pl.BlockSpec(memory_spa...  5.04 us
    pallas_call x1, Pallas kernels, local_tree(): pl.pallas_call(body, grid=(beams_dev,), in_specs=[pl.BlockSpec(memory_spa...  4.9 us
    broadcast_in_dim x1, local copies, waits for them, and re-layouts, local(): series = local_tree(tail_samples, block_samples, tail_blocks)[:, None]  2.48 us
    unnamed x3, local copies, waits for them, and re-layouts  2.02 us
  transfers between devices with their start and end apart: 4, of which 4 were waited for; matrix products, arithmetic and copies ran while one was open for 1% of the time, Pallas kernels for 0%

profile of v2, /device:TPU:32, one launch (start us, length us, event | category | flops | bytes accessed | tf_op | source)
XLA Modules:
  0.0 56.4 jit_solution(11410593053091310867)
XLA Ops:
  1.3 4.9 %shard_map.113 = f32[1,64,2304]{2,1,0:T(8,128)} custom-call(s32[1]{0:T(128)S(6)} %copy.20.count_ref, bf16[1,64,2048]{2,1,0:T(8,128)(2,1)} %tail_ref.1, bf16[1,64,256]{2,1,0:T(8,128)(2,1)} %block_ref.1, f32[64,64]{1,0:T(8,128)} %constant.55.clone.entry_ref, f32[64,64]{1,0:T(8,128)} %constant.56.clone.mid_ref.leave_ref, f32[64,64]{1,0:T(8,128)} %constant.56.clone.mid_ref.leave_ref), custom_call_target="tpu_custom_call" | custom-call | tf_op jit(solution)/shard_map/pallas_call | solution.py:167
  6.2 2.5 %copy.14 = f32[1,1,64,2304]{3,1,0,2:T(1,128)} copy(f32[1,1,64,2304]{3,2,1,0:T(8,128)} %bitcast.29) | data formatting | bytes 1179648 | tf_op jit(solution)/shard_map/broadcast_in_dim | solution.py:215
  8.7 7.3 %all-to-all-start = ((f32[1,1,64,2304]{3,1,0,2:T(1,128)}), f32[1,1,64,2304]{3,1,0,2:T(1,128)S(1)}, u32[]{:S(2)}, u32[]{:S(2)}) async-start(f32[1,1,64,2304]{3,1,0,2:T(1,128)} %copy.14), calls=%async_computation | async-start | bytes 1179648 | tf_op jit(solution)/shard_map/all_to_all | solution.py:218
  16.7 11.1 %all-to-all-done = f32[1,1,64,2304]{3,1,0,2:T(1,128)S(1)} async-done(((f32[1,1,64,2304]{3,1,0,2:T(1,128)}), f32[1,1,64,2304]{3,1,0,2:T(1,128)S(1)}, u32[]{:S(2)}, u32[]{:S(2)}) %all-to-all-start) | async-done | bytes 589856 | tf_op jit(solution)/shard_map/all_to_all | solution.py:218
  27.8 0.8 %copy.19 = f32[1,1,64,2304]{3,2,0,1:T(8,128)} copy(f32[1,1,64,2304]{3,1,0,2:T(1,128)S(1)} %all-to-all-done) | data formatting | bytes 1179648
  28.7 5.0 %shard_map.114 = f32[1,64,2304]{2,1,0:T(8,128)} custom-call(s32[1]{0:T(128)} %bitcast.1.off_ref, f32[1,64,2304]{2,1,0:T(8,128)} %bitcast.28, f32[64,64]{1,0:T(8,128)} %constant.55.clone.entry_ref, f32[64,64]{1,0:T(8,128)} %constant.56.clone.mid_ref.leave_ref, f32[64,64]{1,0:T(8,128)} %constant.56.clone.mid_ref.leave_ref), custom_call_target="tpu_custom_call" | custom-call | tf_op jit(solution)/shard_map/pallas_call | solution.py:196
  33.7 0.9 %slice_reduce_fusion = f32[64]{0:T(128)S(1)} fusion(f32[1,64,2304]{2,1,0:T(8,128)} %shard_map.114), kind=kLoop, calls=%fused_computation.27 | loop fusion | flops 16320 | bytes 65792 | tf_op jit(solution)/shard_map/reduce_sum | solution.py:52
  34.7 1.0 %slice.61 = f32[1,64,319]{2,1,0:T(8,128)S(1)} slice(f32[1,64,2304]{2,1,0:T(8,128)} %shard_map.114), slice={[0:1], [0:64], [1984:2303]} | slice | bytes 163328 | tf_op jit(solution)/shard_map/slice | solution.py:62
  35.7 1.0 %multiply_reduce_fusion = f32[64]{0:T(128)S(1)} fusion(f32[1,64,2304]{2,1,0:T(8,128)} %shard_map.114, f32[64]{0:T(128)S(1)} %get-tuple-element.16), kind=kLoop, calls=%fused_computation.18 | loop fusion | flops 49088 | bytes 66048 | tf_op jit(solution)/shard_map/reduce_sum | solution.py:53
  36.7 1.0 %slice_add_fusion = f32[1,64,320]{2,1,0:T(8,128)S(1)} fusion(f32[1,64,2304]{2,1,0:T(8,128)} %shard_map.114, f32[1,64,319]{2,1,0:T(8,128)S(1)} %slice.61), kind=kLoop, calls=%fused_computation.1 | loop fusion | flops 20480 | bytes 245504 | tf_op jit(solution)/shard_map/add | solution.py:62
  37.7 0.1 pad_add_fusion.3
  37.8 0.1 pad_add_fusion.2
  37.9 0.1 pad_add_fusion.1
  38.0 0.1 pad_add_fusion
  38.1 1.1 %divide_reduce_fusion = (f32[64]{0:T(128)S(1)}, f32[64]{0:T(128)S(1)}) fusion(f32[1,64,2304]{2,1,0:T(8,128)} %shard_map.114, f32[64]{0:T(128)S(1)} %get-tuple-element.9, f32[64]{0:T(128)S(1)} %get-tuple-element.16, f32[64]{0:T(128)S(1)} %get-tuple-element.21, f32[64]{0:T(128)S(1)} %get-tuple-element.15, f32[1,64,320]{2,1,0:T(8,128)S(1)} %slice_add_fusion), kind=kLoop, calls=%fused_computation.19 | loop fusion | flops 98176 | bytes 132608 | tf_op jit(solution)/shard_map/reduce_max | solution.py:66
  39.2 0.2 fusion.8
  39.4 0.3 fusion.11
  39.8 0.2 collective-permute-start
  40.0 3.5 %collective-permute-done = f32[7,64]{1,0:T(8,128)S(1)} collective-permute-done((f32[7,64]{1,0:T(8,128)S(1)}, f32[7,64]{1,0:T(8,128)S(1)}, u32[]{:S(2)}, u32[]{:S(2)}) %collective-permute-start) | collective-permute-done | bytes 1824 | tf_op jit(solution)/shard_map/ppermute | solution.py:231
  43.5 3.3 %collective-permute-start.1 = (f32[7,64]{1,0:T(8,128)S(1)}, f32[7,64]{1,0:T(8,128)S(1)}, u32[]{:S(2)}, u32[]{:S(2)}) collective-permute-start(f32[7,64]{1,0:T(8,128)S(1)} %fusion.12), channel_id=1, source_target_pairs={{0,2},{1,3},{2,0},{3,1},{4,6},{5,7},{6,4},{7,5},{8,10},{9,11},{10,... | collective-permute-start | bytes 5384 | tf_op jit(solution)/shard_map/ppermute | solution.py:231
  46.8 1.6 %collective-permute-done.1 = f32[7,64]{1,0:T(8,128)S(1)} collective-permute-done((f32[7,64]{1,0:T(8,128)S(1)}, f32[7,64]{1,0:T(8,128)S(1)}, u32[]{:S(2)}, u32[]{:S(2)}) %collective-permute-start.1) | collective-permute-done | bytes 1824 | tf_op jit(solution)/shard_map/ppermute | solution.py:231
  48.3 5.9 %collective-permute-start.2 = (f32[7,64]{1,0:T(8,128)S(1)}, f32[7,64]{1,0:T(8,128)S(1)}, u32[]{:S(2)}, u32[]{:S(2)}) collective-permute-start(f32[7,64]{1,0:T(8,128)S(1)} %add.89), channel_id=1, source_target_pairs={{0,4},{1,5},{2,6},{3,7},{4,0},{5,1},{6,2},{7,3},{8,12},{9,13},{10,... | collective-permute-start | bytes 5384 | tf_op jit(solution)/shard_map/ppermute | solution.py:231
  54.3 0.6 %copy.15 = f32[1,7,64]{2,0,1:T(1,128)} copy(f32[1,7,64]{2,1,0:T(8,128)S(1)} %broadcast_select_fusion.1) | data formatting | bytes 3584
  54.9 1.0 %collective-permute-done.2 = f32[7,64]{1,0:T(8,128)S(1)} collective-permute-done((f32[7,64]{1,0:T(8,128)S(1)}, f32[7,64]{1,0:T(8,128)S(1)}, u32[]{:S(2)}, u32[]{:S(2)}) %collective-permute-start.2) | collective-permute-done | bytes 1824 | tf_op jit(solution)/shard_map/ppermute | solution.py:231
  55.9 0.6 %copy.16 = f32[1,7,64]{2,0,1:T(1,128)} copy(f32[1,7,64]{2,1,0:T(8,128)S(1)} %subtract_bitcast_fusion) | data formatting | bytes 3584
  (11 shorter events, 0.1 us)
Async XLA Ops:
  8.7 19.2 %all-to-all-start = ((f32[1,1,64,2304]{3,1,0,2:T(1,128)}), f32[1,1,64,2304]{3,1,0,2:T(1,128)S(1)}, u32[]{:S(2)}, u32[]{:S(2)}) async-start(f32[1,1,64,2304]{3,1,0,2:T(1,128)} %copy.14), calls=%async_computation | async-start | bytes 1179648 | tf_op jit(solution)/shard_map/all_to_all | solution.py:218
  39.8 3.7 %collective-permute-start = (f32[7,64]{1,0:T(8,128)S(1)}, f32[7,64]{1,0:T(8,128)S(1)}, u32[]{:S(2)}, u32[]{:S(2)}) collective-permute-start(f32[7,64]{1,0:T(8,128)S(1)} %broadcast_select_fusion), channel_id=1, source_target_pairs={{0,1},{1,0},{2,3},{3,2},{4,5},{5,4},{6,7},{7,6},{8,9},{9,8},{10,11... | collective-permute-start | bytes 5384 | tf_op jit(solution)/shard_map/ppermute | solution.py:231
  43.5 4.9 %collective-permute-start.1 = (f32[7,64]{1,0:T(8,128)S(1)}, f32[7,64]{1,0:T(8,128)S(1)}, u32[]{:S(2)}, u32[]{:S(2)}) collective-permute-start(f32[7,64]{1,0:T(8,128)S(1)} %fusion.12), channel_id=1, source_target_pairs={{0,2},{1,3},{2,0},{3,1},{4,6},{5,7},{6,4},{7,5},{8,10},{9,11},{10,... | collective-permute-start | bytes 5384 | tf_op jit(solution)/shard_map/ppermute | solution.py:231
  48.3 7.5 %collective-permute-start.2 = (f32[7,64]{1,0:T(8,128)S(1)}, f32[7,64]{1,0:T(8,128)S(1)}, u32[]{:S(2)}, u32[]{:S(2)}) collective-permute-start(f32[7,64]{1,0:T(8,128)S(1)} %add.89), channel_id=1, source_target_pairs={{0,4},{1,5},{2,6},{3,7},{4,0},{5,1},{6,2},{7,3},{8,12},{9,13},{10,... | collective-permute-start | bytes 5384 | tf_op jit(solution)/shard_map/ppermute | solution.py:231

commit v3 on v2

--- a/solution.py
+++ b/solution.py
@@ -83,7 +83,7 @@
 
 def tree_in_place(buf, mid_ref, subbands, trials, first_trial, tile):
     length = buf.shape[1]
-    while subbands > 1 and subbands // 2 >= tile:
+    while subbands > 1 and trials < tile:
         half = subbands // 2
         lanes = lax.broadcasted_iota(jnp.int32, (half, length), 1)
         for k in range(trials):
@@ -134,7 +134,7 @@
     return np.eye(len(targets), dtype=np.float32)[targets]
 
 
-def tables(subbands, trials, tile):
+def tables(subbands, trials, tile, split=False):
     rows = subbands * trials
     order = bit_reversed(subbands)
     entry = one_hot([order[r % subbands] * trials + r // subbands for r in range(rows)])
@@ -142,6 +142,8 @@
     mid = one_hot([(r % tile) * at_switch + r // tile for r in range(rows)])
     groups = rows // tile
     leave = one_hot([(d % groups) * tile + d // groups for d in range(rows)])
+    if split:
+        leave = leave[np.concatenate([np.arange(0, rows, 2), np.arange(1, rows, 2)])]
     return entry, mid, leave
 
 
@@ -151,7 +153,7 @@
 def local_tree(tail_samples, block_samples, tail_blocks):
     beams_dev, rows, tail_len = tail_samples.shape
     length = tail_len + block_samples.shape[2]
-    entry, mid, leave = tables(rows, 1, TILE)
+    entry, mid, leave = tables(rows, 1, TILE, split=True)
 
     def body(count_ref, tail_ref, block_ref, entry_ref, mid_ref, leave_ref, o_ref, buf):
         beam = pl.program_id(0)
@@ -212,25 +214,27 @@
 def local(block_samples, tail_samples, tail_blocks, dm_limit):
     beams_dev, local_chan, block_len = block_samples.shape
     tail_len = tail_samples.shape[2]
-    series = local_tree(tail_samples, block_samples, tail_blocks)[:, None]
-    devices = lax.axis_size("freq")
+    series = local_tree(tail_samples, block_samples, tail_blocks)
     position = lax.axis_index("freq")
-    series = lax.all_to_all(series, "freq", split_axis=2, concat_axis=1, tiled=True)
-    per_dev = series.shape[2]
-    dm_rows = merge_tree(series, position * per_dev)
-    scores = peak_ratios(dm_rows, tail_len)
-    out_rows = scores.shape[-1]
-    trial_ids = position * out_rows + jnp.arange(out_rows, dtype=jnp.int32)
-    peak_snr = jnp.where(
-        trial_ids[None, None, :] < dm_limit[:, None, None], scores, jnp.float32(0.0)
-    )
-    beam_total = jnp.sum(peak_snr, axis=0)
     beam_count = lax.axis_size("beam")
-    for level_bit in range(beam_count.bit_length() - 1):
-        pairs = [(i, i ^ (1 << level_bit)) for i in range(beam_count)]
-        beam_total = beam_total + lax.ppermute(beam_total, "beam", pairs)
-    excess_snr = peak_snr - beam_total[None] / (beams_dev * lax.axis_size("beam"))
-    return (peak_snr, excess_snr)
+    halves = series.reshape(beams_dev, 2, local_chan // 2, series.shape[-1])
+    peak_parts, excess_parts = [], []
+    for parity in range(2):
+        part = lax.all_to_all(halves[:, parity][:, None], "freq", split_axis=2, concat_axis=1, tiled=True)
+        dm_rows = merge_tree(part, 2 * position + parity)
+        scores = peak_ratios(dm_rows, tail_len)
+        out_rows = scores.shape[-1]
+        trial_ids = (2 * position + parity) * out_rows + jnp.arange(out_rows, dtype=jnp.int32)
+        peak_snr = jnp.where(
+            trial_ids[None, None, :] < dm_limit[:, None, None], scores, jnp.float32(0.0)
+        )
+        beam_total = jnp.sum(peak_snr, axis=0)
+        for level_bit in range(beam_count.bit_length() - 1):
+            pairs = [(i, i ^ (1 << level_bit)) for i in range(beam_count)]
+            beam_total = beam_total + lax.ppermute(beam_total, "beam", pairs)
+        peak_parts.append(peak_snr)
+        excess_parts.append(peak_snr - beam_total[None] / (beams_dev * beam_count))
+    return (jnp.concatenate(peak_parts, axis=-1), jnp.concatenate(excess_parts, axis=-1))
 
 
 def solution(mesh):

time: 57 us -> 74.8 us (1.31)
  starting transfers between devices: 16.7 us -> 26 us
  other arithmetic: 5 us -> 9.17 us
  Pallas kernels: 9.95 us -> 13 us
  local copies, waits for them, and re-layouts: 5.53 us -> 7.58 us
  waiting for transfers between devices: 17.2 us -> 16 us
    ppermute x3 -> x6, starting transfers between devices: 9.4 us -> 14.8 us  [local(): beam_total = beam_total + lax.ppermute(beam_total, 'beam', pairs)]
    all_to_all x1 -> x2, starting transfers between devices: 7.34 us -> 11.2 us  [local(): lax.all_to_all(halves[:, parity][:, None], 'freq', split_axis=2, concat_a...]
    pallas_call x1 -> x2, Pallas kernels: 5.04 us -> 8.09 us  [merge_tree(): pl.pallas_call(body, grid=(beams_dev,), in_specs=[pl.BlockSpec(memory_spa...]
    unnamed x3 -> x6, local copies, waits for them, and re-layouts: 2.02 us -> 4.65 us
    broadcast_in_dim x1 -> x0, local copies, waits for them, and re-layouts: 2.48 us -> none  [local(): series = local_tree(tail_samples, block_samples, tail_blocks)[:, None]]
    reduce_max x3 -> x6, other arithmetic: 1.61 us -> 2.87 us  [peak_ratios(): results.append(jnp.max(ratio, axis=-1))]
    slice x0 -> x1, local copies, waits for them, and re-layouts: none -> 1.09 us  [local(): halves[:, parity][:, None]]
    add x5 -> x10, other arithmetic: 1.37 us -> 2.41 us  [peak_ratios(): boxcar = boxcar + jnp.pad(boxcar[..., :-half_width], pad_spec)]
  transfers between devices with their start and end apart: 4 -> 8, of which waited for: 4 -> 4; matrix products, arithmetic and copies ran while one was open for 1% -> 11% of each run, Pallas kernels for 0% -> 5%
where the time goes in v3:
time: 74.8 us; the launch traced here: 73.8 us
  starting transfers between devices  26 us (35%)
  waiting for transfers between devices  16 us (21%)
  Pallas kernels  13 us (17%)
  other arithmetic  9.17 us (12%)
  local copies, waits for them, and re-layouts  7.58 us (10%)
  between operations  2.11 us (3%)
    ppermute x6, starting transfers between devices, local(): beam_total = beam_total + lax.ppermute(beam_total, 'beam', pairs)  14.8 us
    all_to_all x2, starting transfers between devices, local(): lax.all_to_all(halves[:, parity][:, None], 'freq', split_axis=2, concat_a...  11.2 us
    all_to_all x2, waiting for transfers between devices, local(): lax.all_to_all(halves[:, parity][:, None], 'freq', split_axis=2, concat_a...  10.2 us
    pallas_call x2, Pallas kernels, merge_tree(): pl.pallas_call(body, grid=(beams_dev,), in_specs=[pl.BlockSpec(memory_spa...  8.09 us
    ppermute x6, waiting for transfers between devices, local(): beam_total = beam_total + lax.ppermute(beam_total, 'beam', pairs)  5.85 us
    pallas_call x1, Pallas kernels, local_tree(): pl.pallas_call(body, grid=(beams_dev,), in_specs=[pl.BlockSpec(memory_spa...  4.9 us
    unnamed x6, local copies, waits for them, and re-layouts  4.65 us
    reduce_max x6, other arithmetic, peak_ratios(): results.append(jnp.max(ratio, axis=-1))  2.87 us
  transfers between devices with their start and end apart: 8, of which 4 were waited for; matrix products, arithmetic and copies ran while one was open for 11% of the time, Pallas kernels for 5%

profile of v3, /device:TPU:32, one launch (start us, length us, event | category | flops | bytes accessed | tf_op | source)
XLA Modules:
  0.0 73.8 jit_solution(463833294358285409)
XLA Ops:
  1.3 4.9 %shard_map.140 = f32[1,64,2304]{2,1,0:T(8,128)} custom-call(s32[1]{0:T(128)S(6)} %copy.29.count_ref, bf16[1,64,2048]{2,1,0:T(8,128)(2,1)} %tail_ref.1, bf16[1,64,256]{2,1,0:T(8,128)(2,1)} %block_ref.1, f32[64,64]{1,0:T(8,128)} %constant.76.clone.entry_ref, f32[64,64]{1,0:T(8,128)} %constant.77.clone.mid_ref, f32[64,64]{1,0:T(8,128)} %constant.78.clone.leave_ref), custom_call_target="tpu_custom_call" | custom-call | tf_op jit(solution)/shard_map/pallas_call | solution.py:169
  6.2 1.1 %fusion.24 = (f32[1,1,32,2304]{3,2,1,0:T(8,128)S(1)}, f32[1,1,32,2304]{3,2,1,0:T(8,128)S(1)}) fusion(f32[1,2,32,2304]{3,2,1,0:T(8,128)} %bitcast.54), kind=kLoop, calls=%fused_computation.94 | loop fusion | bytes 1179648 | tf_op jit(solution)/shard_map/slice | solution.py:223
  7.3 1.0 %copy.23 = f32[1,1,32,2304]{3,1,0,2:T(1,128)} copy(f32[1,1,32,2304]{3,2,1,0:T(8,128)S(1)} %get-tuple-element.14) | data formatting | bytes 589824
  8.3 7.3 %all-to-all-start = ((f32[1,1,32,2304]{3,1,0,2:T(1,128)}), f32[1,1,32,2304]{3,1,0,2:T(1,128)S(1)}, u32[]{:S(2)}, u32[]{:S(2)}) async-start(f32[1,1,32,2304]{3,1,0,2:T(1,128)} %copy.23), calls=%async_computation | async-start | bytes 589824 | tf_op jit(solution)/shard_map/all_to_all | solution.py:223
  16.3 1.0 %copy.24 = f32[1,1,32,2304]{3,1,0,2:T(1,128)} copy(f32[1,1,32,2304]{3,2,1,0:T(8,128)S(1)} %get-tuple-element.15) | data formatting | bytes 589824
  17.3 7.5 %all-to-all-done = f32[1,1,32,2304]{3,1,0,2:T(1,128)S(1)} async-done(((f32[1,1,32,2304]{3,1,0,2:T(1,128)}), f32[1,1,32,2304]{3,1,0,2:T(1,128)S(1)}, u32[]{:S(2)}, u32[]{:S(2)}) %all-to-all-start) | async-done | bytes 294944 | tf_op jit(solution)/shard_map/all_to_all | solution.py:223
  24.8 3.9 %all-to-all-start.1 = ((f32[1,1,32,2304]{3,1,0,2:T(1,128)}), f32[1,1,32,2304]{3,1,0,2:T(1,128)S(1)}, u32[]{:S(2)}, u32[]{:S(2)}) async-start(f32[1,1,32,2304]{3,1,0,2:T(1,128)} %copy.24), calls=%async_computation.1 | async-start | bytes 589824 | tf_op jit(solution)/shard_map/all_to_all | solution.py:223
  28.7 0.7 copy.28
  29.5 4.0 %shard_map.141 = f32[1,32,2304]{2,1,0:T(8,128)} custom-call(s32[1]{0:T(128)} %bitcast.1.off_ref, f32[1,32,2304]{2,1,0:T(8,128)} %bitcast.56, f32[32,32]{1,0:T(8,128)} %constant.79.clone.entry_ref, f32[32,32]{1,0:T(8,128)} %constant.80.clone.mid_ref, f32[32,32]{1,0:T(8,128)} %constant.81.clone.leave_ref), custom_call_target="tpu_custom_call" | custom-call | tf_op jit(solution)/shard_map/pallas_call | solution.py:198
  33.5 0.9 %slice.129 = f32[1,32,319]{2,1,0:T(8,128)S(1)} slice(f32[1,32,2304]{2,1,0:T(8,128)} %shard_map.141), slice={[0:1], [0:32], [1984:2303]} | slice | bytes 81664 | tf_op jit(solution)/shard_map/slice | solution.py:62
  34.4 0.9 %slice_reduce_fusion.1 = f32[32]{0:T(128)S(1)} fusion(f32[1,32,2304]{2,1,0:T(8,128)} %shard_map.141), kind=kLoop, calls=%fused_computation.55 | loop fusion | flops 8160 | bytes 32896 | tf_op jit(solution)/shard_map/reduce_sum | solution.py:52
  35.2 2.6 %all-to-all-done.1 = f32[1,1,32,2304]{3,1,0,2:T(1,128)S(1)} async-done(((f32[1,1,32,2304]{3,1,0,2:T(1,128)}), f32[1,1,32,2304]{3,1,0,2:T(1,128)S(1)}, u32[]{:S(2)}, u32[]{:S(2)}) %all-to-all-start.1) | async-done | bytes 294944 | tf_op jit(solution)/shard_map/all_to_all | solution.py:223
  37.9 0.7 copy.27
  38.6 4.0 %shard_map.142 = f32[1,32,2304]{2,1,0:T(8,128)} custom-call(s32[1]{0:T(128)} %bitcast.10.off_ref, f32[1,32,2304]{2,1,0:T(8,128)} %bitcast.55, f32[32,32]{1,0:T(8,128)} %constant.79.clone.entry_ref, f32[32,32]{1,0:T(8,128)} %constant.80.clone.mid_ref, f32[32,32]{1,0:T(8,128)} %constant.81.clone.leave_ref), custom_call_target="tpu_custom_call" | custom-call | tf_op jit(solution)/shard_map/pallas_call | solution.py:198
  42.7 0.9 %slice.144 = f32[1,32,319]{2,1,0:T(8,128)S(1)} slice(f32[1,32,2304]{2,1,0:T(8,128)} %shard_map.142), slice={[0:1], [0:32], [1984:2303]} | slice | bytes 81664 | tf_op jit(solution)/shard_map/slice | solution.py:62
  43.5 0.9 %slice_reduce_fusion = f32[32]{0:T(128)S(1)} fusion(f32[1,32,2304]{2,1,0:T(8,128)} %shard_map.142), kind=kLoop, calls=%fused_computation.53 | loop fusion | flops 8160 | bytes 32896 | tf_op jit(solution)/shard_map/reduce_sum | solution.py:52
  44.4 0.9 %slice_add_fusion.1 = f32[1,32,320]{2,1,0:T(8,128)S(1)} fusion(f32[1,32,2304]{2,1,0:T(8,128)} %shard_map.141, f32[1,32,319]{2,1,0:T(8,128)S(1)} %slice.129), kind=kLoop, calls=%fused_computation.3 | loop fusion | flops 10240 | bytes 122752 | tf_op jit(solution)/shard_map/add | solution.py:62
  45.7 0.9 %multiply_reduce_fusion.1 = f32[32]{0:T(128)S(1)} fusion(f32[1,32,2304]{2,1,0:T(8,128)} %shard_map.141, f32[32]{0:T(128)S(1)} %get-tuple-element.22), kind=kLoop, calls=%fused_computation.37 | loop fusion | flops 24544 | bytes 33024 | tf_op jit(solution)/shard_map/reduce_sum | solution.py:53
  46.6 1.0 %divide_reduce_fusion.1 = (f32[32]{0:T(128)S(1)}, f32[32]{0:T(128)S(1)}) fusion(f32[1,32,2304]{2,1,0:T(8,128)} %shard_map.141, f32[32]{0:T(128)S(1)} %get-tuple-element.11, f32[32]{0:T(128)S(1)} %get-tuple-element.22, f32[32]{0:T(128)S(1)} %get-tuple-element.27, f32[32]{0:T(128)S(1)} %get-tuple-element.21, f32[1,32,320]{2,1,0:T(8,128)S(1)} %slice_add_fusion.1), kind=kLoop, calls=%fused_computation.39 | loop fusion | flops 49088 | bytes 66304 | tf_op jit(solution)/shard_map/reduce_max | solution.py:66
  47.8 0.3 fusion.22
  48.3 0.9 %slice_add_fusion = f32[1,32,320]{2,1,0:T(8,128)S(1)} fusion(f32[1,32,2304]{2,1,0:T(8,128)} %shard_map.142, f32[1,32,319]{2,1,0:T(8,128)S(1)} %slice.144), kind=kLoop, calls=%fused_computation.2 | loop fusion | flops 10240 | bytes 122752 | tf_op jit(solution)/shard_map/add | solution.py:62
  49.5 0.9 %multiply_reduce_fusion = f32[32]{0:T(128)S(1)} fusion(f32[1,32,2304]{2,1,0:T(8,128)} %shard_map.142, f32[32]{0:T(128)S(1)} %get-tuple-element.34), kind=kLoop, calls=%fused_computation.35 | loop fusion | flops 24544 | bytes 33024 | tf_op jit(solution)/shard_map/reduce_sum | solution.py:53
  50.5 1.0 %divide_reduce_fusion = (f32[32]{0:T(128)S(1)}, f32[32]{0:T(128)S(1)}) fusion(f32[1,32,2304]{2,1,0:T(8,128)} %shard_map.142, f32[32]{0:T(128)S(1)} %get-tuple-element.13, f32[32]{0:T(128)S(1)} %get-tuple-element.34, f32[32]{0:T(128)S(1)} %get-tuple-element.39, f32[32]{0:T(128)S(1)} %get-tuple-element.33, f32[1,32,320]{2,1,0:T(8,128)S(1)} %slice_add_fusion), kind=kLoop, calls=%fused_computation.38 | loop fusion | flops 49088 | bytes 66304 | tf_op jit(solution)/shard_map/reduce_max | solution.py:66
  51.7 0.3 fusion.23
  52.0 2.0 %collective-permute-start.3 = (f32[7,32]{1,0:T(8,128)S(1)}, f32[7,32]{1,0:T(8,128)S(1)}, u32[]{:S(2)}, u32[]{:S(2)}) collective-permute-start(f32[7,32]{1,0:T(8,128)S(1)} %broadcast_select_fusion), channel_id=1, source_target_pairs={{0,1},{1,0},{2,3},{3,2},{4,5},{5,4},{6,7},{7,6},{8,9},{9,8},{10,11... | collective-permute-start | bytes 2696 | tf_op jit(solution)/shard_map/ppermute | solution.py:234
  54.1 3.3 %collective-permute-start.1 = (f32[7,32]{1,0:T(8,128)S(1)}, f32[7,32]{1,0:T(8,128)S(1)}, u32[]{:S(2)}, u32[]{:S(2)}) collective-permute-start(f32[7,32]{1,0:T(8,128)S(1)} %fusion.25), channel_id=1, source_target_pairs={{0,2},{1,3},{2,0},{3,1},{4,6},{5,7},{6,4},{7,5},{8,10},{9,11},{10,... | collective-permute-start | bytes 2696 | tf_op jit(solution)/shard_map/ppermute | solution.py:234
  57.4 1.5 %collective-permute-start.4 = (f32[7,32]{1,0:T(8,128)S(1)}, f32[7,32]{1,0:T(8,128)S(1)}, u32[]{:S(2)}, u32[]{:S(2)}) collective-permute-start(f32[7,32]{1,0:T(8,128)S(1)} %fusion.26), channel_id=1, source_target_pairs={{0,2},{1,3},{2,0},{3,1},{4,6},{5,7},{6,4},{7,5},{8,10},{9,11},{10,... | collective-permute-start | bytes 2696 | tf_op jit(solution)/shard_map/ppermute | solution.py:234
  59.0 6.0 %collective-permute-start.2 = (f32[7,32]{1,0:T(8,128)S(1)}, f32[7,32]{1,0:T(8,128)S(1)}, u32[]{:S(2)}, u32[]{:S(2)}) collective-permute-start(f32[7,32]{1,0:T(8,128)S(1)} %add.174), channel_id=1, source_target_pairs={{0,4},{1,5},{2,6},{3,7},{4,0},{5,1},{6,2},{7,3},{8,12},{9,13},{10,... | collective-permute-start | bytes 2696 | tf_op jit(solution)/shard_map/ppermute | solution.py:234
  65.1 0.6 copy.19
  65.7 1.7 %collective-permute-start.5 = (f32[7,32]{1,0:T(8,128)S(1)}, f32[7,32]{1,0:T(8,128)S(1)}, u32[]{:S(2)}, u32[]{:S(2)}) collective-permute-start(f32[7,32]{1,0:T(8,128)S(1)} %add.177), channel_id=1, source_target_pairs={{0,4},{1,5},{2,6},{3,7},{4,0},{5,1},{6,2},{7,3},{8,12},{9,13},{10,... | collective-permute-start | bytes 2696 | tf_op jit(solution)/shard_map/ppermute | solution.py:234
  67.4 5.8 %collective-permute-done.5 = f32[7,32]{1,0:T(8,128)S(1)} collective-permute-done((f32[7,32]{1,0:T(8,128)S(1)}, f32[7,32]{1,0:T(8,128)S(1)}, u32[]{:S(2)}, u32[]{:S(2)}) %collective-permute-start.5) | collective-permute-done | bytes 928 | tf_op jit(solution)/shard_map/ppermute | solution.py:234
  73.3 0.6 copy.20
  (40 shorter events, 1.7 us)
Async XLA Ops:
  8.3 16.5 %all-to-all-start = ((f32[1,1,32,2304]{3,1,0,2:T(1,128)}), f32[1,1,32,2304]{3,1,0,2:T(1,128)S(1)}, u32[]{:S(2)}, u32[]{:S(2)}) async-start(f32[1,1,32,2304]{3,1,0,2:T(1,128)} %copy.23), calls=%async_computation | async-start | bytes 589824 | tf_op jit(solution)/shard_map/all_to_all | solution.py:223
  24.8 13.1 %all-to-all-start.1 = ((f32[1,1,32,2304]{3,1,0,2:T(1,128)}), f32[1,1,32,2304]{3,1,0,2:T(1,128)S(1)}, u32[]{:S(2)}, u32[]{:S(2)}) async-start(f32[1,1,32,2304]{3,1,0,2:T(1,128)} %copy.24), calls=%async_computation.1 | async-start | bytes 589824 | tf_op jit(solution)/shard_map/all_to_all | solution.py:223
  48.1 6.0 %collective-permute-start = (f32[7,32]{1,0:T(8,128)S(1)}, f32[7,32]{1,0:T(8,128)S(1)}, u32[]{:S(2)}, u32[]{:S(2)}) collective-permute-start(f32[7,32]{1,0:T(8,128)S(1)} %broadcast_select_fusion.1), channel_id=1, source_target_pairs={{0,1},{1,0},{2,3},{3,2},{4,5},{5,4},{6,7},{7,6},{8,9},{9,8},{10,11... | collective-permute-start | bytes 2696 | tf_op jit(solution)/shard_map/ppermute | solution.py:234
  52.0 5.5 %collective-permute-start.3 = (f32[7,32]{1,0:T(8,128)S(1)}, f32[7,32]{1,0:T(8,128)S(1)}, u32[]{:S(2)}, u32[]{:S(2)}) collective-permute-start(f32[7,32]{1,0:T(8,128)S(1)} %broadcast_select_fusion), channel_id=1, source_target_pairs={{0,1},{1,0},{2,3},{3,2},{4,5},{5,4},{6,7},{7,6},{8,9},{9,8},{10,11... | collective-permute-start | bytes 2696 | tf_op jit(solution)/shard_map/ppermute | solution.py:234
  54.1 4.9 %collective-permute-start.1 = (f32[7,32]{1,0:T(8,128)S(1)}, f32[7,32]{1,0:T(8,128)S(1)}, u32[]{:S(2)}, u32[]{:S(2)}) collective-permute-start(f32[7,32]{1,0:T(8,128)S(1)} %fusion.25), channel_id=1, source_target_pairs={{0,2},{1,3},{2,0},{3,1},{4,6},{5,7},{6,4},{7,5},{8,10},{9,11},{10,... | collective-permute-start | bytes 2696 | tf_op jit(solution)/shard_map/ppermute | solution.py:234
  57.4 8.2 %collective-permute-start.4 = (f32[7,32]{1,0:T(8,128)S(1)}, f32[7,32]{1,0:T(8,128)S(1)}, u32[]{:S(2)}, u32[]{:S(2)}) collective-permute-start(f32[7,32]{1,0:T(8,128)S(1)} %fusion.26), channel_id=1, source_target_pairs={{0,2},{1,3},{2,0},{3,1},{4,6},{5,7},{6,4},{7,5},{8,10},{9,11},{10,... | collective-permute-start | bytes 2696 | tf_op jit(solution)/shard_map/ppermute | solution.py:234
  59.0 8.4 %collective-permute-start.2 = (f32[7,32]{1,0:T(8,128)S(1)}, f32[7,32]{1,0:T(8,128)S(1)}, u32[]{:S(2)}, u32[]{:S(2)}) collective-permute-start(f32[7,32]{1,0:T(8,128)S(1)} %add.174), channel_id=1, source_target_pairs={{0,4},{1,5},{2,6},{3,7},{4,0},{5,1},{6,2},{7,3},{8,12},{9,13},{10,... | collective-permute-start | bytes 2696 | tf_op jit(solution)/shard_map/ppermute | solution.py:234
  65.7 7.5 %collective-permute-start.5 = (f32[7,32]{1,0:T(8,128)S(1)}, f32[7,32]{1,0:T(8,128)S(1)}, u32[]{:S(2)}, u32[]{:S(2)}) collective-permute-start(f32[7,32]{1,0:T(8,128)S(1)} %add.177), channel_id=1, source_target_pairs={{0,4},{1,5},{2,6},{3,7},{4,0},{5,1},{6,2},{7,3},{8,12},{9,13},{10,... | collective-permute-start | bytes 2696 | tf_op jit(solution)/shard_map/ppermute | solution.py:234

commit v4 on v2

--- a/solution.py
+++ b/solution.py
@@ -226,9 +226,9 @@
     )
     beam_total = jnp.sum(peak_snr, axis=0)
     beam_count = lax.axis_size("beam")
-    for level_bit in range(beam_count.bit_length() - 1):
-        pairs = [(i, i ^ (1 << level_bit)) for i in range(beam_count)]
-        beam_total = beam_total + lax.ppermute(beam_total, "beam", pairs)
+    copies = jnp.broadcast_to(beam_total[None], (beam_count,) + beam_total.shape)
+    gathered = lax.all_to_all(copies, "beam", split_axis=0, concat_axis=0, tiled=True)
+    beam_total = jnp.sum(gathered, axis=0)
     excess_snr = peak_snr - beam_total[None] / (beams_dev * lax.axis_size("beam"))
     return (peak_snr, excess_snr)
 

time: 57 us -> 60.1 us (1.054)
  the two profiles are of different devices: /device:TPU:32 before, /device:TPU:1 now
where the time goes in v4:
time: 60.1 us; the launch traced here: 59.6 us
  waiting for transfers between devices  18.3 us (30%)
  starting transfers between devices  16.8 us (28%)
  Pallas kernels  9.95 us (17%)
  local copies, waits for them, and re-layouts  6.78 us (11%)
  other arithmetic  5.7 us (9%)
  between operations  2.06 us (3%)
    all_to_all x1, waiting for transfers between devices, local(): lax.all_to_all(series, 'freq', split_axis=2, concat_axis=1, tiled=True)  11.6 us
    all_to_all x1, starting transfers between devices, local(): lax.all_to_all(series, 'freq', split_axis=2, concat_axis=1, tiled=True)  8.59 us
    all_to_all x1, starting transfers between devices, local(): lax.all_to_all(copies, 'beam', split_axis=0, concat_axis=0, tiled=True)  8.19 us
    all_to_all x1, waiting for transfers between devices, local(): lax.all_to_all(copies, 'beam', split_axis=0, concat_axis=0, tiled=True)  6.68 us
    pallas_call x1, Pallas kernels, merge_tree(): pl.pallas_call(body, grid=(beams_dev,), in_specs=[pl.BlockSpec(memory_spa...  5.05 us
    pallas_call x1, Pallas kernels, local_tree(): pl.pallas_call(body, grid=(beams_dev,), in_specs=[pl.BlockSpec(memory_spa...  4.91 us
    unnamed x5, local copies, waits for them, and re-layouts  2.77 us
    broadcast_in_dim x1, local copies, waits for them, and re-layouts, local(): series = local_tree(tail_samples, block_samples, tail_blocks)[:, None]  2.48 us
  transfers between devices with their start and end apart: 2, of which 2 were waited for; matrix products, arithmetic and copies ran while one was open for 0% of the time, Pallas kernels for 0%

profile of v4, /device:TPU:1, one launch (start us, length us, event | category | flops | bytes accessed | tf_op | source)
XLA Modules:
  0.0 59.6 jit_solution(4366515872215769050)
XLA Ops:
  1.3 4.9 %shard_map.113 = f32[1,64,2304]{2,1,0:T(8,128)} custom-call(s32[1]{0:T(128)S(6)} %copy.28.count_ref, bf16[1,64,2048]{2,1,0:T(8,128)(2,1)} %tail_ref.1, bf16[1,64,256]{2,1,0:T(8,128)(2,1)} %block_ref.1, f32[64,64]{1,0:T(8,128)} %constant.55.clone.entry_ref, f32[64,64]{1,0:T(8,128)} %constant.56.clone.mid_ref.leave_ref, f32[64,64]{1,0:T(8,128)} %constant.56.clone.mid_ref.leave_ref), custom_call_target="tpu_custom_call" | custom-call | tf_op jit(solution)/shard_map/pallas_call | solution.py:167
  6.2 2.5 %copy.20 = f32[1,1,64,2304]{3,1,0,2:T(1,128)} copy(f32[1,1,64,2304]{3,2,1,0:T(8,128)} %bitcast.29) | data formatting | bytes 1179648 | tf_op jit(solution)/shard_map/broadcast_in_dim | solution.py:215
  8.7 8.6 %all-to-all-start = ((f32[1,1,64,2304]{3,1,0,2:T(1,128)}), f32[1,1,64,2304]{3,1,0,2:T(1,128)S(1)}, u32[]{:S(2)}, u32[]{:S(2)}) async-start(f32[1,1,64,2304]{3,1,0,2:T(1,128)} %copy.20), calls=%async_computation | async-start | bytes 1179648 | tf_op jit(solution)/shard_map/all_to_all | solution.py:218
  17.9 11.6 %all-to-all-done = f32[1,1,64,2304]{3,1,0,2:T(1,128)S(1)} async-done(((f32[1,1,64,2304]{3,1,0,2:T(1,128)}), f32[1,1,64,2304]{3,1,0,2:T(1,128)S(1)}, u32[]{:S(2)}, u32[]{:S(2)}) %all-to-all-start) | async-done | bytes 589856 | tf_op jit(solution)/shard_map/all_to_all | solution.py:218
  29.5 0.8 %copy.27 = f32[1,1,64,2304]{3,2,0,1:T(8,128)} copy(f32[1,1,64,2304]{3,1,0,2:T(1,128)S(1)} %all-to-all-done) | data formatting | bytes 1179648
  30.4 5.0 %shard_map.114 = f32[1,64,2304]{2,1,0:T(8,128)} custom-call(s32[1]{0:T(128)} %bitcast.1.off_ref, f32[1,64,2304]{2,1,0:T(8,128)} %bitcast.28, f32[64,64]{1,0:T(8,128)} %constant.55.clone.entry_ref, f32[64,64]{1,0:T(8,128)} %constant.56.clone.mid_ref.leave_ref, f32[64,64]{1,0:T(8,128)} %constant.56.clone.mid_ref.leave_ref), custom_call_target="tpu_custom_call" | custom-call | tf_op jit(solution)/shard_map/pallas_call | solution.py:196
  35.4 1.0 %slice.61 = f32[1,64,319]{2,1,0:T(8,128)S(1)} slice(f32[1,64,2304]{2,1,0:T(8,128)} %shard_map.114), slice={[0:1], [0:64], [1984:2303]} | slice | bytes 163328 | tf_op jit(solution)/shard_map/slice | solution.py:62
  36.4 0.9 %slice_reduce_fusion = f32[64]{0:T(128)S(1)} fusion(f32[1,64,2304]{2,1,0:T(8,128)} %shard_map.114), kind=kLoop, calls=%fused_computation.27 | loop fusion | flops 16320 | bytes 65792 | tf_op jit(solution)/shard_map/reduce_sum | solution.py:52
  37.4 1.0 %slice_add_fusion = f32[1,64,320]{2,1,0:T(8,128)S(1)} fusion(f32[1,64,2304]{2,1,0:T(8,128)} %shard_map.114, f32[1,64,319]{2,1,0:T(8,128)S(1)} %slice.61), kind=kLoop, calls=%fused_computation.1 | loop fusion | flops 20480 | bytes 245504 | tf_op jit(solution)/shard_map/add | solution.py:62
  38.4 0.1 pad_add_fusion.3
  38.5 0.1 pad_add_fusion.2
  38.6 0.1 pad_add_fusion.1
  38.7 0.1 pad_add_fusion
  38.8 1.0 %multiply_reduce_fusion = f32[64]{0:T(128)S(1)} fusion(f32[1,64,2304]{2,1,0:T(8,128)} %shard_map.114, f32[64]{0:T(128)S(1)} %get-tuple-element.22), kind=kLoop, calls=%fused_computation.18 | loop fusion | flops 49088 | bytes 66048 | tf_op jit(solution)/shard_map/reduce_sum | solution.py:53
  39.9 1.1 %divide_reduce_fusion = (f32[64]{0:T(128)S(1)}, f32[64]{0:T(128)S(1)}) fusion(f32[1,64,2304]{2,1,0:T(8,128)} %shard_map.114, f32[64]{0:T(128)S(1)} %get-tuple-element.15, f32[64]{0:T(128)S(1)} %get-tuple-element.22, f32[64]{0:T(128)S(1)} %get-tuple-element.27, f32[64]{0:T(128)S(1)} %get-tuple-element.21, f32[1,64,320]{2,1,0:T(8,128)S(1)} %slice_add_fusion), kind=kLoop, calls=%fused_computation.19 | loop fusion | flops 98176 | bytes 132608 | tf_op jit(solution)/shard_map/reduce_max | solution.py:66
  40.9 0.2 fusion.8
  41.2 0.3 fusion.11
  41.5 0.7 %reshape.414 = f32[8,1,448]{2,1,0:T(1,128)} reshape(f32[8,7,64]{2,1,0:T(8,128)S(1)} %broadcast_in_dim.35) | data formatting | bytes 28672
  42.2 8.2 %all-to-all-start.1 = ((f32[8,1,448]{2,1,0:T(1,128)}), f32[8,1,448]{2,1,0:T(1,128)S(1)}, u32[]{:S(2)}, u32[]{:S(2)}) async-start(f32[8,1,448]{2,1,0:T(1,128)} %reshape.414), calls=%async_computation.1 | async-start | bytes 32768 | tf_op jit(solution)/shard_map/all_to_all | solution.py:230
  50.4 6.7 %all-to-all-done.1 = f32[8,1,448]{2,1,0:T(1,128)S(1)} async-done(((f32[8,1,448]{2,1,0:T(1,128)}), f32[8,1,448]{2,1,0:T(1,128)S(1)}, u32[]{:S(2)}, u32[]{:S(2)}) %all-to-all-start.1) | async-done | bytes 14368 | tf_op jit(solution)/shard_map/all_to_all | solution.py:230
  57.1 0.5 broadcast.253
  57.6 0.7 %reduce.9 = f32[8,448]{1,0:T(8,128)S(1)} reduce(f32[8,1,448]{2,1,0:T(1,128)S(1)} %all-to-all-done.1, f32[]{:T(128)} %broadcast.253), dimensions={1}, to_apply=%all_to_all.5.reduce_sub_computation | reduce | bytes 28676 | tf_op jit(solution)/shard_map/all_to_all | solution.py:230
  58.3 0.1 reshape.415
  58.4 0.6 copy.22
  59.0 0.6 copy.23
  (10 shorter events, 0.1 us)
Async XLA Ops:
  8.7 20.9 %all-to-all-start = ((f32[1,1,64,2304]{3,1,0,2:T(1,128)}), f32[1,1,64,2304]{3,1,0,2:T(1,128)S(1)}, u32[]{:S(2)}, u32[]{:S(2)}) async-start(f32[1,1,64,2304]{3,1,0,2:T(1,128)} %copy.20), calls=%async_computation | async-start | bytes 1179648 | tf_op jit(solution)/shard_map/all_to_all | solution.py:218
  42.2 14.9 %all-to-all-start.1 = ((f32[8,1,448]{2,1,0:T(1,128)}), f32[8,1,448]{2,1,0:T(1,128)S(1)}, u32[]{:S(2)}, u32[]{:S(2)}) async-start(f32[8,1,448]{2,1,0:T(1,128)} %reshape.414), calls=%async_computation.1 | async-start | bytes 32768 | tf_op jit(solution)/shard_map/all_to_all | solution.py:230

commit v5 on v2

--- a/solution.py
+++ b/solution.py
@@ -181,7 +181,26 @@
     )(tail_blocks.astype(jnp.int32), tail_samples, block_samples, entry, mid, leave)
 
 
-def merge_tree(parts, first_trial):
+def peaks_of(dm_rows, tail_len, block_len):
+    trials = dm_rows.shape[0]
+    searched = dm_rows[:, tail_len:]
+    average = jnp.sum(searched, axis=1, keepdims=True) / jnp.float32(block_len)
+    spread = jnp.sum((searched - average) ** 2, axis=1, keepdims=True) / jnp.float32(block_len)
+    deviation = jnp.sqrt(spread + jnp.float32(1e-05))
+    boxcar = dm_rows[:, tail_len - 128 :]
+    lane_ids = lax.broadcasted_iota(jnp.int32, (trials, 128), 1)
+    table = jnp.zeros((trials, 128), jnp.float32)
+    for width_bit in range(WIDTHS):
+        width_now = 2**width_bit
+        if width_bit > 0:
+            boxcar = boxcar + pltpu.roll(boxcar, width_now // 2, 1)
+        top = jnp.max(boxcar[:, 128:], axis=1, keepdims=True)
+        ratio = (top - width_now * average) / (np.sqrt(np.float32(width_now)) * deviation)
+        table = jnp.where(lane_ids == width_bit, ratio, table)
+    return table.T[:8]
+
+
+def merge_tree(parts, first_trial, tail_len):
     beams_dev, subbands, trials, length = parts.shape
     rows = subbands * trials
     entry, mid, leave = tables(subbands, trials, TILE)
@@ -189,7 +208,8 @@
     def body(off_ref, x_ref, entry_ref, mid_ref, leave_ref, o_ref, buf):
         buf[...] = permute_rows(entry_ref[...], x_ref[...])
         tree_in_place(buf, mid_ref, subbands, trials, off_ref[0], TILE)
-        o_ref[...] = permute_rows(leave_ref[...], buf[...])
+        buf[...] = permute_rows(leave_ref[...], buf[...])
+        o_ref[...] = peaks_of(buf[...], tail_len, length - tail_len)
 
     spec = pl.BlockSpec((None, rows, length), lambda b: (b, 0, 0))
     table_spec = pl.BlockSpec((rows, rows), lambda b: (0, 0))
@@ -197,8 +217,8 @@
         body,
         grid=(beams_dev,),
         in_specs=[pl.BlockSpec(memory_space=pltpu.SMEM), spec, table_spec, table_spec, table_spec],
-        out_specs=spec,
-        out_shape=jax.ShapeDtypeStruct((beams_dev, rows, length), jnp.float32),
+        out_specs=pl.BlockSpec((None, 8, rows), lambda b: (b, 0, 0)),
+        out_shape=jax.ShapeDtypeStruct((beams_dev, 8, rows), jnp.float32),
         scratch_shapes=[pltpu.VMEM((rows, length), jnp.float32)],
     )(
         jnp.reshape(first_trial, (1,)).astype(jnp.int32),
@@ -206,7 +226,7 @@
         entry,
         mid,
         leave,
-    )
+    )[:, :WIDTHS]
 
 
 def local(block_samples, tail_samples, tail_blocks, dm_limit):
@@ -217,8 +237,7 @@
     position = lax.axis_index("freq")
     series = lax.all_to_all(series, "freq", split_axis=2, concat_axis=1, tiled=True)
     per_dev = series.shape[2]
-    dm_rows = merge_tree(series, position * per_dev)
-    scores = peak_ratios(dm_rows, tail_len)
+    scores = merge_tree(series, position * per_dev, tail_len)
     out_rows = scores.shape[-1]
     trial_ids = position * out_rows + jnp.arange(out_rows, dtype=jnp.int32)
     peak_snr = jnp.where(

time: 57 us -> 52 us (0.912)
  other arithmetic: 5 us -> 0.77 us
  local copies, waits for them, and re-layouts: 5.53 us -> 4.52 us
    reduce_max x3 -> x0, other arithmetic: 1.61 us -> none  [peak_ratios(): results.append(jnp.max(ratio, axis=-1))]
    add x5 -> x0, other arithmetic: 1.37 us -> none  [peak_ratios(): boxcar = boxcar + jnp.pad(boxcar[..., :-half_width], pad_spec)]
    reduce_sum x2 -> x1, other arithmetic: 1.96 us -> 0.74 us  [local(): beam_total = jnp.sum(peak_snr, axis=0)]
    slice x1 -> x0, local copies, waits for them, and re-layouts: 0.98 us -> none  [peak_ratios(): boxcar = boxcar + jnp.pad(boxcar[..., :-half_width], pad_spec)]
    unnamed x3 -> x5, local copies, waits for them, and re-layouts: 2.02 us -> 2.04 us
where the time goes in v5:
time: 52 us; the launch traced here: 51.6 us
  waiting for transfers between devices  17.3 us (33%)
  starting transfers between devices  16.7 us (32%)
  Pallas kernels  10.5 us (20%)
  local copies, waits for them, and re-layouts  4.52 us (9%)
  between operations  1.95 us (4%)
  other arithmetic  0.77 us (1%)
    all_to_all x1, waiting for transfers between devices, local(): lax.all_to_all(series, 'freq', split_axis=2, concat_axis=1, tiled=True)  11.1 us
    ppermute x3, starting transfers between devices, local(): beam_total = beam_total + lax.ppermute(beam_total, 'beam', pairs)  9.34 us
    all_to_all x1, starting transfers between devices, local(): lax.all_to_all(series, 'freq', split_axis=2, concat_axis=1, tiled=True)  7.34 us
    ppermute x3, waiting for transfers between devices, local(): beam_total = beam_total + lax.ppermute(beam_total, 'beam', pairs)  6.11 us
    pallas_call x1, Pallas kernels, merge_tree(): pl.pallas_call(body, grid=(beams_dev,), in_specs=[pl.BlockSpec(memory_spa...  5.54 us
    pallas_call x1, Pallas kernels, local_tree(): pl.pallas_call(body, grid=(beams_dev,), in_specs=[pl.BlockSpec(memory_spa...  4.92 us
    broadcast_in_dim x1, local copies, waits for them, and re-layouts, local(): series = local_tree(tail_samples, block_samples, tail_blocks)[:, None]  2.49 us
    unnamed x5, local copies, waits for them, and re-layouts  2.04 us
  transfers between devices with their start and end apart: 4, of which 4 were waited for; matrix products, arithmetic and copies ran while one was open for 1% of the time, Pallas kernels for 0%

profile of v5, /device:TPU:32, one launch (start us, length us, event | category | flops | bytes accessed | tf_op | source)
XLA Modules:
  0.0 51.6 jit_solution(12164595805272386702)
XLA Ops:
  1.3 4.9 %shard_map.113 = f32[1,64,2304]{2,1,0:T(8,128)} custom-call(s32[1]{0:T(128)S(6)} %copy.20.count_ref, bf16[1,64,2048]{2,1,0:T(8,128)(2,1)} %tail_ref.1, bf16[1,64,256]{2,1,0:T(8,128)(2,1)} %block_ref.1, f32[64,64]{1,0:T(8,128)} %constant.19.clone.entry_ref, f32[64,64]{1,0:T(8,128)} %constant.20.clone.mid_ref.leave_ref, f32[64,64]{1,0:T(8,128)} %constant.20.clone.mid_ref.leave_ref), custom_call_target="tpu_custom_call" | custom-call | tf_op jit(solution)/shard_map/pallas_call | solution.py:167
  6.2 2.5 %copy.14 = f32[1,1,64,2304]{3,1,0,2:T(1,128)} copy(f32[1,1,64,2304]{3,2,1,0:T(8,128)} %bitcast.13) | data formatting | bytes 1179648 | tf_op jit(solution)/shard_map/broadcast_in_dim | solution.py:235
  8.7 7.3 %all-to-all-start = ((f32[1,1,64,2304]{3,1,0,2:T(1,128)}), f32[1,1,64,2304]{3,1,0,2:T(1,128)S(1)}, u32[]{:S(2)}, u32[]{:S(2)}) async-start(f32[1,1,64,2304]{3,1,0,2:T(1,128)} %copy.14), calls=%async_computation | async-start | bytes 1179648 | tf_op jit(solution)/shard_map/all_to_all | solution.py:238
  16.7 11.1 %all-to-all-done = f32[1,1,64,2304]{3,1,0,2:T(1,128)S(1)} async-done(((f32[1,1,64,2304]{3,1,0,2:T(1,128)}), f32[1,1,64,2304]{3,1,0,2:T(1,128)S(1)}, u32[]{:S(2)}, u32[]{:S(2)}) %all-to-all-start) | async-done | bytes 589856 | tf_op jit(solution)/shard_map/all_to_all | solution.py:238
  27.8 0.9 %copy.19 = f32[1,1,64,2304]{3,2,0,1:T(8,128)} copy(f32[1,1,64,2304]{3,1,0,2:T(1,128)S(1)} %all-to-all-done) | data formatting | bytes 1179648
  28.7 5.5 %shard_map.114 = f32[1,8,64]{2,1,0:T(8,128)} custom-call(s32[1]{0:T(128)} %bitcast.1.off_ref, f32[1,64,2304]{2,1,0:T(8,128)} %bitcast.12, f32[64,64]{1,0:T(8,128)} %constant.19.clone.entry_ref, f32[64,64]{1,0:T(8,128)} %constant.20.clone.mid_ref.leave_ref, f32[64,64]{1,0:T(8,128)} %constant.20.clone.mid_ref.leave_ref), custom_call_target="tpu_custom_call" | custom-call | tf_op jit(solution)/shard_map/pallas_call | solution.py:216
  34.2 0.0 copy-start
  34.2 0.7 %fusion = f32[7,64]{1,0:T(8,128)S(1)} fusion(f32[1,8,64]{2,1,0:T(8,128)} %shard_map.114, pred[64]{0:T(512)(128)(4,1)S(1)} %add_compare_fusion), kind=kLoop, calls=%fused_computation.5 | loop fusion | flops 448 | bytes 3648 | tf_op jit(solution)/shard_map/reduce_sum | solution.py:246
  35.0 0.1 collective-permute-start
  35.1 3.5 %collective-permute-done = f32[7,64]{1,0:T(8,128)S(1)} collective-permute-done((f32[7,64]{1,0:T(8,128)S(1)}, f32[7,64]{1,0:T(8,128)S(1)}, u32[]{:S(2)}, u32[]{:S(2)}) %collective-permute-start) | collective-permute-done | bytes 1824 | tf_op jit(solution)/shard_map/ppermute | solution.py:250
  38.6 0.0 copy-done
  38.6 3.3 %collective-permute-start.1 = (f32[7,64]{1,0:T(8,128)S(1)}, f32[7,64]{1,0:T(8,128)S(1)}, u32[]{:S(2)}, u32[]{:S(2)}) collective-permute-start(f32[7,64]{1,0:T(8,128)S(1)} %bitcast_add_fusion), channel_id=1, source_target_pairs={{0,2},{1,3},{2,0},{3,1},{4,6},{5,7},{6,4},{7,5},{8,10},{9,11},{10,... | collective-permute-start | bytes 5384 | tf_op jit(solution)/shard_map/ppermute | solution.py:250
  41.9 1.6 %collective-permute-done.1 = f32[7,64]{1,0:T(8,128)S(1)} collective-permute-done((f32[7,64]{1,0:T(8,128)S(1)}, f32[7,64]{1,0:T(8,128)S(1)}, u32[]{:S(2)}, u32[]{:S(2)}) %collective-permute-start.1) | collective-permute-done | bytes 1824 | tf_op jit(solution)/shard_map/ppermute | solution.py:250
  43.5 5.9 %collective-permute-start.2 = (f32[7,64]{1,0:T(8,128)S(1)}, f32[7,64]{1,0:T(8,128)S(1)}, u32[]{:S(2)}, u32[]{:S(2)}) collective-permute-start(f32[7,64]{1,0:T(8,128)S(1)} %add.22), channel_id=1, source_target_pairs={{0,4},{1,5},{2,6},{3,7},{4,0},{5,1},{6,2},{7,3},{8,12},{9,13},{10,... | collective-permute-start | bytes 5384 | tf_op jit(solution)/shard_map/ppermute | solution.py:250
  49.5 0.6 %copy.15 = f32[1,7,64]{2,0,1:T(1,128)} copy(f32[1,7,64]{2,1,0:T(8,128)S(1)} %slice_select_fusion) | data formatting | bytes 3584
  50.0 1.0 %collective-permute-done.2 = f32[7,64]{1,0:T(8,128)S(1)} collective-permute-done((f32[7,64]{1,0:T(8,128)S(1)}, f32[7,64]{1,0:T(8,128)S(1)}, u32[]{:S(2)}, u32[]{:S(2)}) %collective-permute-start.2) | collective-permute-done | bytes 1824 | tf_op jit(solution)/shard_map/ppermute | solution.py:250
  51.0 0.6 %copy.16 = f32[1,7,64]{2,0,1:T(1,128)} copy(f32[1,7,64]{2,1,0:T(8,128)S(1)} %bitcast_subtract_fusion) | data formatting | bytes 3584
  (5 shorter events, 0.0 us)
Async XLA Ops:
  8.7 19.2 %all-to-all-start = ((f32[1,1,64,2304]{3,1,0,2:T(1,128)}), f32[1,1,64,2304]{3,1,0,2:T(1,128)S(1)}, u32[]{:S(2)}, u32[]{:S(2)}) async-start(f32[1,1,64,2304]{3,1,0,2:T(1,128)} %copy.14), calls=%async_computation | async-start | bytes 1179648 | tf_op jit(solution)/shard_map/all_to_all | solution.py:238
  34.2 4.4 %copy-start = (f32[1,8,64]{2,1,0:T(8,128)S(1)}, f32[1,8,64]{2,1,0:T(8,128)}, u32[]{:S(2)}) copy-start(f32[1,8,64]{2,1,0:T(8,128)} %shard_map.114) | copy-start | bytes 6148
  35.0 3.6 %collective-permute-start = (f32[7,64]{1,0:T(8,128)S(1)}, f32[7,64]{1,0:T(8,128)S(1)}, u32[]{:S(2)}, u32[]{:S(2)}) collective-permute-start(f32[7,64]{1,0:T(8,128)S(1)} %fusion), channel_id=1, source_target_pairs={{0,1},{1,0},{2,3},{3,2},{4,5},{5,4},{6,7},{7,6},{8,9},{9,8},{10,11... | collective-permute-start | bytes 5384 | tf_op jit(solution)/shard_map/ppermute | solution.py:250
  38.6 4.9 %collective-permute-start.1 = (f32[7,64]{1,0:T(8,128)S(1)}, f32[7,64]{1,0:T(8,128)S(1)}, u32[]{:S(2)}, u32[]{:S(2)}) collective-permute-start(f32[7,64]{1,0:T(8,128)S(1)} %bitcast_add_fusion), channel_id=1, source_target_pairs={{0,2},{1,3},{2,0},{3,1},{4,6},{5,7},{6,4},{7,5},{8,10},{9,11},{10,... | collective-permute-start | bytes 5384 | tf_op jit(solution)/shard_map/ppermute | solution.py:250
  43.5 7.5 %collective-permute-start.2 = (f32[7,64]{1,0:T(8,128)S(1)}, f32[7,64]{1,0:T(8,128)S(1)}, u32[]{:S(2)}, u32[]{:S(2)}) collective-permute-start(f32[7,64]{1,0:T(8,128)S(1)} %add.22), channel_id=1, source_target_pairs={{0,4},{1,5},{2,6},{3,7},{4,0},{5,1},{6,2},{7,3},{8,12},{9,13},{10,... | collective-permute-start | bytes 5384 | tf_op jit(solution)/shard_map/ppermute | solution.py:250

commit v6 on v5

--- a/solution.py
+++ b/solution.py
@@ -157,9 +157,10 @@
         beam = pl.program_id(0)
         lanes = lax.broadcasted_iota(jnp.int32, (rows, tail_len), 1)
         keep = lanes >= tail_len - 128 * count_ref[beam]
-        buf[:, :tail_len] = jnp.where(keep, tail_ref[...].astype(jnp.float32), jnp.float32(0.0))
-        buf[:, tail_len:] = block_ref[...].astype(jnp.float32)
-        buf[...] = permute_rows(entry_ref[...], buf[...])
+        order = entry_ref[...].astype(jnp.bfloat16)
+        tail = jnp.dot(order, tail_ref[...], preferred_element_type=jnp.float32)
+        buf[:, :tail_len] = jnp.where(keep, tail, jnp.float32(0.0))
+        buf[:, tail_len:] = jnp.dot(order, block_ref[...], preferred_element_type=jnp.float32)
         tree_in_place(buf, mid_ref, rows, 1, 0, TILE)
         o_ref[...] = permute_rows(leave_ref[...], buf[...])
 
@@ -181,7 +182,7 @@
     )(tail_blocks.astype(jnp.int32), tail_samples, block_samples, entry, mid, leave)
 
 
-def peaks_of(dm_rows, tail_len, block_len):
+def peaks_of(dm_rows, tail_len, block_len, leave):
     trials = dm_rows.shape[0]
     searched = dm_rows[:, tail_len:]
     average = jnp.sum(searched, axis=1, keepdims=True) / jnp.float32(block_len)
@@ -197,7 +198,7 @@
         top = jnp.max(boxcar[:, 128:], axis=1, keepdims=True)
         ratio = (top - width_now * average) / (np.sqrt(np.float32(width_now)) * deviation)
         table = jnp.where(lane_ids == width_bit, ratio, table)
-    return table.T[:8]
+    return permute_rows(leave, table).T[:8]
 
 
 def merge_tree(parts, first_trial, tail_len):
@@ -208,8 +209,7 @@
     def body(off_ref, x_ref, entry_ref, mid_ref, leave_ref, o_ref, buf):
         buf[...] = permute_rows(entry_ref[...], x_ref[...])
         tree_in_place(buf, mid_ref, subbands, trials, off_ref[0], TILE)
-        buf[...] = permute_rows(leave_ref[...], buf[...])
-        o_ref[...] = peaks_of(buf[...], tail_len, length - tail_len)
+        o_ref[...] = peaks_of(buf[...], tail_len, length - tail_len, leave_ref[...])
 
     spec = pl.BlockSpec((None, rows, length), lambda b: (b, 0, 0))
     table_spec = pl.BlockSpec((rows, rows), lambda b: (0, 0))

time: 52 us -> 50.6 us (0.973)
  Pallas kernels: 10.5 us -> 9.05 us
    pallas_call x1, Pallas kernels: 5.54 us -> 4.52 us  [merge_tree(): pl.pallas_call(body, grid=(beams_dev,), in_specs=[pl.BlockSpec(memory_spa...]
where the time goes in v6:
time: 50.6 us; the launch traced here: 50.2 us
  waiting for transfers between devices  17.2 us (34%)
  starting transfers between devices  16.7 us (33%)
  Pallas kernels  9.05 us (18%)
  local copies, waits for them, and re-layouts  4.52 us (9%)
  between operations  1.95 us (4%)
  other arithmetic  0.77 us (2%)
    all_to_all x1, waiting for transfers between devices, local(): lax.all_to_all(series, 'freq', split_axis=2, concat_axis=1, tiled=True)  11.1 us
    ppermute x3, starting transfers between devices, local(): beam_total = beam_total + lax.ppermute(beam_total, 'beam', pairs)  9.41 us
    all_to_all x1, starting transfers between devices, local(): lax.all_to_all(series, 'freq', split_axis=2, concat_axis=1, tiled=True)  7.32 us
    ppermute x3, waiting for transfers between devices, local(): beam_total = beam_total + lax.ppermute(beam_total, 'beam', pairs)  6.08 us
    pallas_call x1, Pallas kernels, local_tree(): pl.pallas_call(body, grid=(beams_dev,), in_specs=[pl.BlockSpec(memory_spa...  4.53 us
    pallas_call x1, Pallas kernels, merge_tree(): pl.pallas_call(body, grid=(beams_dev,), in_specs=[pl.BlockSpec(memory_spa...  4.52 us
    broadcast_in_dim x1, local copies, waits for them, and re-layouts, local(): series = local_tree(tail_samples, block_samples, tail_blocks)[:, None]  2.49 us
    unnamed x5, local copies, waits for them, and re-layouts  2.04 us
  transfers between devices with their start and end apart: 4, of which 4 were waited for; matrix products, arithmetic and copies ran while one was open for 1% of the time, Pallas kernels for 0%

profile of v6, /device:TPU:32, one launch (start us, length us, event | category | flops | bytes accessed | tf_op | source)
XLA Modules:
  0.0 50.2 jit_solution(13144347639620563358)
XLA Ops:
  1.3 4.5 %shard_map.113 = f32[1,64,2304]{2,1,0:T(8,128)} custom-call(s32[1]{0:T(128)S(6)} %copy.20.count_ref, bf16[1,64,2048]{2,1,0:T(8,128)(2,1)} %tail_ref.1, bf16[1,64,256]{2,1,0:T(8,128)(2,1)} %block_ref.1, f32[64,64]{1,0:T(8,128)} %constant.19.clone.entry_ref, f32[64,64]{1,0:T(8,128)} %constant.20.clone.mid_ref.leave_ref, f32[64,64]{1,0:T(8,128)} %constant.20.clone.mid_ref.leave_ref), custom_call_target="tpu_custom_call" | custom-call | tf_op jit(solution)/shard_map/pallas_call | solution.py:168
  5.8 2.5 %copy.14 = f32[1,1,64,2304]{3,1,0,2:T(1,128)} copy(f32[1,1,64,2304]{3,2,1,0:T(8,128)} %bitcast.13) | data formatting | bytes 1179648 | tf_op jit(solution)/shard_map/broadcast_in_dim | solution.py:235
  8.3 7.3 %all-to-all-start = ((f32[1,1,64,2304]{3,1,0,2:T(1,128)}), f32[1,1,64,2304]{3,1,0,2:T(1,128)S(1)}, u32[]{:S(2)}, u32[]{:S(2)}) async-start(f32[1,1,64,2304]{3,1,0,2:T(1,128)} %copy.14), calls=%async_computation | async-start | bytes 1179648 | tf_op jit(solution)/shard_map/all_to_all | solution.py:238
  16.3 11.1 %all-to-all-done = f32[1,1,64,2304]{3,1,0,2:T(1,128)S(1)} async-done(((f32[1,1,64,2304]{3,1,0,2:T(1,128)}), f32[1,1,64,2304]{3,1,0,2:T(1,128)S(1)}, u32[]{:S(2)}, u32[]{:S(2)}) %all-to-all-start) | async-done | bytes 589856 | tf_op jit(solution)/shard_map/all_to_all | solution.py:238
  27.4 0.9 %copy.19 = f32[1,1,64,2304]{3,2,0,1:T(8,128)} copy(f32[1,1,64,2304]{3,1,0,2:T(1,128)S(1)} %all-to-all-done) | data formatting | bytes 1179648
  28.3 4.5 %shard_map.114 = f32[1,8,64]{2,1,0:T(8,128)} custom-call(s32[1]{0:T(128)} %bitcast.1.off_ref, f32[1,64,2304]{2,1,0:T(8,128)} %bitcast.12, f32[64,64]{1,0:T(8,128)} %constant.19.clone.entry_ref, f32[64,64]{1,0:T(8,128)} %constant.20.clone.mid_ref.leave_ref, f32[64,64]{1,0:T(8,128)} %constant.20.clone.mid_ref.leave_ref), custom_call_target="tpu_custom_call" | custom-call | tf_op jit(solution)/shard_map/pallas_call | solution.py:216
  32.8 0.0 copy-start
  32.8 0.7 %fusion = f32[7,64]{1,0:T(8,128)S(1)} fusion(f32[1,8,64]{2,1,0:T(8,128)} %shard_map.114, pred[64]{0:T(512)(128)(4,1)S(1)} %add_compare_fusion), kind=kLoop, calls=%fused_computation.5 | loop fusion | flops 448 | bytes 3648 | tf_op jit(solution)/shard_map/reduce_sum | solution.py:246
  33.6 0.1 collective-permute-start
  33.7 3.5 %collective-permute-done = f32[7,64]{1,0:T(8,128)S(1)} collective-permute-done((f32[7,64]{1,0:T(8,128)S(1)}, f32[7,64]{1,0:T(8,128)S(1)}, u32[]{:S(2)}, u32[]{:S(2)}) %collective-permute-start) | collective-permute-done | bytes 1824 | tf_op jit(solution)/shard_map/ppermute | solution.py:250
  37.2 0.0 copy-done
  37.2 3.4 %collective-permute-start.1 = (f32[7,64]{1,0:T(8,128)S(1)}, f32[7,64]{1,0:T(8,128)S(1)}, u32[]{:S(2)}, u32[]{:S(2)}) collective-permute-start(f32[7,64]{1,0:T(8,128)S(1)} %bitcast_add_fusion), channel_id=1, source_target_pairs={{0,2},{1,3},{2,0},{3,1},{4,6},{5,7},{6,4},{7,5},{8,10},{9,11},{10,... | collective-permute-start | bytes 5384 | tf_op jit(solution)/shard_map/ppermute | solution.py:250
  40.5 1.6 %collective-permute-done.1 = f32[7,64]{1,0:T(8,128)S(1)} collective-permute-done((f32[7,64]{1,0:T(8,128)S(1)}, f32[7,64]{1,0:T(8,128)S(1)}, u32[]{:S(2)}, u32[]{:S(2)}) %collective-permute-start.1) | collective-permute-done | bytes 1824 | tf_op jit(solution)/shard_map/ppermute | solution.py:250
  42.1 5.9 %collective-permute-start.2 = (f32[7,64]{1,0:T(8,128)S(1)}, f32[7,64]{1,0:T(8,128)S(1)}, u32[]{:S(2)}, u32[]{:S(2)}) collective-permute-start(f32[7,64]{1,0:T(8,128)S(1)} %add.22), channel_id=1, source_target_pairs={{0,4},{1,5},{2,6},{3,7},{4,0},{5,1},{6,2},{7,3},{8,12},{9,13},{10,... | collective-permute-start | bytes 5384 | tf_op jit(solution)/shard_map/ppermute | solution.py:250
  48.1 0.6 %copy.15 = f32[1,7,64]{2,0,1:T(1,128)} copy(f32[1,7,64]{2,1,0:T(8,128)S(1)} %slice_select_fusion) | data formatting | bytes 3584
  48.6 1.0 %collective-permute-done.2 = f32[7,64]{1,0:T(8,128)S(1)} collective-permute-done((f32[7,64]{1,0:T(8,128)S(1)}, f32[7,64]{1,0:T(8,128)S(1)}, u32[]{:S(2)}, u32[]{:S(2)}) %collective-permute-start.2) | collective-permute-done | bytes 1824 | tf_op jit(solution)/shard_map/ppermute | solution.py:250
  49.6 0.6 %copy.16 = f32[1,7,64]{2,0,1:T(1,128)} copy(f32[1,7,64]{2,1,0:T(8,128)S(1)} %bitcast_subtract_fusion) | data formatting | bytes 3584
  (5 shorter events, 0.0 us)
Async XLA Ops:
  8.3 19.1 %all-to-all-start = ((f32[1,1,64,2304]{3,1,0,2:T(1,128)}), f32[1,1,64,2304]{3,1,0,2:T(1,128)S(1)}, u32[]{:S(2)}, u32[]{:S(2)}) async-start(f32[1,1,64,2304]{3,1,0,2:T(1,128)} %copy.14), calls=%async_computation | async-start | bytes 1179648 | tf_op jit(solution)/shard_map/all_to_all | solution.py:238
  32.8 4.4 %copy-start = (f32[1,8,64]{2,1,0:T(8,128)S(1)}, f32[1,8,64]{2,1,0:T(8,128)}, u32[]{:S(2)}) copy-start(f32[1,8,64]{2,1,0:T(8,128)} %shard_map.114) | copy-start | bytes 6148
  33.6 3.6 %collective-permute-start = (f32[7,64]{1,0:T(8,128)S(1)}, f32[7,64]{1,0:T(8,128)S(1)}, u32[]{:S(2)}, u32[]{:S(2)}) collective-permute-start(f32[7,64]{1,0:T(8,128)S(1)} %fusion), channel_id=1, source_target_pairs={{0,1},{1,0},{2,3},{3,2},{4,5},{5,4},{6,7},{7,6},{8,9},{9,8},{10,11... | collective-permute-start | bytes 5384 | tf_op jit(solution)/shard_map/ppermute | solution.py:250
  37.2 4.9 %collective-permute-start.1 = (f32[7,64]{1,0:T(8,128)S(1)}, f32[7,64]{1,0:T(8,128)S(1)}, u32[]{:S(2)}, u32[]{:S(2)}) collective-permute-start(f32[7,64]{1,0:T(8,128)S(1)} %bitcast_add_fusion), channel_id=1, source_target_pairs={{0,2},{1,3},{2,0},{3,1},{4,6},{5,7},{6,4},{7,5},{8,10},{9,11},{10,... | collective-permute-start | bytes 5384 | tf_op jit(solution)/shard_map/ppermute | solution.py:250
  42.1 7.5 %collective-permute-start.2 = (f32[7,64]{1,0:T(8,128)S(1)}, f32[7,64]{1,0:T(8,128)S(1)}, u32[]{:S(2)}, u32[]{:S(2)}) collective-permute-start(f32[7,64]{1,0:T(8,128)S(1)} %add.22), channel_id=1, source_target_pairs={{0,4},{1,5},{2,6},{3,7},{4,0},{5,1},{6,2},{7,3},{8,12},{9,13},{10,... | collective-permute-start | bytes 5384 | tf_op jit(solution)/shard_map/ppermute | solution.py:250

commit v7 on v6

--- a/solution.py
+++ b/solution.py
@@ -81,6 +81,12 @@
     return jnp.dot(matrix, rows, precision=lax.Precision.HIGHEST, preferred_element_type=jnp.float32)
 
 
+def swap_blocks(rows, tile):
+    length = rows.shape[1]
+    blocks = rows.reshape(tile, tile, length)
+    return pltpu.einshape("abt->bat", blocks).reshape(tile * tile, length)
+
+
 def tree_in_place(buf, mid_ref, subbands, trials, first_trial, tile):
     length = buf.shape[1]
     while subbands > 1 and subbands // 2 >= tile:
@@ -97,7 +103,10 @@
         subbands = half
         trials = 2 * trials
         first_trial = 2 * first_trial
-    buf[...] = permute_rows(mid_ref[...], buf[...])
+    if subbands == tile and buf.shape[0] == tile * tile:
+        buf[...] = swap_blocks(buf[...], tile)
+    else:
+        buf[...] = permute_rows(mid_ref[...], buf[...])
     groups, step = 1, 1
     lanes = lax.broadcasted_iota(jnp.int32, (tile, length), 1)
     if not isinstance(first_trial, int):
@@ -162,7 +171,7 @@
         buf[:, :tail_len] = jnp.where(keep, tail, jnp.float32(0.0))
         buf[:, tail_len:] = jnp.dot(order, block_ref[...], preferred_element_type=jnp.float32)
         tree_in_place(buf, mid_ref, rows, 1, 0, TILE)
-        o_ref[...] = permute_rows(leave_ref[...], buf[...])
+        o_ref[...] = swap_blocks(buf[...], TILE)
 
     table_spec = pl.BlockSpec((rows, rows), lambda b: (0, 0))
     return pl.pallas_call(

time: 50.6 us -> 48.5 us (0.958)
  Pallas kernels: 9.05 us -> 6.96 us
    pallas_call x1, Pallas kernels: 4.53 us -> 2.97 us  [local_tree(): pl.pallas_call(body, grid=(beams_dev,), in_specs=[pl.BlockSpec(memory_spa...]
    pallas_call x1, Pallas kernels: 4.52 us -> 4 us  [merge_tree(): pl.pallas_call(body, grid=(beams_dev,), in_specs=[pl.BlockSpec(memory_spa...]
where the time goes in v7:
time: 48.5 us; the launch traced here: 48.2 us
  waiting for transfers between devices  17.2 us (35%)
  starting transfers between devices  16.7 us (34%)
  Pallas kernels  6.96 us (14%)
  local copies, waits for them, and re-layouts  4.52 us (9%)
  between operations  1.95 us (4%)
  other arithmetic  0.77 us (2%)
    all_to_all x1, waiting for transfers between devices, local(): lax.all_to_all(series, 'freq', split_axis=2, concat_axis=1, tiled=True)  11.1 us
    ppermute x3, starting transfers between devices, local(): beam_total = beam_total + lax.ppermute(beam_total, 'beam', pairs)  9.41 us
    all_to_all x1, starting transfers between devices, local(): lax.all_to_all(series, 'freq', split_axis=2, concat_axis=1, tiled=True)  7.32 us
    ppermute x3, waiting for transfers between devices, local(): beam_total = beam_total + lax.ppermute(beam_total, 'beam', pairs)  6.08 us
    pallas_call x1, Pallas kernels, merge_tree(): pl.pallas_call(body, grid=(beams_dev,), in_specs=[pl.BlockSpec(memory_spa...  4 us
    pallas_call x1, Pallas kernels, local_tree(): pl.pallas_call(body, grid=(beams_dev,), in_specs=[pl.BlockSpec(memory_spa...  2.97 us
    broadcast_in_dim x1, local copies, waits for them, and re-layouts, local(): series = local_tree(tail_samples, block_samples, tail_blocks)[:, None]  2.49 us
    unnamed x5, local copies, waits for them, and re-layouts  2.04 us
  transfers between devices with their start and end apart: 4, of which 4 were waited for; matrix products, arithmetic and copies ran while one was open for 1% of the time, Pallas kernels for 0%

profile of v7, /device:TPU:32, one launch (start us, length us, event | category | flops | bytes accessed | tf_op | source)
XLA Modules:
  0.0 48.2 jit_solution(13001750938357285522)
XLA Ops:
  1.3 3.0 %shard_map.113 = f32[1,64,2304]{2,1,0:T(8,128)} custom-call(s32[1]{0:T(128)S(6)} %copy.20.count_ref, bf16[1,64,2048]{2,1,0:T(8,128)(2,1)} %tail_ref.1, bf16[1,64,256]{2,1,0:T(8,128)(2,1)} %block_ref.1, f32[64,64]{1,0:T(8,128)} %constant.19.clone.entry_ref, f32[64,64]{1,0:T(8,128)} %constant.20.clone.mid_ref.leave_ref, f32[64,64]{1,0:T(8,128)} %constant.20.clone.mid_ref.leave_ref), custom_call_target="tpu_custom_call" | custom-call | tf_op jit(solution)/shard_map/pallas_call | solution.py:177
  4.2 2.5 %copy.14 = f32[1,1,64,2304]{3,1,0,2:T(1,128)} copy(f32[1,1,64,2304]{3,2,1,0:T(8,128)} %bitcast.13) | data formatting | bytes 1179648 | tf_op jit(solution)/shard_map/broadcast_in_dim | solution.py:244
  6.7 7.3 %all-to-all-start = ((f32[1,1,64,2304]{3,1,0,2:T(1,128)}), f32[1,1,64,2304]{3,1,0,2:T(1,128)S(1)}, u32[]{:S(2)}, u32[]{:S(2)}) async-start(f32[1,1,64,2304]{3,1,0,2:T(1,128)} %copy.14), calls=%async_computation | async-start | bytes 1179648 | tf_op jit(solution)/shard_map/all_to_all | solution.py:247
  14.7 11.1 %all-to-all-done = f32[1,1,64,2304]{3,1,0,2:T(1,128)S(1)} async-done(((f32[1,1,64,2304]{3,1,0,2:T(1,128)}), f32[1,1,64,2304]{3,1,0,2:T(1,128)S(1)}, u32[]{:S(2)}, u32[]{:S(2)}) %all-to-all-start) | async-done | bytes 589856 | tf_op jit(solution)/shard_map/all_to_all | solution.py:247
  25.9 0.9 %copy.19 = f32[1,1,64,2304]{3,2,0,1:T(8,128)} copy(f32[1,1,64,2304]{3,1,0,2:T(1,128)S(1)} %all-to-all-done) | data formatting | bytes 1179648
  26.7 4.0 %shard_map.114 = f32[1,8,64]{2,1,0:T(8,128)} custom-call(s32[1]{0:T(128)} %bitcast.1.off_ref, f32[1,64,2304]{2,1,0:T(8,128)} %bitcast.12, f32[64,64]{1,0:T(8,128)} %constant.19.clone.entry_ref, f32[64,64]{1,0:T(8,128)} %constant.20.clone.mid_ref.leave_ref, f32[64,64]{1,0:T(8,128)} %constant.20.clone.mid_ref.leave_ref), custom_call_target="tpu_custom_call" | custom-call | tf_op jit(solution)/shard_map/pallas_call | solution.py:225
  30.7 0.0 copy-start
  30.7 0.7 %fusion = f32[7,64]{1,0:T(8,128)S(1)} fusion(f32[1,8,64]{2,1,0:T(8,128)} %shard_map.114, pred[64]{0:T(512)(128)(4,1)S(1)} %add_compare_fusion), kind=kLoop, calls=%fused_computation.5 | loop fusion | flops 448 | bytes 3648 | tf_op jit(solution)/shard_map/reduce_sum | solution.py:255
  31.5 0.1 collective-permute-start
  31.6 3.5 %collective-permute-done = f32[7,64]{1,0:T(8,128)S(1)} collective-permute-done((f32[7,64]{1,0:T(8,128)S(1)}, f32[7,64]{1,0:T(8,128)S(1)}, u32[]{:S(2)}, u32[]{:S(2)}) %collective-permute-start) | collective-permute-done | bytes 1824 | tf_op jit(solution)/shard_map/ppermute | solution.py:259
  35.1 0.0 copy-done
  35.1 3.4 %collective-permute-start.1 = (f32[7,64]{1,0:T(8,128)S(1)}, f32[7,64]{1,0:T(8,128)S(1)}, u32[]{:S(2)}, u32[]{:S(2)}) collective-permute-start(f32[7,64]{1,0:T(8,128)S(1)} %bitcast_add_fusion), channel_id=1, source_target_pairs={{0,2},{1,3},{2,0},{3,1},{4,6},{5,7},{6,4},{7,5},{8,10},{9,11},{10,... | collective-permute-start | bytes 5384 | tf_op jit(solution)/shard_map/ppermute | solution.py:259
  38.4 1.6 %collective-permute-done.1 = f32[7,64]{1,0:T(8,128)S(1)} collective-permute-done((f32[7,64]{1,0:T(8,128)S(1)}, f32[7,64]{1,0:T(8,128)S(1)}, u32[]{:S(2)}, u32[]{:S(2)}) %collective-permute-start.1) | collective-permute-done | bytes 1824 | tf_op jit(solution)/shard_map/ppermute | solution.py:259
  40.0 5.9 %collective-permute-start.2 = (f32[7,64]{1,0:T(8,128)S(1)}, f32[7,64]{1,0:T(8,128)S(1)}, u32[]{:S(2)}, u32[]{:S(2)}) collective-permute-start(f32[7,64]{1,0:T(8,128)S(1)} %add.22), channel_id=1, source_target_pairs={{0,4},{1,5},{2,6},{3,7},{4,0},{5,1},{6,2},{7,3},{8,12},{9,13},{10,... | collective-permute-start | bytes 5384 | tf_op jit(solution)/shard_map/ppermute | solution.py:259
  46.0 0.6 %copy.15 = f32[1,7,64]{2,0,1:T(1,128)} copy(f32[1,7,64]{2,1,0:T(8,128)S(1)} %slice_select_fusion) | data formatting | bytes 3584
  46.6 1.0 %collective-permute-done.2 = f32[7,64]{1,0:T(8,128)S(1)} collective-permute-done((f32[7,64]{1,0:T(8,128)S(1)}, f32[7,64]{1,0:T(8,128)S(1)}, u32[]{:S(2)}, u32[]{:S(2)}) %collective-permute-start.2) | collective-permute-done | bytes 1824 | tf_op jit(solution)/shard_map/ppermute | solution.py:259
  47.6 0.6 %copy.16 = f32[1,7,64]{2,0,1:T(1,128)} copy(f32[1,7,64]{2,1,0:T(8,128)S(1)} %bitcast_subtract_fusion) | data formatting | bytes 3584
  (5 shorter events, 0.0 us)
Async XLA Ops:
  6.7 19.1 %all-to-all-start = ((f32[1,1,64,2304]{3,1,0,2:T(1,128)}), f32[1,1,64,2304]{3,1,0,2:T(1,128)S(1)}, u32[]{:S(2)}, u32[]{:S(2)}) async-start(f32[1,1,64,2304]{3,1,0,2:T(1,128)} %copy.14), calls=%async_computation | async-start | bytes 1179648 | tf_op jit(solution)/shard_map/all_to_all | solution.py:247
  30.7 4.4 %copy-start = (f32[1,8,64]{2,1,0:T(8,128)S(1)}, f32[1,8,64]{2,1,0:T(8,128)}, u32[]{:S(2)}) copy-start(f32[1,8,64]{2,1,0:T(8,128)} %shard_map.114) | copy-start | bytes 6148
  31.5 3.6 %collective-permute-start = (f32[7,64]{1,0:T(8,128)S(1)}, f32[7,64]{1,0:T(8,128)S(1)}, u32[]{:S(2)}, u32[]{:S(2)}) collective-permute-start(f32[7,64]{1,0:T(8,128)S(1)} %fusion), channel_id=1, source_target_pairs={{0,1},{1,0},{2,3},{3,2},{4,5},{5,4},{6,7},{7,6},{8,9},{9,8},{10,11... | collective-permute-start | bytes 5384 | tf_op jit(solution)/shard_map/ppermute | solution.py:259
  35.1 4.9 %collective-permute-start.1 = (f32[7,64]{1,0:T(8,128)S(1)}, f32[7,64]{1,0:T(8,128)S(1)}, u32[]{:S(2)}, u32[]{:S(2)}) collective-permute-start(f32[7,64]{1,0:T(8,128)S(1)} %bitcast_add_fusion), channel_id=1, source_target_pairs={{0,2},{1,3},{2,0},{3,1},{4,6},{5,7},{6,4},{7,5},{8,10},{9,11},{10,... | collective-permute-start | bytes 5384 | tf_op jit(solution)/shard_map/ppermute | solution.py:259
  40.0 7.5 %collective-permute-start.2 = (f32[7,64]{1,0:T(8,128)S(1)}, f32[7,64]{1,0:T(8,128)S(1)}, u32[]{:S(2)}, u32[]{:S(2)}) collective-permute-start(f32[7,64]{1,0:T(8,128)S(1)} %add.22), channel_id=1, source_target_pairs={{0,4},{1,5},{2,6},{3,7},{4,0},{5,1},{6,2},{7,3},{8,12},{9,13},{10,... | collective-permute-start | bytes 5384 | tf_op jit(solution)/shard_map/ppermute | solution.py:259

commit v8 on v7

--- a/solution.py
+++ b/solution.py
@@ -210,13 +210,21 @@
     return permute_rows(leave, table).T[:8]
 
 
+def trial_major(parts):
+    beams_dev, subbands, trials, length = parts.shape
+    bits = subbands.bit_length() - 1
+    split = parts.reshape((beams_dev,) + (2,) * bits + (trials, length))
+    order = (0, bits + 1) + tuple(range(bits, 0, -1)) + (bits + 2,)
+    return jnp.transpose(split, order).reshape(beams_dev, subbands * trials, length)
+
+
 def merge_tree(parts, first_trial, tail_len):
     beams_dev, subbands, trials, length = parts.shape
     rows = subbands * trials
     entry, mid, leave = tables(subbands, trials, TILE)
 
     def body(off_ref, x_ref, entry_ref, mid_ref, leave_ref, o_ref, buf):
-        buf[...] = permute_rows(entry_ref[...], x_ref[...])
+        buf[...] = x_ref[...]
         tree_in_place(buf, mid_ref, subbands, trials, off_ref[0], TILE)
         o_ref[...] = peaks_of(buf[...], tail_len, length - tail_len, leave_ref[...])
 
@@ -231,7 +239,7 @@
         scratch_shapes=[pltpu.VMEM((rows, length), jnp.float32)],
     )(
         jnp.reshape(first_trial, (1,)).astype(jnp.int32),
-        parts.reshape(beams_dev, rows, length),
+        trial_major(parts),
         entry,
         mid,
         leave,

time: 48.5 us -> 48.8 us (level)
  local copies, waits for them, and re-layouts: 4.52 us -> 5.34 us
    reshape x0 -> x2, local copies, waits for them, and re-layouts: none -> 1.68 us  [the longest x1 1.23 us: trial_major(): jnp.transpose(split, order).reshape(beams_dev, subbands * trials, length)]
    unnamed x5 -> x4, local copies, waits for them, and re-layouts: 2.04 us -> 1.17 us
where the time goes in v8:
time: 48.8 us; the launch traced here: 48.5 us
  waiting for transfers between devices  17.2 us (35%)
  starting transfers between devices  16.7 us (34%)
  Pallas kernels  6.48 us (13%)
  local copies, waits for them, and re-layouts  5.34 us (11%)
  between operations  1.96 us (4%)
  other arithmetic  0.77 us (2%)
    all_to_all x1, waiting for transfers between devices, local(): lax.all_to_all(series, 'freq', split_axis=2, concat_axis=1, tiled=True)  11.1 us
    ppermute x3, starting transfers between devices, local(): beam_total = beam_total + lax.ppermute(beam_total, 'beam', pairs)  9.4 us
    all_to_all x1, starting transfers between devices, local(): lax.all_to_all(series, 'freq', split_axis=2, concat_axis=1, tiled=True)  7.32 us
    ppermute x3, waiting for transfers between devices, local(): beam_total = beam_total + lax.ppermute(beam_total, 'beam', pairs)  6.08 us
    pallas_call x1, Pallas kernels, merge_tree(): pl.pallas_call(body, grid=(beams_dev,), in_specs=[pl.BlockSpec(memory_spa...  3.51 us
    pallas_call x1, Pallas kernels, local_tree(): pl.pallas_call(body, grid=(beams_dev,), in_specs=[pl.BlockSpec(memory_spa...  2.97 us
    broadcast_in_dim x1, local copies, waits for them, and re-layouts, local(): series = local_tree(tail_samples, block_samples, tail_blocks)[:, None]  2.49 us
    reshape x1, local copies, waits for them, and re-layouts, trial_major(): jnp.transpose(split, order).reshape(beams_dev, subbands * trials, length)  1.23 us
  transfers between devices with their start and end apart: 4, of which 4 were waited for; matrix products, arithmetic and copies ran while one was open for 1% of the time, Pallas kernels for 0%

profile of v8, /device:TPU:32, one launch (start us, length us, event | category | flops | bytes accessed | tf_op | source)
XLA Modules:
  0.0 48.5 jit_solution(2867486270732618187)
XLA Ops:
  1.3 3.0 %shard_map.113 = f32[1,64,2304]{2,1,0:T(8,128)} custom-call(s32[1]{0:T(128)S(6)} %copy.21.count_ref, bf16[1,64,2048]{2,1,0:T(8,128)(2,1)} %tail_ref.1, bf16[1,64,256]{2,1,0:T(8,128)(2,1)} %block_ref.1, f32[64,64]{1,0:T(8,128)} %constant.19.clone.entry_ref, f32[64,64]{1,0:T(8,128)} %constant.20.clone.mid_ref.leave_ref, f32[64,64]{1,0:T(8,128)} %constant.20.clone.mid_ref.leave_ref), custom_call_target="tpu_custom_call" | custom-call | tf_op jit(solution)/shard_map/pallas_call | solution.py:177
  4.2 2.5 %copy.15 = f32[1,1,64,2304]{3,1,0,2:T(1,128)} copy(f32[1,1,64,2304]{3,2,1,0:T(8,128)} %bitcast.14) | data formatting | bytes 1179648 | tf_op jit(solution)/shard_map/broadcast_in_dim | solution.py:252
  6.7 7.3 %all-to-all-start = ((f32[1,1,64,2304]{3,1,0,2:T(1,128)}), f32[1,1,64,2304]{3,1,0,2:T(1,128)S(1)}, u32[]{:S(2)}, u32[]{:S(2)}) async-start(f32[1,1,64,2304]{3,1,0,2:T(1,128)} %copy.15), calls=%async_computation | async-start | bytes 1179648 | tf_op jit(solution)/shard_map/all_to_all | solution.py:255
  14.7 11.1 %all-to-all-done = f32[1,1,64,2304]{3,1,0,2:T(1,128)S(1)} async-done(((f32[1,1,64,2304]{3,1,0,2:T(1,128)}), f32[1,1,64,2304]{3,1,0,2:T(1,128)S(1)}, u32[]{:S(2)}, u32[]{:S(2)}) %all-to-all-start) | async-done | bytes 589856 | tf_op jit(solution)/shard_map/all_to_all | solution.py:255
  25.9 0.5 copy.20
  26.3 1.2 %reshape.32.x_ref = f32[1,64,2304]{2,1,0:T(8,128)} reshape(f32[1,2,2,2,2,2,2,2304]{7,6,5,4,3,2,1,0:T(2,128)S(1)} %bitcast.15) | data formatting | bytes 1179648 | tf_op jit(solution)/shard_map/reshape | solution.py:218
  27.6 3.5 %shard_map.114 = f32[1,8,64]{2,1,0:T(8,128)} custom-call(s32[1]{0:T(128)} %bitcast.1.off_ref, f32[1,64,2304]{2,1,0:T(8,128)} %reshape.32.x_ref, f32[64,64]{1,0:T(8,128)} %constant.19.clone.entry_ref, f32[64,64]{1,0:T(8,128)} %constant.20.clone.mid_ref.leave_ref, f32[64,64]{1,0:T(8,128)} %constant.20.clone.mid_ref.leave_ref), custom_call_target="tpu_custom_call" | custom-call | tf_op jit(solution)/shard_map/pallas_call | solution.py:233
  31.1 0.0 copy-start
  31.1 0.7 %fusion = f32[7,64]{1,0:T(8,128)S(1)} fusion(f32[1,8,64]{2,1,0:T(8,128)} %shard_map.114, pred[64]{0:T(512)(128)(4,1)S(1)} %add_compare_fusion), kind=kLoop, calls=%fused_computation.5 | loop fusion | flops 448 | bytes 3648 | tf_op jit(solution)/shard_map/reduce_sum | solution.py:263
  31.8 0.1 collective-permute-start
  31.9 3.5 %collective-permute-done = f32[7,64]{1,0:T(8,128)S(1)} collective-permute-done((f32[7,64]{1,0:T(8,128)S(1)}, f32[7,64]{1,0:T(8,128)S(1)}, u32[]{:S(2)}, u32[]{:S(2)}) %collective-permute-start) | collective-permute-done | bytes 1824 | tf_op jit(solution)/shard_map/ppermute | solution.py:267
  35.4 0.0 copy-done
  35.4 3.4 %collective-permute-start.1 = (f32[7,64]{1,0:T(8,128)S(1)}, f32[7,64]{1,0:T(8,128)S(1)}, u32[]{:S(2)}, u32[]{:S(2)}) collective-permute-start(f32[7,64]{1,0:T(8,128)S(1)} %bitcast_add_fusion), channel_id=1, source_target_pairs={{0,2},{1,3},{2,0},{3,1},{4,6},{5,7},{6,4},{7,5},{8,10},{9,11},{10,... | collective-permute-start | bytes 5384 | tf_op jit(solution)/shard_map/ppermute | solution.py:267
  38.8 1.6 %collective-permute-done.1 = f32[7,64]{1,0:T(8,128)S(1)} collective-permute-done((f32[7,64]{1,0:T(8,128)S(1)}, f32[7,64]{1,0:T(8,128)S(1)}, u32[]{:S(2)}, u32[]{:S(2)}) %collective-permute-start.1) | collective-permute-done | bytes 1824 | tf_op jit(solution)/shard_map/ppermute | solution.py:267
  40.4 5.9 %collective-permute-start.2 = (f32[7,64]{1,0:T(8,128)S(1)}, f32[7,64]{1,0:T(8,128)S(1)}, u32[]{:S(2)}, u32[]{:S(2)}) collective-permute-start(f32[7,64]{1,0:T(8,128)S(1)} %add.22), channel_id=1, source_target_pairs={{0,4},{1,5},{2,6},{3,7},{4,0},{5,1},{6,2},{7,3},{8,12},{9,13},{10,... | collective-permute-start | bytes 5384 | tf_op jit(solution)/shard_map/ppermute | solution.py:267
  46.3 0.6 %copy.17 = f32[1,7,64]{2,0,1:T(1,128)} copy(f32[1,7,64]{2,1,0:T(8,128)S(1)} %slice_select_fusion) | data formatting | bytes 3584
  46.9 1.0 %collective-permute-done.2 = f32[7,64]{1,0:T(8,128)S(1)} collective-permute-done((f32[7,64]{1,0:T(8,128)S(1)}, f32[7,64]{1,0:T(8,128)S(1)}, u32[]{:S(2)}, u32[]{:S(2)}) %collective-permute-start.2) | collective-permute-done | bytes 1824 | tf_op jit(solution)/shard_map/ppermute | solution.py:267
  47.9 0.6 %copy.18 = f32[1,7,64]{2,0,1:T(1,128)} copy(f32[1,7,64]{2,1,0:T(8,128)S(1)} %bitcast_subtract_fusion) | data formatting | bytes 3584
  (5 shorter events, 0.0 us)
Async XLA Ops:
  6.7 19.1 %all-to-all-start = ((f32[1,1,64,2304]{3,1,0,2:T(1,128)}), f32[1,1,64,2304]{3,1,0,2:T(1,128)S(1)}, u32[]{:S(2)}, u32[]{:S(2)}) async-start(f32[1,1,64,2304]{3,1,0,2:T(1,128)} %copy.15), calls=%async_computation | async-start | bytes 1179648 | tf_op jit(solution)/shard_map/all_to_all | solution.py:255
  31.1 4.4 %copy-start = (f32[1,8,64]{2,1,0:T(8,128)S(1)}, f32[1,8,64]{2,1,0:T(8,128)}, u32[]{:S(2)}) copy-start(f32[1,8,64]{2,1,0:T(8,128)} %shard_map.114) | copy-start | bytes 6148
  31.8 3.6 %collective-permute-start = (f32[7,64]{1,0:T(8,128)S(1)}, f32[7,64]{1,0:T(8,128)S(1)}, u32[]{:S(2)}, u32[]{:S(2)}) collective-permute-start(f32[7,64]{1,0:T(8,128)S(1)} %fusion), channel_id=1, source_target_pairs={{0,1},{1,0},{2,3},{3,2},{4,5},{5,4},{6,7},{7,6},{8,9},{9,8},{10,11... | collective-permute-start | bytes 5384 | tf_op jit(solution)/shard_map/ppermute | solution.py:267
  35.4 4.9 %collective-permute-start.1 = (f32[7,64]{1,0:T(8,128)S(1)}, f32[7,64]{1,0:T(8,128)S(1)}, u32[]{:S(2)}, u32[]{:S(2)}) collective-permute-start(f32[7,64]{1,0:T(8,128)S(1)} %bitcast_add_fusion), channel_id=1, source_target_pairs={{0,2},{1,3},{2,0},{3,1},{4,6},{5,7},{6,4},{7,5},{8,10},{9,11},{10,... | collective-permute-start | bytes 5384 | tf_op jit(solution)/shard_map/ppermute | solution.py:267
  40.4 7.5 %collective-permute-start.2 = (f32[7,64]{1,0:T(8,128)S(1)}, f32[7,64]{1,0:T(8,128)S(1)}, u32[]{:S(2)}, u32[]{:S(2)}) collective-permute-start(f32[7,64]{1,0:T(8,128)S(1)} %add.22), channel_id=1, source_target_pairs={{0,4},{1,5},{2,6},{3,7},{4,0},{5,1},{6,2},{7,3},{8,12},{9,13},{10,... | collective-permute-start | bytes 5384 | tf_op jit(solution)/shard_map/ppermute | solution.py:267

commit v9 on v7

--- a/solution.py
+++ b/solution.py
@@ -171,7 +171,9 @@
         buf[:, :tail_len] = jnp.where(keep, tail, jnp.float32(0.0))
         buf[:, tail_len:] = jnp.dot(order, block_ref[...], preferred_element_type=jnp.float32)
         tree_in_place(buf, mid_ref, rows, 1, 0, TILE)
-        o_ref[...] = swap_blocks(buf[...], TILE)
+        buf[...] = swap_blocks(buf[...], TILE)
+        for r in range(rows):
+            o_ref[r] = buf[r : r + 1, :]
 
     table_spec = pl.BlockSpec((rows, rows), lambda b: (0, 0))
     return pl.pallas_call(
@@ -185,10 +187,12 @@
             table_spec,
             table_spec,
         ],
-        out_specs=pl.BlockSpec((None, rows, length), lambda b: (b, 0, 0)),
-        out_shape=jax.ShapeDtypeStruct((beams_dev, rows, length), jnp.float32),
+        out_specs=pl.BlockSpec((None, rows, 1, length), lambda b: (b, 0, 0, 0)),
+        out_shape=jax.ShapeDtypeStruct((beams_dev, rows, 1, length), jnp.float32),
         scratch_shapes=[pltpu.VMEM((rows, length), jnp.float32)],
-    )(tail_blocks.astype(jnp.int32), tail_samples, block_samples, entry, mid, leave)
+    )(tail_blocks.astype(jnp.int32), tail_samples, block_samples, entry, mid, leave).reshape(
+        beams_dev, rows, length
+    )
 
 
 def peaks_of(dm_rows, tail_len, block_len, leave):

time: 48.5 us -> 46 us (0.948)
  local copies, waits for them, and re-layouts: 4.52 us -> 2.04 us
    broadcast_in_dim x1 -> x0, local copies, waits for them, and re-layouts: 2.49 us -> none  [local(): series = local_tree(tail_samples, block_samples, tail_blocks)[:, None]]
where the time goes in v9:
time: 46 us; the launch traced here: 45.7 us
  waiting for transfers between devices  17.2 us (37%)
  starting transfers between devices  16.7 us (36%)
  Pallas kernels  7.04 us (15%)
  local copies, waits for them, and re-layouts  2.04 us (4%)
  between operations  1.95 us (4%)
  other arithmetic  0.77 us (2%)
    all_to_all x1, waiting for transfers between devices, local(): lax.all_to_all(series, 'freq', split_axis=2, concat_axis=1, tiled=True)  11.1 us
    ppermute x3, starting transfers between devices, local(): beam_total = beam_total + lax.ppermute(beam_total, 'beam', pairs)  9.39 us
    all_to_all x1, starting transfers between devices, local(): lax.all_to_all(series, 'freq', split_axis=2, concat_axis=1, tiled=True)  7.32 us
    ppermute x3, waiting for transfers between devices, local(): beam_total = beam_total + lax.ppermute(beam_total, 'beam', pairs)  6.08 us
    pallas_call x1, Pallas kernels, merge_tree(): pl.pallas_call(body, grid=(beams_dev,), in_specs=[pl.BlockSpec(memory_spa...  4 us
    pallas_call x1, Pallas kernels, local_tree(): pl.pallas_call(body, grid=(beams_dev,), in_specs=[pl.BlockSpec(memory_spa...  3.04 us
    unnamed x5, local copies, waits for them, and re-layouts  2.04 us
  transfers between devices with their start and end apart: 4, of which 4 were waited for; matrix products, arithmetic and copies ran while one was open for 1% of the time, Pallas kernels for 0%

profile of v9, /device:TPU:32, one launch (start us, length us, event | category | flops | bytes accessed | tf_op | source)
XLA Modules:
  0.0 45.7 jit_solution(6018332530398419987)
XLA Ops:
  1.3 3.0 %shard_map.113 = f32[1,64,1,2304]{3,2,1,0:T(1,128)} custom-call(s32[1]{0:T(128)S(6)} %copy.20.count_ref, bf16[1,64,2048]{2,1,0:T(8,128)(2,1)} %tail_ref.1, bf16[1,64,256]{2,1,0:T(8,128)(2,1)} %block_ref.1, f32[64,64]{1,0:T(8,128)} %constant.19.clone.entry_ref, f32[64,64]{1,0:T(8,128)} %constant.20.clone.mid_ref.leave_ref, ...), custom_call_target="tpu_custom_call" | custom-call | tf_op jit(solution)/shard_map/pallas_call | solution.py:179
  4.3 7.3 %all-to-all-start = ((f32[1,1,64,2304]{3,1,0,2:T(1,128)}), f32[1,1,64,2304]{3,1,0,2:T(1,128)S(1)}, u32[]{:S(2)}, u32[]{:S(2)}) async-start(f32[1,1,64,2304]{3,1,0,2:T(1,128)} %bitcast.14), calls=%async_computation | async-start | bytes 1179648 | tf_op jit(solution)/shard_map/all_to_all | solution.py:251
  12.3 11.1 %all-to-all-done = f32[1,1,64,2304]{3,1,0,2:T(1,128)S(1)} async-done(((f32[1,1,64,2304]{3,1,0,2:T(1,128)}), f32[1,1,64,2304]{3,1,0,2:T(1,128)S(1)}, u32[]{:S(2)}, u32[]{:S(2)}) %all-to-all-start) | async-done | bytes 589856 | tf_op jit(solution)/shard_map/all_to_all | solution.py:251
  23.5 0.9 %copy.19 = f32[1,1,64,2304]{3,2,0,1:T(8,128)} copy(f32[1,1,64,2304]{3,1,0,2:T(1,128)S(1)} %all-to-all-done) | data formatting | bytes 1179648
  24.3 4.0 %shard_map.114 = f32[1,8,64]{2,1,0:T(8,128)} custom-call(s32[1]{0:T(128)} %bitcast.1.off_ref, f32[1,64,2304]{2,1,0:T(8,128)} %bitcast.15, f32[64,64]{1,0:T(8,128)} %constant.19.clone.entry_ref, f32[64,64]{1,0:T(8,128)} %constant.20.clone.mid_ref.leave_ref, f32[64,64]{1,0:T(8,128)} %constant.20.clone.mid_ref.leave_ref), custom_call_target="tpu_custom_call" | custom-call | tf_op jit(solution)/shard_map/pallas_call | solution.py:229
  28.3 0.0 copy-start
  28.3 0.7 %fusion = f32[7,64]{1,0:T(8,128)S(1)} fusion(f32[1,8,64]{2,1,0:T(8,128)} %shard_map.114, pred[64]{0:T(512)(128)(4,1)S(1)} %add_compare_fusion), kind=kLoop, calls=%fused_computation.5 | loop fusion | flops 448 | bytes 3648 | tf_op jit(solution)/shard_map/reduce_sum | solution.py:259
  29.1 0.1 collective-permute-start
  29.2 3.5 %collective-permute-done = f32[7,64]{1,0:T(8,128)S(1)} collective-permute-done((f32[7,64]{1,0:T(8,128)S(1)}, f32[7,64]{1,0:T(8,128)S(1)}, u32[]{:S(2)}, u32[]{:S(2)}) %collective-permute-start) | collective-permute-done | bytes 1824 | tf_op jit(solution)/shard_map/ppermute | solution.py:263
  32.7 0.0 copy-done
  32.7 3.3 %collective-permute-start.1 = (f32[7,64]{1,0:T(8,128)S(1)}, f32[7,64]{1,0:T(8,128)S(1)}, u32[]{:S(2)}, u32[]{:S(2)}) collective-permute-start(f32[7,64]{1,0:T(8,128)S(1)} %bitcast_add_fusion), channel_id=1, source_target_pairs={{0,2},{1,3},{2,0},{3,1},{4,6},{5,7},{6,4},{7,5},{8,10},{9,11},{10,... | collective-permute-start | bytes 5384 | tf_op jit(solution)/shard_map/ppermute | solution.py:263
  36.0 1.6 %collective-permute-done.1 = f32[7,64]{1,0:T(8,128)S(1)} collective-permute-done((f32[7,64]{1,0:T(8,128)S(1)}, f32[7,64]{1,0:T(8,128)S(1)}, u32[]{:S(2)}, u32[]{:S(2)}) %collective-permute-start.1) | collective-permute-done | bytes 1824 | tf_op jit(solution)/shard_map/ppermute | solution.py:263
  37.6 5.9 %collective-permute-start.2 = (f32[7,64]{1,0:T(8,128)S(1)}, f32[7,64]{1,0:T(8,128)S(1)}, u32[]{:S(2)}, u32[]{:S(2)}) collective-permute-start(f32[7,64]{1,0:T(8,128)S(1)} %add.22), channel_id=1, source_target_pairs={{0,4},{1,5},{2,6},{3,7},{4,0},{5,1},{6,2},{7,3},{8,12},{9,13},{10,... | collective-permute-start | bytes 5384 | tf_op jit(solution)/shard_map/ppermute | solution.py:263
  43.6 0.6 %copy.15 = f32[1,7,64]{2,0,1:T(1,128)} copy(f32[1,7,64]{2,1,0:T(8,128)S(1)} %slice_select_fusion) | data formatting | bytes 3584
  44.1 1.0 %collective-permute-done.2 = f32[7,64]{1,0:T(8,128)S(1)} collective-permute-done((f32[7,64]{1,0:T(8,128)S(1)}, f32[7,64]{1,0:T(8,128)S(1)}, u32[]{:S(2)}, u32[]{:S(2)}) %collective-permute-start.2) | collective-permute-done | bytes 1824 | tf_op jit(solution)/shard_map/ppermute | solution.py:263
  45.1 0.6 %copy.16 = f32[1,7,64]{2,0,1:T(1,128)} copy(f32[1,7,64]{2,1,0:T(8,128)S(1)} %bitcast_subtract_fusion) | data formatting | bytes 3584
  (5 shorter events, 0.0 us)
Async XLA Ops:
  4.3 19.1 %all-to-all-start = ((f32[1,1,64,2304]{3,1,0,2:T(1,128)}), f32[1,1,64,2304]{3,1,0,2:T(1,128)S(1)}, u32[]{:S(2)}, u32[]{:S(2)}) async-start(f32[1,1,64,2304]{3,1,0,2:T(1,128)} %bitcast.14), calls=%async_computation | async-start | bytes 1179648 | tf_op jit(solution)/shard_map/all_to_all | solution.py:251
  28.3 4.4 %copy-start = (f32[1,8,64]{2,1,0:T(8,128)S(1)}, f32[1,8,64]{2,1,0:T(8,128)}, u32[]{:S(2)}) copy-start(f32[1,8,64]{2,1,0:T(8,128)} %shard_map.114) | copy-start | bytes 6148
  29.1 3.6 %collective-permute-start = (f32[7,64]{1,0:T(8,128)S(1)}, f32[7,64]{1,0:T(8,128)S(1)}, u32[]{:S(2)}, u32[]{:S(2)}) collective-permute-start(f32[7,64]{1,0:T(8,128)S(1)} %fusion), channel_id=1, source_target_pairs={{0,1},{1,0},{2,3},{3,2},{4,5},{5,4},{6,7},{7,6},{8,9},{9,8},{10,11... | collective-permute-start | bytes 5384 | tf_op jit(solution)/shard_map/ppermute | solution.py:263
  32.7 4.9 %collective-permute-start.1 = (f32[7,64]{1,0:T(8,128)S(1)}, f32[7,64]{1,0:T(8,128)S(1)}, u32[]{:S(2)}, u32[]{:S(2)}) collective-permute-start(f32[7,64]{1,0:T(8,128)S(1)} %bitcast_add_fusion), channel_id=1, source_target_pairs={{0,2},{1,3},{2,0},{3,1},{4,6},{5,7},{6,4},{7,5},{8,10},{9,11},{10,... | collective-permute-start | bytes 5384 | tf_op jit(solution)/shard_map/ppermute | solution.py:263
  37.6 7.5 %collective-permute-start.2 = (f32[7,64]{1,0:T(8,128)S(1)}, f32[7,64]{1,0:T(8,128)S(1)}, u32[]{:S(2)}, u32[]{:S(2)}) collective-permute-start(f32[7,64]{1,0:T(8,128)S(1)} %add.22), channel_id=1, source_target_pairs={{0,4},{1,5},{2,6},{3,7},{4,0},{5,1},{6,2},{7,3},{8,12},{9,13},{10,... | collective-permute-start | bytes 5384 | tf_op jit(solution)/shard_map/ppermute | solution.py:263

commit v10 on v9

--- a/solution.py
+++ b/solution.py
@@ -219,12 +219,17 @@
     rows = subbands * trials
     entry, mid, leave = tables(subbands, trials, TILE)
 
+    order = bit_reversed(subbands)
+
     def body(off_ref, x_ref, entry_ref, mid_ref, leave_ref, o_ref, buf):
-        buf[...] = permute_rows(entry_ref[...], x_ref[...])
+        for pos in range(subbands):
+            for trial in range(trials):
+                source = int(order[pos]) * trials + trial
+                buf[trial * subbands + pos : trial * subbands + pos + 1, :] = x_ref[source]
         tree_in_place(buf, mid_ref, subbands, trials, off_ref[0], TILE)
         o_ref[...] = peaks_of(buf[...], tail_len, length - tail_len, leave_ref[...])
 
-    spec = pl.BlockSpec((None, rows, length), lambda b: (b, 0, 0))
+    spec = pl.BlockSpec((None, rows, 1, length), lambda b: (b, 0, 0, 0))
     table_spec = pl.BlockSpec((rows, rows), lambda b: (0, 0))
     return pl.pallas_call(
         body,
@@ -235,7 +240,7 @@
         scratch_shapes=[pltpu.VMEM((rows, length), jnp.float32)],
     )(
         jnp.reshape(first_trial, (1,)).astype(jnp.int32),
-        parts.reshape(beams_dev, rows, length),
+        parts.reshape(beams_dev, rows, 1, length),
         entry,
         mid,
         leave,

time: 46 us -> 45.9 us (level)
    unnamed x5 -> x6, local copies, waits for them, and re-layouts: 2.04 us -> 1.99 us
where the time goes in v10:
time: 45.9 us; the launch traced here: 45.6 us
  waiting for transfers between devices  17.2 us (37%)
  starting transfers between devices  16.7 us (36%)
  Pallas kernels  6.91 us (15%)
  local copies, waits for them, and re-layouts  1.99 us (4%)
  between operations  1.95 us (4%)
  other arithmetic  0.78 us (2%)
    all_to_all x1, waiting for transfers between devices, local(): lax.all_to_all(series, 'freq', split_axis=2, concat_axis=1, tiled=True)  11.1 us
    ppermute x3, starting transfers between devices, local(): beam_total = beam_total + lax.ppermute(beam_total, 'beam', pairs)  9.4 us
    all_to_all x1, starting transfers between devices, local(): lax.all_to_all(series, 'freq', split_axis=2, concat_axis=1, tiled=True)  7.32 us
    ppermute x3, waiting for transfers between devices, local(): beam_total = beam_total + lax.ppermute(beam_total, 'beam', pairs)  6.08 us
    pallas_call x1, Pallas kernels, merge_tree(): pl.pallas_call(body, grid=(beams_dev,), in_specs=[pl.BlockSpec(memory_spa...  3.88 us
    pallas_call x1, Pallas kernels, local_tree(): pl.pallas_call(body, grid=(beams_dev,), in_specs=[pl.BlockSpec(memory_spa...  3.04 us
    unnamed x6, local copies, waits for them, and re-layouts  1.99 us
  transfers between devices with their start and end apart: 4, of which 4 were waited for; matrix products, arithmetic and copies ran while one was open for 1% of the time, Pallas kernels for 0%

profile of v10, /device:TPU:32, one launch (start us, length us, event | category | flops | bytes accessed | tf_op | source)
XLA Modules:
  0.0 45.6 jit_solution(10168836626267187486)
XLA Ops:
  1.3 3.0 %shard_map.113 = f32[1,64,1,2304]{3,2,1,0:T(1,128)} custom-call(s32[1]{0:T(128)S(6)} %copy.17.count_ref, bf16[1,64,2048]{2,1,0:T(8,128)(2,1)} %tail_ref.1, bf16[1,64,256]{2,1,0:T(8,128)(2,1)} %block_ref.1, f32[64,64]{1,0:T(8,128)} %constant.19.clone.entry_ref, f32[64,64]{1,0:T(8,128)} %constant.20.clone.mid_ref.leave_ref, ...), custom_call_target="tpu_custom_call" | custom-call | tf_op jit(solution)/shard_map/pallas_call | solution.py:179
  4.3 7.3 %all-to-all-start = ((f32[1,1,64,2304]{3,0,1,2:T(1,128)}), f32[1,1,64,2304]{3,0,1,2:T(1,128)S(1)}, u32[]{:S(2)}, u32[]{:S(2)}) async-start(f32[1,1,64,2304]{3,0,1,2:T(1,128)} %bitcast.13), calls=%async_computation | async-start | bytes 1179648 | tf_op jit(solution)/shard_map/all_to_all | solution.py:256
  12.3 11.1 %all-to-all-done = f32[1,1,64,2304]{3,0,1,2:T(1,128)S(1)} async-done(((f32[1,1,64,2304]{3,0,1,2:T(1,128)}), f32[1,1,64,2304]{3,0,1,2:T(1,128)S(1)}, u32[]{:S(2)}, u32[]{:S(2)}) %all-to-all-start) | async-done | bytes 589856 | tf_op jit(solution)/shard_map/all_to_all | solution.py:256
  23.4 0.0 copy-start
  23.5 0.8 %copy-done = f32[1,1,64,2304]{3,0,1,2:T(1,128)} copy-done((f32[1,1,64,2304]{3,0,1,2:T(1,128)}, f32[1,1,64,2304]{3,0,1,2:T(1,128)S(1)}, u32[]{:S(2)}) %copy-start) | copy-done | bytes 589848
  24.3 3.9 %shard_map.114 = f32[1,8,64]{2,1,0:T(8,128)} custom-call(s32[1]{0:T(128)} %bitcast.1.off_ref, f32[1,64,1,2304]{3,2,1,0:T(1,128)} %bitcast.12, f32[64,64]{1,0:T(8,128)} %constant.19.clone.entry_ref, f32[64,64]{1,0:T(8,128)} %constant.20.clone.mid_ref.leave_ref, f32[64,64]{1,0:T(8,128)} %constant.20.clone.mid_ref.leave_ref), custom_call_target="tpu_custom_call" | custom-call | tf_op jit(solution)/shard_map/pallas_call | solution.py:234
  28.1 0.0 copy-start.1
  28.1 0.8 %fusion = f32[7,64]{1,0:T(8,128)S(1)} fusion(f32[1,8,64]{2,1,0:T(8,128)} %shard_map.114, pred[64]{0:T(512)(128)(4,1)S(1)} %add_compare_fusion), kind=kLoop, calls=%fused_computation.4 | loop fusion | flops 448 | bytes 3648 | tf_op jit(solution)/shard_map/reduce_sum | solution.py:264
  28.9 0.1 collective-permute-start
  29.0 3.5 %collective-permute-done = f32[7,64]{1,0:T(8,128)S(1)} collective-permute-done((f32[7,64]{1,0:T(8,128)S(1)}, f32[7,64]{1,0:T(8,128)S(1)}, u32[]{:S(2)}, u32[]{:S(2)}) %collective-permute-start) | collective-permute-done | bytes 1824 | tf_op jit(solution)/shard_map/ppermute | solution.py:268
  32.5 0.0 copy-done.1
  32.5 3.4 %collective-permute-start.1 = (f32[7,64]{1,0:T(8,128)S(1)}, f32[7,64]{1,0:T(8,128)S(1)}, u32[]{:S(2)}, u32[]{:S(2)}) collective-permute-start(f32[7,64]{1,0:T(8,128)S(1)} %bitcast_add_fusion), channel_id=1, source_target_pairs={{0,2},{1,3},{2,0},{3,1},{4,6},{5,7},{6,4},{7,5},{8,10},{9,11},{10,... | collective-permute-start | bytes 5384 | tf_op jit(solution)/shard_map/ppermute | solution.py:268
  35.9 1.6 %collective-permute-done.1 = f32[7,64]{1,0:T(8,128)S(1)} collective-permute-done((f32[7,64]{1,0:T(8,128)S(1)}, f32[7,64]{1,0:T(8,128)S(1)}, u32[]{:S(2)}, u32[]{:S(2)}) %collective-permute-start.1) | collective-permute-done | bytes 1824 | tf_op jit(solution)/shard_map/ppermute | solution.py:268
  37.5 5.9 %collective-permute-start.2 = (f32[7,64]{1,0:T(8,128)S(1)}, f32[7,64]{1,0:T(8,128)S(1)}, u32[]{:S(2)}, u32[]{:S(2)}) collective-permute-start(f32[7,64]{1,0:T(8,128)S(1)} %add.22), channel_id=1, source_target_pairs={{0,4},{1,5},{2,6},{3,7},{4,0},{5,1},{6,2},{7,3},{8,12},{9,13},{10,... | collective-permute-start | bytes 5384 | tf_op jit(solution)/shard_map/ppermute | solution.py:268
  43.4 0.6 %copy.15 = f32[1,7,64]{2,0,1:T(1,128)} copy(f32[1,7,64]{2,1,0:T(8,128)S(1)} %slice_select_fusion) | data formatting | bytes 3584
  44.0 1.0 %collective-permute-done.2 = f32[7,64]{1,0:T(8,128)S(1)} collective-permute-done((f32[7,64]{1,0:T(8,128)S(1)}, f32[7,64]{1,0:T(8,128)S(1)}, u32[]{:S(2)}, u32[]{:S(2)}) %collective-permute-start.2) | collective-permute-done | bytes 1824 | tf_op jit(solution)/shard_map/ppermute | solution.py:268
  45.0 0.6 %copy.16 = f32[1,7,64]{2,0,1:T(1,128)} copy(f32[1,7,64]{2,1,0:T(8,128)S(1)} %bitcast_subtract_fusion) | data formatting | bytes 3584
  (5 shorter events, 0.0 us)
Async XLA Ops:
  4.3 19.1 %all-to-all-start = ((f32[1,1,64,2304]{3,0,1,2:T(1,128)}), f32[1,1,64,2304]{3,0,1,2:T(1,128)S(1)}, u32[]{:S(2)}, u32[]{:S(2)}) async-start(f32[1,1,64,2304]{3,0,1,2:T(1,128)} %bitcast.13), calls=%async_computation | async-start | bytes 1179648 | tf_op jit(solution)/shard_map/all_to_all | solution.py:256
  23.4 0.8 %copy-start = (f32[1,1,64,2304]{3,0,1,2:T(1,128)}, f32[1,1,64,2304]{3,0,1,2:T(1,128)S(1)}, u32[]{:S(2)}) copy-start(f32[1,1,64,2304]{3,0,1,2:T(1,128)S(1)} %all-to-all-done) | copy-start | bytes 1769476
  28.1 4.4 %copy-start.1 = (f32[1,8,64]{2,1,0:T(8,128)S(1)}, f32[1,8,64]{2,1,0:T(8,128)}, u32[]{:S(2)}) copy-start(f32[1,8,64]{2,1,0:T(8,128)} %shard_map.114) | copy-start | bytes 6148
  28.9 3.6 %collective-permute-start = (f32[7,64]{1,0:T(8,128)S(1)}, f32[7,64]{1,0:T(8,128)S(1)}, u32[]{:S(2)}, u32[]{:S(2)}) collective-permute-start(f32[7,64]{1,0:T(8,128)S(1)} %fusion), channel_id=1, source_target_pairs={{0,1},{1,0},{2,3},{3,2},{4,5},{5,4},{6,7},{7,6},{8,9},{9,8},{10,11... | collective-permute-start | bytes 5384 | tf_op jit(solution)/shard_map/ppermute | solution.py:268
  32.5 4.9 %collective-permute-start.1 = (f32[7,64]{1,0:T(8,128)S(1)}, f32[7,64]{1,0:T(8,128)S(1)}, u32[]{:S(2)}, u32[]{:S(2)}) collective-permute-start(f32[7,64]{1,0:T(8,128)S(1)} %bitcast_add_fusion), channel_id=1, source_target_pairs={{0,2},{1,3},{2,0},{3,1},{4,6},{5,7},{6,4},{7,5},{8,10},{9,11},{10,... | collective-permute-start | bytes 5384 | tf_op jit(solution)/shard_map/ppermute | solution.py:268
  37.5 7.5 %collective-permute-start.2 = (f32[7,64]{1,0:T(8,128)S(1)}, f32[7,64]{1,0:T(8,128)S(1)}, u32[]{:S(2)}, u32[]{:S(2)}) collective-permute-start(f32[7,64]{1,0:T(8,128)S(1)} %add.22), channel_id=1, source_target_pairs={{0,4},{1,5},{2,6},{3,7},{4,0},{5,1},{6,2},{7,3},{8,12},{9,13},{10,... | collective-permute-start | bytes 5384 | tf_op jit(solution)/shard_map/ppermute | solution.py:268

commit v11 on v10

--- a/solution.py
+++ b/solution.py
@@ -264,7 +264,11 @@
     beam_total = jnp.sum(peak_snr, axis=0)
     beam_count = lax.axis_size("beam")
     for level_bit in range(beam_count.bit_length() - 1):
-        pairs = [(i, i ^ (1 << level_bit)) for i in range(beam_count)]
+        span = 1 << level_bit
+        if 2 * span == beam_count:
+            pairs = [(i, beam_count - 1 - i) for i in range(beam_count)]
+        else:
+            pairs = [(i, i ^ span) for i in range(beam_count)]
         beam_total = beam_total + lax.ppermute(beam_total, "beam", pairs)
     excess_snr = peak_snr - beam_total[None] / (beams_dev * lax.axis_size("beam"))
     return (peak_snr, excess_snr)

time: 45.9 us -> 45.4 us (0.989)
  no operation moved by 1% of the time
where the time goes in v11:
time: 45.4 us; the launch traced here: 45.1 us
  waiting for transfers between devices  17.2 us (38%)
  starting transfers between devices  16.3 us (36%)
  Pallas kernels  6.91 us (15%)
  local copies, waits for them, and re-layouts  1.99 us (4%)
  between operations  1.95 us (4%)
  other arithmetic  0.78 us (2%)
    all_to_all x1, waiting for transfers between devices, local(): lax.all_to_all(series, 'freq', split_axis=2, concat_axis=1, tiled=True)  11.1 us
    ppermute x3, starting transfers between devices, local(): beam_total = beam_total + lax.ppermute(beam_total, 'beam', pairs)  8.95 us
    all_to_all x1, starting transfers between devices, local(): lax.all_to_all(series, 'freq', split_axis=2, concat_axis=1, tiled=True)  7.32 us
    ppermute x3, waiting for transfers between devices, local(): beam_total = beam_total + lax.ppermute(beam_total, 'beam', pairs)  6.08 us
    pallas_call x1, Pallas kernels, merge_tree(): pl.pallas_call(body, grid=(beams_dev,), in_specs=[pl.BlockSpec(memory_spa...  3.88 us
    pallas_call x1, Pallas kernels, local_tree(): pl.pallas_call(body, grid=(beams_dev,), in_specs=[pl.BlockSpec(memory_spa...  3.04 us
    unnamed x6, local copies, waits for them, and re-layouts  1.99 us
  transfers between devices with their start and end apart: 4, of which 4 were waited for; matrix products, arithmetic and copies ran while one was open for 1% of the time, Pallas kernels for 0%

profile of v11, /device:TPU:32, one launch (start us, length us, event | category | flops | bytes accessed | tf_op | source)
XLA Modules:
  0.0 45.1 jit_solution(8742067384275128242)
XLA Ops:
  1.3 3.0 %shard_map.113 = f32[1,64,1,2304]{3,2,1,0:T(1,128)} custom-call(s32[1]{0:T(128)S(6)} %copy.17.count_ref, bf16[1,64,2048]{2,1,0:T(8,128)(2,1)} %tail_ref.1, bf16[1,64,256]{2,1,0:T(8,128)(2,1)} %block_ref.1, f32[64,64]{1,0:T(8,128)} %constant.19.clone.entry_ref, f32[64,64]{1,0:T(8,128)} %constant.20.clone.mid_ref.leave_ref, ...), custom_call_target="tpu_custom_call" | custom-call | tf_op jit(solution)/shard_map/pallas_call | solution.py:179
  4.3 7.3 %all-to-all-start = ((f32[1,1,64,2304]{3,0,1,2:T(1,128)}), f32[1,1,64,2304]{3,0,1,2:T(1,128)S(1)}, u32[]{:S(2)}, u32[]{:S(2)}) async-start(f32[1,1,64,2304]{3,0,1,2:T(1,128)} %bitcast.13), calls=%async_computation | async-start | bytes 1179648 | tf_op jit(solution)/shard_map/all_to_all | solution.py:256
  12.3 11.1 %all-to-all-done = f32[1,1,64,2304]{3,0,1,2:T(1,128)S(1)} async-done(((f32[1,1,64,2304]{3,0,1,2:T(1,128)}), f32[1,1,64,2304]{3,0,1,2:T(1,128)S(1)}, u32[]{:S(2)}, u32[]{:S(2)}) %all-to-all-start) | async-done | bytes 589856 | tf_op jit(solution)/shard_map/all_to_all | solution.py:256
  23.4 0.0 copy-start
  23.5 0.8 %copy-done = f32[1,1,64,2304]{3,0,1,2:T(1,128)} copy-done((f32[1,1,64,2304]{3,0,1,2:T(1,128)}, f32[1,1,64,2304]{3,0,1,2:T(1,128)S(1)}, u32[]{:S(2)}) %copy-start) | copy-done | bytes 589848
  24.3 3.9 %shard_map.114 = f32[1,8,64]{2,1,0:T(8,128)} custom-call(s32[1]{0:T(128)} %bitcast.1.off_ref, f32[1,64,1,2304]{3,2,1,0:T(1,128)} %bitcast.12, f32[64,64]{1,0:T(8,128)} %constant.19.clone.entry_ref, f32[64,64]{1,0:T(8,128)} %constant.20.clone.mid_ref.leave_ref, f32[64,64]{1,0:T(8,128)} %constant.20.clone.mid_ref.leave_ref), custom_call_target="tpu_custom_call" | custom-call | tf_op jit(solution)/shard_map/pallas_call | solution.py:234
  28.1 0.0 copy-start.1
  28.1 0.8 %fusion = f32[7,64]{1,0:T(8,128)S(1)} fusion(f32[1,8,64]{2,1,0:T(8,128)} %shard_map.114, pred[64]{0:T(512)(128)(4,1)S(1)} %add_compare_fusion), kind=kLoop, calls=%fused_computation.4 | loop fusion | flops 448 | bytes 3648 | tf_op jit(solution)/shard_map/reduce_sum | solution.py:264
  28.9 0.1 collective-permute-start
  29.0 3.5 %collective-permute-done = f32[7,64]{1,0:T(8,128)S(1)} collective-permute-done((f32[7,64]{1,0:T(8,128)S(1)}, f32[7,64]{1,0:T(8,128)S(1)}, u32[]{:S(2)}, u32[]{:S(2)}) %collective-permute-start) | collective-permute-done | bytes 1824 | tf_op jit(solution)/shard_map/ppermute | solution.py:272
  32.5 0.0 copy-done.1
  32.5 3.4 %collective-permute-start.1 = (f32[7,64]{1,0:T(8,128)S(1)}, f32[7,64]{1,0:T(8,128)S(1)}, u32[]{:S(2)}, u32[]{:S(2)}) collective-permute-start(f32[7,64]{1,0:T(8,128)S(1)} %bitcast_add_fusion), channel_id=1, source_target_pairs={{0,2},{1,3},{2,0},{3,1},{4,6},{5,7},{6,4},{7,5},{8,10},{9,11},{10,... | collective-permute-start | bytes 5384 | tf_op jit(solution)/shard_map/ppermute | solution.py:272
  35.9 1.6 %collective-permute-done.1 = f32[7,64]{1,0:T(8,128)S(1)} collective-permute-done((f32[7,64]{1,0:T(8,128)S(1)}, f32[7,64]{1,0:T(8,128)S(1)}, u32[]{:S(2)}, u32[]{:S(2)}) %collective-permute-start.1) | collective-permute-done | bytes 1824 | tf_op jit(solution)/shard_map/ppermute | solution.py:272
  37.5 5.5 %collective-permute-start.2 = (f32[7,64]{1,0:T(8,128)S(1)}, f32[7,64]{1,0:T(8,128)S(1)}, u32[]{:S(2)}, u32[]{:S(2)}) collective-permute-start(f32[7,64]{1,0:T(8,128)S(1)} %add.22), channel_id=1, source_target_pairs={{0,7},{1,6},{2,5},{3,4},{4,3},{5,2},{6,1},{7,0},{8,15},{9,14},{10,... | collective-permute-start | bytes 5384 | tf_op jit(solution)/shard_map/ppermute | solution.py:272
  43.0 0.6 %copy.15 = f32[1,7,64]{2,0,1:T(1,128)} copy(f32[1,7,64]{2,1,0:T(8,128)S(1)} %slice_select_fusion) | data formatting | bytes 3584
  43.6 1.0 %collective-permute-done.2 = f32[7,64]{1,0:T(8,128)S(1)} collective-permute-done((f32[7,64]{1,0:T(8,128)S(1)}, f32[7,64]{1,0:T(8,128)S(1)}, u32[]{:S(2)}, u32[]{:S(2)}) %collective-permute-start.2) | collective-permute-done | bytes 1824 | tf_op jit(solution)/shard_map/ppermute | solution.py:272
  44.6 0.6 %copy.16 = f32[1,7,64]{2,0,1:T(1,128)} copy(f32[1,7,64]{2,1,0:T(8,128)S(1)} %bitcast_subtract_fusion) | data formatting | bytes 3584
  (5 shorter events, 0.0 us)
Async XLA Ops:
  4.3 19.1 %all-to-all-start = ((f32[1,1,64,2304]{3,0,1,2:T(1,128)}), f32[1,1,64,2304]{3,0,1,2:T(1,128)S(1)}, u32[]{:S(2)}, u32[]{:S(2)}) async-start(f32[1,1,64,2304]{3,0,1,2:T(1,128)} %bitcast.13), calls=%async_computation | async-start | bytes 1179648 | tf_op jit(solution)/shard_map/all_to_all | solution.py:256
  23.4 0.8 %copy-start = (f32[1,1,64,2304]{3,0,1,2:T(1,128)}, f32[1,1,64,2304]{3,0,1,2:T(1,128)S(1)}, u32[]{:S(2)}) copy-start(f32[1,1,64,2304]{3,0,1,2:T(1,128)S(1)} %all-to-all-done) | copy-start | bytes 1769476
  28.1 4.4 %copy-start.1 = (f32[1,8,64]{2,1,0:T(8,128)S(1)}, f32[1,8,64]{2,1,0:T(8,128)}, u32[]{:S(2)}) copy-start(f32[1,8,64]{2,1,0:T(8,128)} %shard_map.114) | copy-start | bytes 6148
  28.9 3.6 %collective-permute-start = (f32[7,64]{1,0:T(8,128)S(1)}, f32[7,64]{1,0:T(8,128)S(1)}, u32[]{:S(2)}, u32[]{:S(2)}) collective-permute-start(f32[7,64]{1,0:T(8,128)S(1)} %fusion), channel_id=1, source_target_pairs={{0,1},{1,0},{2,3},{3,2},{4,5},{5,4},{6,7},{7,6},{8,9},{9,8},{10,11... | collective-permute-start | bytes 5384 | tf_op jit(solution)/shard_map/ppermute | solution.py:272
  32.5 4.9 %collective-permute-start.1 = (f32[7,64]{1,0:T(8,128)S(1)}, f32[7,64]{1,0:T(8,128)S(1)}, u32[]{:S(2)}, u32[]{:S(2)}) collective-permute-start(f32[7,64]{1,0:T(8,128)S(1)} %bitcast_add_fusion), channel_id=1, source_target_pairs={{0,2},{1,3},{2,0},{3,1},{4,6},{5,7},{6,4},{7,5},{8,10},{9,11},{10,... | collective-permute-start | bytes 5384 | tf_op jit(solution)/shard_map/ppermute | solution.py:272
  37.5 7.1 %collective-permute-start.2 = (f32[7,64]{1,0:T(8,128)S(1)}, f32[7,64]{1,0:T(8,128)S(1)}, u32[]{:S(2)}, u32[]{:S(2)}) collective-permute-start(f32[7,64]{1,0:T(8,128)S(1)} %add.22), channel_id=1, source_target_pairs={{0,7},{1,6},{2,5},{3,4},{4,3},{5,2},{6,1},{7,0},{8,15},{9,14},{10,... | collective-permute-start | bytes 5384 | tf_op jit(solution)/shard_map/ppermute | solution.py:272

commit v12 on v10

--- a/solution.py
+++ b/solution.py
@@ -263,9 +263,13 @@
     )
     beam_total = jnp.sum(peak_snr, axis=0)
     beam_count = lax.axis_size("beam")
-    for level_bit in range(beam_count.bit_length() - 1):
-        pairs = [(i, i ^ (1 << level_bit)) for i in range(beam_count)]
-        beam_total = beam_total + lax.ppermute(beam_total, "beam", pairs)
+    terms = [beam_total] + [
+        lax.ppermute(beam_total, "beam", [(i, (i + step) % beam_count) for i in range(beam_count)])
+        for step in range(1, beam_count)
+    ]
+    while len(terms) > 1:
+        terms = [terms[i] + terms[i + 1] for i in range(0, len(terms) - 1, 2)] + terms[len(terms) - len(terms) % 2 :]
+    beam_total = terms[0]
     excess_snr = peak_snr - beam_total[None] / (beams_dev * lax.axis_size("beam"))
     return (peak_snr, excess_snr)
 

time: 45.9 us -> 50.2 us (1.094)
  the two profiles are of different devices: /device:TPU:32 before, /device:TPU:8 now
where the time goes in v12:
time: 50.2 us; the launch traced here: 49.9 us
  starting transfers between devices  24.7 us (49%)
  waiting for transfers between devices  13.6 us (27%)
  Pallas kernels  6.9 us (14%)
  local copies, waits for them, and re-layouts  1.98 us (4%)
  between operations  1.96 us (4%)
  other arithmetic  0.77 us (2%)
    ppermute x7, starting transfers between devices, local(): lax.ppermute(beam_total, 'beam', [(i, (i + step) % beam_count) for i in r...  17.2 us
    all_to_all x1, waiting for transfers between devices, local(): lax.all_to_all(series, 'freq', split_axis=2, concat_axis=1, tiled=True)  10.1 us
    all_to_all x1, starting transfers between devices, local(): lax.all_to_all(series, 'freq', split_axis=2, concat_axis=1, tiled=True)  7.53 us
    pallas_call x1, Pallas kernels, merge_tree(): pl.pallas_call(body, grid=(beams_dev,), in_specs=[pl.BlockSpec(memory_spa...  3.87 us
    ppermute x7, waiting for transfers between devices, local(): lax.ppermute(beam_total, 'beam', [(i, (i + step) % beam_count) for i in r...  3.52 us
    pallas_call x1, Pallas kernels, local_tree(): pl.pallas_call(body, grid=(beams_dev,), in_specs=[pl.BlockSpec(memory_spa...  3.03 us
    unnamed x6, local copies, waits for them, and re-layouts  1.98 us
  transfers between devices with their start and end apart: 8, of which 4 were waited for; matrix products, arithmetic and copies ran while one was open for 1% of the time, Pallas kernels for 0%

profile of v12, /device:TPU:8, one launch (start us, length us, event | category | flops | bytes accessed | tf_op | source)
XLA Modules:
  0.0 49.9 jit_solution(18255669390268941434)
XLA Ops:
  1.3 3.0 %shard_map.113 = f32[1,64,1,2304]{3,2,1,0:T(1,128)} custom-call(s32[1]{0:T(128)S(6)} %copy.17.count_ref, bf16[1,64,2048]{2,1,0:T(8,128)(2,1)} %tail_ref.1, bf16[1,64,256]{2,1,0:T(8,128)(2,1)} %block_ref.1, f32[64,64]{1,0:T(8,128)} %constant.19.clone.entry_ref, f32[64,64]{1,0:T(8,128)} %constant.20.clone.mid_ref.leave_ref, ...), custom_call_target="tpu_custom_call" | custom-call | tf_op jit(solution)/shard_map/pallas_call | solution.py:179
  4.3 7.5 %all-to-all-start = ((f32[1,1,64,2304]{3,0,1,2:T(1,128)}), f32[1,1,64,2304]{3,0,1,2:T(1,128)S(1)}, u32[]{:S(2)}, u32[]{:S(2)}) async-start(f32[1,1,64,2304]{3,0,1,2:T(1,128)} %bitcast.13), calls=%async_computation | async-start | bytes 1179648 | tf_op jit(solution)/shard_map/all_to_all | solution.py:256
  12.5 10.1 %all-to-all-done = f32[1,1,64,2304]{3,0,1,2:T(1,128)S(1)} async-done(((f32[1,1,64,2304]{3,0,1,2:T(1,128)}), f32[1,1,64,2304]{3,0,1,2:T(1,128)S(1)}, u32[]{:S(2)}, u32[]{:S(2)}) %all-to-all-start) | async-done | bytes 589856 | tf_op jit(solution)/shard_map/all_to_all | solution.py:256
  22.6 0.0 copy-start
  22.6 0.8 %copy-done = f32[1,1,64,2304]{3,0,1,2:T(1,128)} copy-done((f32[1,1,64,2304]{3,0,1,2:T(1,128)}, f32[1,1,64,2304]{3,0,1,2:T(1,128)S(1)}, u32[]{:S(2)}) %copy-start) | copy-done | bytes 589848
  23.4 3.9 %shard_map.114 = f32[1,8,64]{2,1,0:T(8,128)} custom-call(s32[1]{0:T(128)} %bitcast.1.off_ref, f32[1,64,1,2304]{3,2,1,0:T(1,128)} %bitcast.12, f32[64,64]{1,0:T(8,128)} %constant.19.clone.entry_ref, f32[64,64]{1,0:T(8,128)} %constant.20.clone.mid_ref.leave_ref, f32[64,64]{1,0:T(8,128)} %constant.20.clone.mid_ref.leave_ref), custom_call_target="tpu_custom_call" | custom-call | tf_op jit(solution)/shard_map/pallas_call | solution.py:234
  27.3 0.0 copy-start.1
  27.3 0.7 %fusion = f32[7,64]{1,0:T(8,128)S(1)} fusion(f32[1,8,64]{2,1,0:T(8,128)} %shard_map.114, pred[64]{0:T(512)(128)(4,1)S(1)} %add_compare_fusion), kind=kLoop, calls=%fused_computation.3 | loop fusion | flops 448 | bytes 3648 | tf_op jit(solution)/shard_map/reduce_sum | solution.py:264
  28.0 6.3 %collective-permute-start.5 = (f32[7,64]{1,0:T(8,128)S(1)}, f32[7,64]{1,0:T(8,128)S(1)}, u32[]{:S(2)}, u32[]{:S(2)}) collective-permute-start(f32[7,64]{1,0:T(8,128)S(1)} %fusion), channel_id=1, source_target_pairs={{0,6},{1,7},{2,0},{3,1},{4,2},{5,3},{6,4},{7,5},{8,14},{9,15},{10,... | collective-permute-start | bytes 5384 | tf_op jit(solution)/shard_map/ppermute | solution.py:267
  34.3 1.0 %collective-permute-start.4 = (f32[7,64]{1,0:T(8,128)S(1)}, f32[7,64]{1,0:T(8,128)S(1)}, u32[]{:S(2)}, u32[]{:S(2)}) collective-permute-start(f32[7,64]{1,0:T(8,128)S(1)} %fusion), channel_id=1, source_target_pairs={{0,5},{1,6},{2,7},{3,0},{4,1},{5,2},{6,3},{7,4},{8,13},{9,14},{10,... | collective-permute-start | bytes 5384 | tf_op jit(solution)/shard_map/ppermute | solution.py:267
  35.3 4.5 %collective-permute-start.3 = (f32[7,64]{1,0:T(8,128)S(1)}, f32[7,64]{1,0:T(8,128)S(1)}, u32[]{:S(2)}, u32[]{:S(2)}) collective-permute-start(f32[7,64]{1,0:T(8,128)S(1)} %fusion), channel_id=1, source_target_pairs={{0,4},{1,5},{2,6},{3,7},{4,0},{5,1},{6,2},{7,3},{8,12},{9,13},{10,... | collective-permute-start | bytes 5384 | tf_op jit(solution)/shard_map/ppermute | solution.py:267
  39.8 0.0 collective-permute-start.2
  39.8 3.4 %collective-permute-start.1 = (f32[7,64]{1,0:T(8,128)S(1)}, f32[7,64]{1,0:T(8,128)S(1)}, u32[]{:S(2)}, u32[]{:S(2)}) collective-permute-start(f32[7,64]{1,0:T(8,128)S(1)} %fusion), channel_id=1, source_target_pairs={{0,2},{1,3},{2,4},{3,5},{4,6},{5,7},{6,0},{7,1},{8,10},{9,11},{10,... | collective-permute-start | bytes 5384 | tf_op jit(solution)/shard_map/ppermute | solution.py:267
  43.2 0.0 collective-permute-done.5
  43.2 1.3 %collective-permute-start.6 = (f32[7,64]{1,0:T(8,128)S(1)}, f32[7,64]{1,0:T(8,128)S(1)}, u32[]{:S(2)}, u32[]{:S(2)}) collective-permute-start(f32[7,64]{1,0:T(8,128)S(1)} %fusion), channel_id=1, source_target_pairs={{0,7},{1,0},{2,1},{3,2},{4,3},{5,4},{6,5},{7,6},{8,15},{9,8},{10,9... | collective-permute-start | bytes 5384 | tf_op jit(solution)/shard_map/ppermute | solution.py:267
  44.5 0.0 collective-permute-done.4
  44.5 0.7 %collective-permute-start = (f32[7,64]{1,0:T(8,128)S(1)}, f32[7,64]{1,0:T(8,128)S(1)}, u32[]{:S(2)}, u32[]{:S(2)}) collective-permute-start(f32[7,64]{1,0:T(8,128)S(1)} %fusion), channel_id=1, source_target_pairs={{0,1},{1,2},{2,3},{3,4},{4,5},{5,6},{6,7},{7,0},{8,9},{9,10},{10,1... | collective-permute-start | bytes 5384 | tf_op jit(solution)/shard_map/ppermute | solution.py:267
  45.2 0.0 copy-done.1
  45.2 0.6 %copy.15 = f32[1,7,64]{2,0,1:T(1,128)} copy(f32[1,7,64]{2,1,0:T(8,128)S(1)} %slice_select_fusion) | data formatting | bytes 3584
  45.8 0.0 collective-permute-done.3
  45.8 0.6 %collective-permute-done.2 = f32[7,64]{1,0:T(8,128)S(1)} collective-permute-done((f32[7,64]{1,0:T(8,128)S(1)}, f32[7,64]{1,0:T(8,128)S(1)}, u32[]{:S(2)}, u32[]{:S(2)}) %collective-permute-start.2) | collective-permute-done | bytes 1824 | tf_op jit(solution)/shard_map/ppermute | solution.py:267
  46.4 0.0 collective-permute-done.1
  46.4 0.4 collective-permute-done.6
  46.8 2.5 %collective-permute-done = f32[7,64]{1,0:T(8,128)S(1)} collective-permute-done((f32[7,64]{1,0:T(8,128)S(1)}, f32[7,64]{1,0:T(8,128)S(1)}, u32[]{:S(2)}, u32[]{:S(2)}) %collective-permute-start) | collective-permute-done | bytes 1824 | tf_op jit(solution)/shard_map/ppermute | solution.py:267
  49.3 0.6 %copy.16 = f32[1,7,64]{2,0,1:T(1,128)} copy(f32[1,7,64]{2,1,0:T(8,128)S(1)} %bitcast_subtract_fusion) | data formatting | bytes 3584
  (3 shorter events, 0.0 us)
Async XLA Ops:
  4.3 18.3 %all-to-all-start = ((f32[1,1,64,2304]{3,0,1,2:T(1,128)}), f32[1,1,64,2304]{3,0,1,2:T(1,128)S(1)}, u32[]{:S(2)}, u32[]{:S(2)}) async-start(f32[1,1,64,2304]{3,0,1,2:T(1,128)} %bitcast.13), calls=%async_computation | async-start | bytes 1179648 | tf_op jit(solution)/shard_map/all_to_all | solution.py:256
  22.6 0.8 %copy-start = (f32[1,1,64,2304]{3,0,1,2:T(1,128)}, f32[1,1,64,2304]{3,0,1,2:T(1,128)S(1)}, u32[]{:S(2)}) copy-start(f32[1,1,64,2304]{3,0,1,2:T(1,128)S(1)} %all-to-all-done) | copy-start | bytes 1769476
  27.3 17.9 %copy-start.1 = (f32[1,8,64]{2,1,0:T(8,128)S(1)}, f32[1,8,64]{2,1,0:T(8,128)}, u32[]{:S(2)}) copy-start(f32[1,8,64]{2,1,0:T(8,128)} %shard_map.114) | copy-start | bytes 6148
  28.0 15.2 %collective-permute-start.5 = (f32[7,64]{1,0:T(8,128)S(1)}, f32[7,64]{1,0:T(8,128)S(1)}, u32[]{:S(2)}, u32[]{:S(2)}) collective-permute-start(f32[7,64]{1,0:T(8,128)S(1)} %fusion), channel_id=1, source_target_pairs={{0,6},{1,7},{2,0},{3,1},{4,2},{5,3},{6,4},{7,5},{8,14},{9,15},{10,... | collective-permute-start | bytes 5384 | tf_op jit(solution)/shard_map/ppermute | solution.py:267
  34.3 10.2 %collective-permute-start.4 = (f32[7,64]{1,0:T(8,128)S(1)}, f32[7,64]{1,0:T(8,128)S(1)}, u32[]{:S(2)}, u32[]{:S(2)}) collective-permute-start(f32[7,64]{1,0:T(8,128)S(1)} %fusion), channel_id=1, source_target_pairs={{0,5},{1,6},{2,7},{3,0},{4,1},{5,2},{6,3},{7,4},{8,13},{9,14},{10,... | collective-permute-start | bytes 5384 | tf_op jit(solution)/shard_map/ppermute | solution.py:267
  35.3 10.5 %collective-permute-start.3 = (f32[7,64]{1,0:T(8,128)S(1)}, f32[7,64]{1,0:T(8,128)S(1)}, u32[]{:S(2)}, u32[]{:S(2)}) collective-permute-start(f32[7,64]{1,0:T(8,128)S(1)} %fusion), channel_id=1, source_target_pairs={{0,4},{1,5},{2,6},{3,7},{4,0},{5,1},{6,2},{7,3},{8,12},{9,13},{10,... | collective-permute-start | bytes 5384 | tf_op jit(solution)/shard_map/ppermute | solution.py:267
  39.8 6.6 %collective-permute-start.2 = (f32[7,64]{1,0:T(8,128)S(1)}, f32[7,64]{1,0:T(8,128)S(1)}, u32[]{:S(2)}, u32[]{:S(2)}) collective-permute-start(f32[7,64]{1,0:T(8,128)S(1)} %fusion), channel_id=1, source_target_pairs={{0,3},{1,4},{2,5},{3,6},{4,7},{5,0},{6,1},{7,2},{8,11},{9,12},{10,... | collective-permute-start | bytes 5384 | tf_op jit(solution)/shard_map/ppermute | solution.py:267
  39.8 6.6 %collective-permute-start.1 = (f32[7,64]{1,0:T(8,128)S(1)}, f32[7,64]{1,0:T(8,128)S(1)}, u32[]{:S(2)}, u32[]{:S(2)}) collective-permute-start(f32[7,64]{1,0:T(8,128)S(1)} %fusion), channel_id=1, source_target_pairs={{0,2},{1,3},{2,4},{3,5},{4,6},{5,7},{6,0},{7,1},{8,10},{9,11},{10,... | collective-permute-start | bytes 5384 | tf_op jit(solution)/shard_map/ppermute | solution.py:267
  43.2 3.6 %collective-permute-start.6 = (f32[7,64]{1,0:T(8,128)S(1)}, f32[7,64]{1,0:T(8,128)S(1)}, u32[]{:S(2)}, u32[]{:S(2)}) collective-permute-start(f32[7,64]{1,0:T(8,128)S(1)} %fusion), channel_id=1, source_target_pairs={{0,7},{1,0},{2,1},{3,2},{4,3},{5,4},{6,5},{7,6},{8,15},{9,8},{10,9... | collective-permute-start | bytes 5384 | tf_op jit(solution)/shard_map/ppermute | solution.py:267
  44.5 4.8 %collective-permute-start = (f32[7,64]{1,0:T(8,128)S(1)}, f32[7,64]{1,0:T(8,128)S(1)}, u32[]{:S(2)}, u32[]{:S(2)}) collective-permute-start(f32[7,64]{1,0:T(8,128)S(1)} %fusion), channel_id=1, source_target_pairs={{0,1},{1,2},{2,3},{3,4},{4,5},{5,6},{6,7},{7,0},{8,9},{9,10},{10,1... | collective-permute-start | bytes 5384 | tf_op jit(solution)/shard_map/ppermute | solution.py:267

commit v13 on v11

--- a/solution.py
+++ b/solution.py
@@ -67,7 +67,24 @@
     return jnp.stack(results, axis=-2)
 
 
-def shift_in(row_block, amount, lanes, stride):
+def delay_traced(row_block, amount, pad_ref):
+    rows, length = row_block.shape
+    columns = length // 128
+    whole = amount // 128
+    part = amount - whole * 128
+    lane = lax.broadcasted_iota(jnp.int32, (rows, 128), 1)
+    before = jnp.zeros((rows, 128), jnp.float32)
+    for j in range(columns):
+        turned = pltpu.roll(row_block[:, 128 * j : 128 * (j + 1)], part, 1)
+        pad_ref[:rows, length + 128 * j : length + 128 * (j + 1)] = jnp.where(lane >= part, turned, before)
+        before = turned
+    start = pl.multiple_of(length - 128 * jnp.minimum(whole, columns), 128)
+    return pad_ref[:rows, pl.ds(start, length)]
+
+
+def shift_in(row_block, amount, lanes, stride, pad_ref=None):
+    if pad_ref is not None and not stride and not isinstance(amount, int):
+        return delay_traced(row_block, amount, pad_ref)
     if stride:
         moved = pltpu.roll(row_block, amount, 1, stride=stride, stride_axis=0)
         limit = lax.broadcasted_iota(jnp.int32, row_block.shape, 0) * stride + amount
@@ -87,7 +104,7 @@
     return pltpu.einshape("abt->bat", blocks).reshape(tile * tile, length)
 
 
-def tree_in_place(buf, mid_ref, subbands, trials, first_trial, tile):
+def tree_in_place(buf, mid_ref, subbands, trials, first_trial, tile, pad_ref=None):
     length = buf.shape[1]
     while subbands > 1 and subbands // 2 >= tile:
         half = subbands // 2
@@ -96,9 +113,9 @@
             top = k * subbands
             upper = buf[top : top + half, :]
             lower = buf[top + half : top + subbands, :]
-            buf[top : top + half, :] = upper + shift_in(lower, first_trial + k, lanes, 0)
+            buf[top : top + half, :] = upper + shift_in(lower, first_trial + k, lanes, 0, pad_ref)
             buf[top + half : top + subbands, :] = upper + shift_in(
-                lower, first_trial + k + 1, lanes, 0
+                lower, first_trial + k + 1, lanes, 0, pad_ref
             )
         subbands = half
         trials = 2 * trials
@@ -113,7 +130,7 @@
         order = bit_reversed(subbands)
         for pos in range(subbands):
             rows = slice(pos * tile, (pos + 1) * tile)
-            buf[rows, :] = shift_in(buf[rows, :], first_trial * int(order[pos]), lanes, 0)
+            buf[rows, :] = shift_in(buf[rows, :], first_trial * int(order[pos]), lanes, 0, pad_ref)
         first_trial = 0
     while subbands > 1:
         half = subbands // 2
@@ -221,12 +238,13 @@
 
     order = bit_reversed(subbands)
 
-    def body(off_ref, x_ref, entry_ref, mid_ref, leave_ref, o_ref, buf):
+    def body(off_ref, x_ref, entry_ref, mid_ref, leave_ref, o_ref, buf, pad_ref):
+        pad_ref[:, :length] = jnp.zeros((pad_ref.shape[0], length), jnp.float32)
         for pos in range(subbands):
             for trial in range(trials):
                 source = int(order[pos]) * trials + trial
                 buf[trial * subbands + pos : trial * subbands + pos + 1, :] = x_ref[source]
-        tree_in_place(buf, mid_ref, subbands, trials, off_ref[0], TILE)
+        tree_in_place(buf, mid_ref, subbands, trials, off_ref[0], TILE, pad_ref)
         o_ref[...] = peaks_of(buf[...], tail_len, length - tail_len, leave_ref[...])
 
     spec = pl.BlockSpec((None, rows, 1, length), lambda b: (b, 0, 0, 0))
@@ -237,7 +255,10 @@
         in_specs=[pl.BlockSpec(memory_space=pltpu.SMEM), spec, table_spec, table_spec, table_spec],
         out_specs=pl.BlockSpec((None, 8, rows), lambda b: (b, 0, 0)),
         out_shape=jax.ShapeDtypeStruct((beams_dev, 8, rows), jnp.float32),
-        scratch_shapes=[pltpu.VMEM((rows, length), jnp.float32)],
+        scratch_shapes=[
+            pltpu.VMEM((rows, length), jnp.float32),
+            pltpu.VMEM((2 * TILE, 2 * length), jnp.float32),
+        ],
     )(
         jnp.reshape(first_trial, (1,)).astype(jnp.int32),
         parts.reshape(beams_dev, rows, 1, length),

time: 45.4 us -> 45.1 us (level)
  no operation moved by 1% of the time
where the time goes in v13:
time: 45.1 us; the launch traced here: 44.8 us
  waiting for transfers between devices  17.2 us (38%)
  starting transfers between devices  16.3 us (36%)
  Pallas kernels  6.57 us (15%)
  local copies, waits for them, and re-layouts  1.99 us (4%)
  between operations  1.95 us (4%)
  other arithmetic  0.78 us (2%)
    all_to_all x1, waiting for transfers between devices, local(): lax.all_to_all(series, 'freq', split_axis=2, concat_axis=1, tiled=True)  11.1 us
    ppermute x3, starting transfers between devices, local(): beam_total = beam_total + lax.ppermute(beam_total, 'beam', pairs)  8.96 us
    all_to_all x1, starting transfers between devices, local(): lax.all_to_all(series, 'freq', split_axis=2, concat_axis=1, tiled=True)  7.32 us
    ppermute x3, waiting for transfers between devices, local(): beam_total = beam_total + lax.ppermute(beam_total, 'beam', pairs)  6.08 us
    pallas_call x1, Pallas kernels, merge_tree(): pl.pallas_call(body, grid=(beams_dev,), in_specs=[pl.BlockSpec(memory_spa...  3.53 us
    pallas_call x1, Pallas kernels, local_tree(): pl.pallas_call(body, grid=(beams_dev,), in_specs=[pl.BlockSpec(memory_spa...  3.04 us
    unnamed x6, local copies, waits for them, and re-layouts  1.99 us
  transfers between devices with their start and end apart: 4, of which 4 were waited for; matrix products, arithmetic and copies ran while one was open for 1% of the time, Pallas kernels for 0%

profile of v13, /device:TPU:32, one launch (start us, length us, event | category | flops | bytes accessed | tf_op | source)
XLA Modules:
  0.0 44.8 jit_solution(15086810507957506468)
XLA Ops:
  1.3 3.0 %shard_map.113 = f32[1,64,1,2304]{3,2,1,0:T(1,128)} custom-call(s32[1]{0:T(128)S(6)} %copy.17.count_ref, bf16[1,64,2048]{2,1,0:T(8,128)(2,1)} %tail_ref.1, bf16[1,64,256]{2,1,0:T(8,128)(2,1)} %block_ref.1, f32[64,64]{1,0:T(8,128)} %constant.19.clone.entry_ref, f32[64,64]{1,0:T(8,128)} %constant.20.clone.mid_ref.leave_ref, ...), custom_call_target="tpu_custom_call" | custom-call | tf_op jit(solution)/shard_map/pallas_call | solution.py:196
  4.3 7.3 %all-to-all-start = ((f32[1,1,64,2304]{3,0,1,2:T(1,128)}), f32[1,1,64,2304]{3,0,1,2:T(1,128)S(1)}, u32[]{:S(2)}, u32[]{:S(2)}) async-start(f32[1,1,64,2304]{3,0,1,2:T(1,128)} %bitcast.13), calls=%async_computation | async-start | bytes 1179648 | tf_op jit(solution)/shard_map/all_to_all | solution.py:277
  12.3 11.1 %all-to-all-done = f32[1,1,64,2304]{3,0,1,2:T(1,128)S(1)} async-done(((f32[1,1,64,2304]{3,0,1,2:T(1,128)}), f32[1,1,64,2304]{3,0,1,2:T(1,128)S(1)}, u32[]{:S(2)}, u32[]{:S(2)}) %all-to-all-start) | async-done | bytes 589856 | tf_op jit(solution)/shard_map/all_to_all | solution.py:277
  23.4 0.0 copy-start
  23.5 0.8 %copy-done = f32[1,1,64,2304]{3,0,1,2:T(1,128)} copy-done((f32[1,1,64,2304]{3,0,1,2:T(1,128)}, f32[1,1,64,2304]{3,0,1,2:T(1,128)S(1)}, u32[]{:S(2)}) %copy-start) | copy-done | bytes 589848
  24.3 3.5 %shard_map.114 = f32[1,8,64]{2,1,0:T(8,128)} custom-call(s32[1]{0:T(128)} %bitcast.1.off_ref, f32[1,64,1,2304]{3,2,1,0:T(1,128)} %bitcast.12, f32[64,64]{1,0:T(8,128)} %constant.19.clone.entry_ref, f32[64,64]{1,0:T(8,128)} %constant.20.clone.mid_ref.leave_ref, f32[64,64]{1,0:T(8,128)} %constant.20.clone.mid_ref.leave_ref), custom_call_target="tpu_custom_call" | custom-call | tf_op jit(solution)/shard_map/pallas_call | solution.py:252
  27.8 0.0 copy-start.1
  27.8 0.8 %fusion = f32[7,64]{1,0:T(8,128)S(1)} fusion(f32[1,8,64]{2,1,0:T(8,128)} %shard_map.114, pred[64]{0:T(512)(128)(4,1)S(1)} %add_compare_fusion), kind=kLoop, calls=%fused_computation.4 | loop fusion | flops 448 | bytes 3648 | tf_op jit(solution)/shard_map/reduce_sum | solution.py:285
  28.6 0.1 collective-permute-start
  28.7 3.5 %collective-permute-done = f32[7,64]{1,0:T(8,128)S(1)} collective-permute-done((f32[7,64]{1,0:T(8,128)S(1)}, f32[7,64]{1,0:T(8,128)S(1)}, u32[]{:S(2)}, u32[]{:S(2)}) %collective-permute-start) | collective-permute-done | bytes 1824 | tf_op jit(solution)/shard_map/ppermute | solution.py:293
  32.2 0.0 copy-done.1
  32.2 3.4 %collective-permute-start.1 = (f32[7,64]{1,0:T(8,128)S(1)}, f32[7,64]{1,0:T(8,128)S(1)}, u32[]{:S(2)}, u32[]{:S(2)}) collective-permute-start(f32[7,64]{1,0:T(8,128)S(1)} %bitcast_add_fusion), channel_id=1, source_target_pairs={{0,2},{1,3},{2,0},{3,1},{4,6},{5,7},{6,4},{7,5},{8,10},{9,11},{10,... | collective-permute-start | bytes 5384 | tf_op jit(solution)/shard_map/ppermute | solution.py:293
  35.5 1.6 %collective-permute-done.1 = f32[7,64]{1,0:T(8,128)S(1)} collective-permute-done((f32[7,64]{1,0:T(8,128)S(1)}, f32[7,64]{1,0:T(8,128)S(1)}, u32[]{:S(2)}, u32[]{:S(2)}) %collective-permute-start.1) | collective-permute-done | bytes 1824 | tf_op jit(solution)/shard_map/ppermute | solution.py:293
  37.1 5.5 %collective-permute-start.2 = (f32[7,64]{1,0:T(8,128)S(1)}, f32[7,64]{1,0:T(8,128)S(1)}, u32[]{:S(2)}, u32[]{:S(2)}) collective-permute-start(f32[7,64]{1,0:T(8,128)S(1)} %add.22), channel_id=1, source_target_pairs={{0,7},{1,6},{2,5},{3,4},{4,3},{5,2},{6,1},{7,0},{8,15},{9,14},{10,... | collective-permute-start | bytes 5384 | tf_op jit(solution)/shard_map/ppermute | solution.py:293
  42.6 0.6 %copy.15 = f32[1,7,64]{2,0,1:T(1,128)} copy(f32[1,7,64]{2,1,0:T(8,128)S(1)} %slice_select_fusion) | data formatting | bytes 3584
  43.2 1.0 %collective-permute-done.2 = f32[7,64]{1,0:T(8,128)S(1)} collective-permute-done((f32[7,64]{1,0:T(8,128)S(1)}, f32[7,64]{1,0:T(8,128)S(1)}, u32[]{:S(2)}, u32[]{:S(2)}) %collective-permute-start.2) | collective-permute-done | bytes 1824 | tf_op jit(solution)/shard_map/ppermute | solution.py:293
  44.2 0.6 %copy.16 = f32[1,7,64]{2,0,1:T(1,128)} copy(f32[1,7,64]{2,1,0:T(8,128)S(1)} %bitcast_subtract_fusion) | data formatting | bytes 3584
  (5 shorter events, 0.0 us)
Async XLA Ops:
  4.3 19.1 %all-to-all-start = ((f32[1,1,64,2304]{3,0,1,2:T(1,128)}), f32[1,1,64,2304]{3,0,1,2:T(1,128)S(1)}, u32[]{:S(2)}, u32[]{:S(2)}) async-start(f32[1,1,64,2304]{3,0,1,2:T(1,128)} %bitcast.13), calls=%async_computation | async-start | bytes 1179648 | tf_op jit(solution)/shard_map/all_to_all | solution.py:277
  23.4 0.8 %copy-start = (f32[1,1,64,2304]{3,0,1,2:T(1,128)}, f32[1,1,64,2304]{3,0,1,2:T(1,128)S(1)}, u32[]{:S(2)}) copy-start(f32[1,1,64,2304]{3,0,1,2:T(1,128)S(1)} %all-to-all-done) | copy-start | bytes 1769476
  27.8 4.4 %copy-start.1 = (f32[1,8,64]{2,1,0:T(8,128)S(1)}, f32[1,8,64]{2,1,0:T(8,128)}, u32[]{:S(2)}) copy-start(f32[1,8,64]{2,1,0:T(8,128)} %shard_map.114) | copy-start | bytes 6148
  28.6 3.6 %collective-permute-start = (f32[7,64]{1,0:T(8,128)S(1)}, f32[7,64]{1,0:T(8,128)S(1)}, u32[]{:S(2)}, u32[]{:S(2)}) collective-permute-start(f32[7,64]{1,0:T(8,128)S(1)} %fusion), channel_id=1, source_target_pairs={{0,1},{1,0},{2,3},{3,2},{4,5},{5,4},{6,7},{7,6},{8,9},{9,8},{10,11... | collective-permute-start | bytes 5384 | tf_op jit(solution)/shard_map/ppermute | solution.py:293
  32.2 4.9 %collective-permute-start.1 = (f32[7,64]{1,0:T(8,128)S(1)}, f32[7,64]{1,0:T(8,128)S(1)}, u32[]{:S(2)}, u32[]{:S(2)}) collective-permute-start(f32[7,64]{1,0:T(8,128)S(1)} %bitcast_add_fusion), channel_id=1, source_target_pairs={{0,2},{1,3},{2,0},{3,1},{4,6},{5,7},{6,4},{7,5},{8,10},{9,11},{10,... | collective-permute-start | bytes 5384 | tf_op jit(solution)/shard_map/ppermute | solution.py:293
  37.1 7.1 %collective-permute-start.2 = (f32[7,64]{1,0:T(8,128)S(1)}, f32[7,64]{1,0:T(8,128)S(1)}, u32[]{:S(2)}, u32[]{:S(2)}) collective-permute-start(f32[7,64]{1,0:T(8,128)S(1)} %add.22), channel_id=1, source_target_pairs={{0,7},{1,6},{2,5},{3,4},{4,3},{5,2},{6,1},{7,0},{8,15},{9,14},{10,... | collective-permute-start | bytes 5384 | tf_op jit(solution)/shard_map/ppermute | solution.py:293

commit v14 on v13

--- a/solution.py
+++ b/solution.py
@@ -231,41 +231,51 @@
     return permute_rows(leave, table).T[:8]
 
 
-def merge_tree(parts, first_trial, tail_len):
+def merge_tree(parts, first_trial, tail_len, dm_limit):
     beams_dev, subbands, trials, length = parts.shape
     rows = subbands * trials
     entry, mid, leave = tables(subbands, trials, TILE)
 
     order = bit_reversed(subbands)
 
-    def body(off_ref, x_ref, entry_ref, mid_ref, leave_ref, o_ref, buf, pad_ref):
+    def body(off_ref, limit_ref, x_ref, entry_ref, mid_ref, leave_ref, o_ref, buf, pad_ref):
         pad_ref[:, :length] = jnp.zeros((pad_ref.shape[0], length), jnp.float32)
         for pos in range(subbands):
             for trial in range(trials):
                 source = int(order[pos]) * trials + trial
                 buf[trial * subbands + pos : trial * subbands + pos + 1, :] = x_ref[source]
         tree_in_place(buf, mid_ref, subbands, trials, off_ref[0], TILE, pad_ref)
-        o_ref[...] = peaks_of(buf[...], tail_len, length - tail_len, leave_ref[...])
+        table = peaks_of(buf[...], tail_len, length - tail_len, leave_ref[...])[:WIDTHS]
+        ids = lax.broadcasted_iota(jnp.int32, table.shape, 1) + off_ref[0] * subbands
+        o_ref[...] = jnp.where(ids < limit_ref[pl.program_id(0)], table, jnp.float32(0.0))
 
     spec = pl.BlockSpec((None, rows, 1, length), lambda b: (b, 0, 0, 0))
     table_spec = pl.BlockSpec((rows, rows), lambda b: (0, 0))
     return pl.pallas_call(
         body,
         grid=(beams_dev,),
-        in_specs=[pl.BlockSpec(memory_space=pltpu.SMEM), spec, table_spec, table_spec, table_spec],
-        out_specs=pl.BlockSpec((None, 8, rows), lambda b: (b, 0, 0)),
-        out_shape=jax.ShapeDtypeStruct((beams_dev, 8, rows), jnp.float32),
+        in_specs=[
+            pl.BlockSpec(memory_space=pltpu.SMEM),
+            pl.BlockSpec(memory_space=pltpu.SMEM),
+            spec,
+            table_spec,
+            table_spec,
+            table_spec,
+        ],
+        out_specs=pl.BlockSpec((None, WIDTHS, rows), lambda b: (b, 0, 0)),
+        out_shape=jax.ShapeDtypeStruct((beams_dev, WIDTHS, rows), jnp.float32),
         scratch_shapes=[
             pltpu.VMEM((rows, length), jnp.float32),
             pltpu.VMEM((2 * TILE, 2 * length), jnp.float32),
         ],
     )(
         jnp.reshape(first_trial, (1,)).astype(jnp.int32),
+        dm_limit.astype(jnp.int32),
         parts.reshape(beams_dev, rows, 1, length),
         entry,
         mid,
         leave,
-    )[:, :WIDTHS]
+    )
 
 
 def local(block_samples, tail_samples, tail_blocks, dm_limit):
@@ -276,12 +286,7 @@
     position = lax.axis_index("freq")
     series = lax.all_to_all(series, "freq", split_axis=2, concat_axis=1, tiled=True)
     per_dev = series.shape[2]
-    scores = merge_tree(series, position * per_dev, tail_len)
-    out_rows = scores.shape[-1]
-    trial_ids = position * out_rows + jnp.arange(out_rows, dtype=jnp.int32)
-    peak_snr = jnp.where(
-        trial_ids[None, None, :] < dm_limit[:, None, None], scores, jnp.float32(0.0)
-    )
+    peak_snr = merge_tree(series, position * per_dev, tail_len, dm_limit)
     beam_total = jnp.sum(peak_snr, axis=0)
     beam_count = lax.axis_size("beam")
     for level_bit in range(beam_count.bit_length() - 1):

time: 45.1 us -> 45.1 us (level)
    reduce_sum x1 -> x0, other arithmetic: 0.76 us -> none  [local(): beam_total = jnp.sum(peak_snr, axis=0)]
    add x2, other arithmetic: 0.01 us -> 0.69 us  [local(): beam_total = beam_total + lax.ppermute(beam_total, 'beam', pairs)]
where the time goes in v14:
time: 45.1 us; the launch traced here: 44.8 us
  waiting for transfers between devices  17.4 us (39%)
  starting transfers between devices  16.2 us (36%)
  Pallas kernels  6.57 us (15%)
  local copies, waits for them, and re-layouts  1.99 us (4%)
  between operations  1.94 us (4%)
  other arithmetic  0.7 us (2%)
    all_to_all x1, waiting for transfers between devices, local(): lax.all_to_all(series, 'freq', split_axis=2, concat_axis=1, tiled=True)  11.2 us
    ppermute x3, starting transfers between devices, local(): beam_total = beam_total + lax.ppermute(beam_total, 'beam', pairs)  8.88 us
    all_to_all x1, starting transfers between devices, local(): lax.all_to_all(series, 'freq', split_axis=2, concat_axis=1, tiled=True)  7.32 us
    ppermute x3, waiting for transfers between devices, local(): beam_total = beam_total + lax.ppermute(beam_total, 'beam', pairs)  6.29 us
    pallas_call x1, Pallas kernels, merge_tree(): pl.pallas_call(body, grid=(beams_dev,), in_specs=[pl.BlockSpec(memory_spa...  3.53 us
    pallas_call x1, Pallas kernels, local_tree(): pl.pallas_call(body, grid=(beams_dev,), in_specs=[pl.BlockSpec(memory_spa...  3.04 us
    unnamed x6, local copies, waits for them, and re-layouts  1.99 us
  transfers between devices with their start and end apart: 4, of which 4 were waited for; matrix products, arithmetic and copies ran while one was open for 1% of the time, Pallas kernels for 0%

profile of v14, /device:TPU:32, one launch (start us, length us, event | category | flops | bytes accessed | tf_op | source)
XLA Modules:
  0.0 44.8 jit_solution(2524942256976281254)
XLA Ops:
  1.3 3.0 %shard_map.113 = f32[1,64,1,2304]{3,2,1,0:T(1,128)} custom-call(s32[1]{0:T(128)S(6)} %copy.17.count_ref, bf16[1,64,2048]{2,1,0:T(8,128)(2,1)} %tail_ref.1, bf16[1,64,256]{2,1,0:T(8,128)(2,1)} %block_ref.1, f32[64,64]{1,0:T(8,128)} %constant.16.clone.entry_ref, f32[64,64]{1,0:T(8,128)} %constant.17.clone.mid_ref.leave_ref, ...), custom_call_target="tpu_custom_call" | custom-call | tf_op jit(solution)/shard_map/pallas_call | solution.py:196
  4.3 7.3 %all-to-all-start = ((f32[1,1,64,2304]{3,0,1,2:T(1,128)}), f32[1,1,64,2304]{3,0,1,2:T(1,128)S(1)}, u32[]{:S(2)}, u32[]{:S(2)}) async-start(f32[1,1,64,2304]{3,0,1,2:T(1,128)} %bitcast.10), calls=%async_computation | async-start | bytes 1179648 | tf_op jit(solution)/shard_map/all_to_all | solution.py:287
  12.3 11.2 %all-to-all-done = f32[1,1,64,2304]{3,0,1,2:T(1,128)S(1)} async-done(((f32[1,1,64,2304]{3,0,1,2:T(1,128)}), f32[1,1,64,2304]{3,0,1,2:T(1,128)S(1)}, u32[]{:S(2)}, u32[]{:S(2)}) %all-to-all-start) | async-done | bytes 589856 | tf_op jit(solution)/shard_map/all_to_all | solution.py:287
  23.4 0.0 copy-start
  23.5 0.8 %copy-done = f32[1,1,64,2304]{3,0,1,2:T(1,128)} copy-done((f32[1,1,64,2304]{3,0,1,2:T(1,128)}, f32[1,1,64,2304]{3,0,1,2:T(1,128)S(1)}, u32[]{:S(2)}) %copy-start) | copy-done | bytes 589848
  24.3 3.5 %shard_map.114 = f32[1,7,64]{2,1,0:T(8,128)} custom-call(s32[1]{0:T(128)} %bitcast.off_ref, s32[1]{0:T(128)S(6)} %copy.18.limit_ref, f32[1,64,1,2304]{3,2,1,0:T(1,128)} %bitcast.9, f32[64,64]{1,0:T(8,128)} %constant.16.clone.entry_ref, f32[64,64]{1,0:T(8,128)} %constant.17.clone.mid_ref.leave_ref, f32[64,64]{1,0:T(8,128)} %constant.17.clone.mid_ref.leave_ref), custom_call_target="tpu_custom_call" | custom-call | tf_op jit(solution)/shard_map/pallas_call | solution.py:254
  27.8 0.1 collective-permute-start
  27.9 3.7 %collective-permute-done = f32[7,64]{1,0:T(8,128)S(1)} collective-permute-done((f32[7,64]{1,0:T(8,128)}, f32[7,64]{1,0:T(8,128)S(1)}, u32[]{:S(2)}, u32[]{:S(2)}) %collective-permute-start) | collective-permute-done | bytes 1824 | tf_op jit(solution)/shard_map/ppermute | solution.py:298
  31.6 0.7 %bitcast_add_fusion = f32[7,64]{1,0:T(8,128)S(1)} fusion(f32[7,64]{1,0:T(8,128)S(1)} %collective-permute-done, f32[1,7,64]{2,1,0:T(8,128)} %shard_map.114), kind=kLoop, calls=%fused_computation.1 | loop fusion | flops 448 | bytes 5376 | tf_op jit(solution)/shard_map/add | solution.py:298
  32.3 0.0 copy-start.1
  32.3 3.3 %collective-permute-start.1 = (f32[7,64]{1,0:T(8,128)S(1)}, f32[7,64]{1,0:T(8,128)S(1)}, u32[]{:S(2)}, u32[]{:S(2)}) collective-permute-start(f32[7,64]{1,0:T(8,128)S(1)} %bitcast_add_fusion), channel_id=1, source_target_pairs={{0,2},{1,3},{2,0},{3,1},{4,6},{5,7},{6,4},{7,5},{8,10},{9,11},{10,... | collective-permute-start | bytes 5384 | tf_op jit(solution)/shard_map/ppermute | solution.py:298
  35.6 1.6 %collective-permute-done.1 = f32[7,64]{1,0:T(8,128)S(1)} collective-permute-done((f32[7,64]{1,0:T(8,128)S(1)}, f32[7,64]{1,0:T(8,128)S(1)}, u32[]{:S(2)}, u32[]{:S(2)}) %collective-permute-start.1) | collective-permute-done | bytes 1824 | tf_op jit(solution)/shard_map/ppermute | solution.py:298
  37.2 5.5 %collective-permute-start.2 = (f32[7,64]{1,0:T(8,128)S(1)}, f32[7,64]{1,0:T(8,128)S(1)}, u32[]{:S(2)}, u32[]{:S(2)}) collective-permute-start(f32[7,64]{1,0:T(8,128)S(1)} %add.10), channel_id=1, source_target_pairs={{0,7},{1,6},{2,5},{3,4},{4,3},{5,2},{6,1},{7,0},{8,15},{9,14},{10,... | collective-permute-start | bytes 5384 | tf_op jit(solution)/shard_map/ppermute | solution.py:298
  42.7 0.0 copy-done.1
  42.7 0.6 %copy.15 = f32[1,7,64]{2,0,1:T(1,128)} copy(f32[1,7,64]{2,1,0:T(8,128)S(1)} %copy-done.1) | data formatting | bytes 3584
  43.3 1.0 %collective-permute-done.2 = f32[7,64]{1,0:T(8,128)S(1)} collective-permute-done((f32[7,64]{1,0:T(8,128)S(1)}, f32[7,64]{1,0:T(8,128)S(1)}, u32[]{:S(2)}, u32[]{:S(2)}) %collective-permute-start.2) | collective-permute-done | bytes 1824 | tf_op jit(solution)/shard_map/ppermute | solution.py:298
  44.3 0.6 %copy.16 = f32[1,7,64]{2,0,1:T(1,128)} copy(f32[1,7,64]{2,1,0:T(8,128)S(1)} %bitcast_subtract_fusion) | data formatting | bytes 3584
  (2 shorter events, 0.0 us)
Async XLA Ops:
  4.3 19.1 %all-to-all-start = ((f32[1,1,64,2304]{3,0,1,2:T(1,128)}), f32[1,1,64,2304]{3,0,1,2:T(1,128)S(1)}, u32[]{:S(2)}, u32[]{:S(2)}) async-start(f32[1,1,64,2304]{3,0,1,2:T(1,128)} %bitcast.10), calls=%async_computation | async-start | bytes 1179648 | tf_op jit(solution)/shard_map/all_to_all | solution.py:287
  23.4 0.8 %copy-start = (f32[1,1,64,2304]{3,0,1,2:T(1,128)}, f32[1,1,64,2304]{3,0,1,2:T(1,128)S(1)}, u32[]{:S(2)}) copy-start(f32[1,1,64,2304]{3,0,1,2:T(1,128)S(1)} %all-to-all-done) | copy-start | bytes 1769476
  27.8 3.8 %collective-permute-start = (f32[7,64]{1,0:T(8,128)}, f32[7,64]{1,0:T(8,128)S(1)}, u32[]{:S(2)}, u32[]{:S(2)}) collective-permute-start(f32[7,64]{1,0:T(8,128)} %bitcast.11), channel_id=1, source_target_pairs={{0,1},{1,0},{2,3},{3,2},{4,5},{5,4},{6,7},{7,6},{8,9},{9,8},{10,11... | collective-permute-start | bytes 5384 | tf_op jit(solution)/shard_map/ppermute | solution.py:298
  32.3 10.4 %copy-start.1 = (f32[1,7,64]{2,1,0:T(8,128)S(1)}, f32[1,7,64]{2,1,0:T(8,128)}, u32[]{:S(2)}) copy-start(f32[1,7,64]{2,1,0:T(8,128)} %shard_map.114) | copy-start | bytes 5380
  32.3 4.9 %collective-permute-start.1 = (f32[7,64]{1,0:T(8,128)S(1)}, f32[7,64]{1,0:T(8,128)S(1)}, u32[]{:S(2)}, u32[]{:S(2)}) collective-permute-start(f32[7,64]{1,0:T(8,128)S(1)} %bitcast_add_fusion), channel_id=1, source_target_pairs={{0,2},{1,3},{2,0},{3,1},{4,6},{5,7},{6,4},{7,5},{8,10},{9,11},{10,... | collective-permute-start | bytes 5384 | tf_op jit(solution)/shard_map/ppermute | solution.py:298
  37.2 7.1 %collective-permute-start.2 = (f32[7,64]{1,0:T(8,128)S(1)}, f32[7,64]{1,0:T(8,128)S(1)}, u32[]{:S(2)}, u32[]{:S(2)}) collective-permute-start(f32[7,64]{1,0:T(8,128)S(1)} %add.10), channel_id=1, source_target_pairs={{0,7},{1,6},{2,5},{3,4},{4,3},{5,2},{6,1},{7,0},{8,15},{9,14},{10,... | collective-permute-start | bytes 5384 | tf_op jit(solution)/shard_map/ppermute | solution.py:298

commit v15 on v14

--- a/solution.py
+++ b/solution.py
@@ -238,7 +238,7 @@
 
     order = bit_reversed(subbands)
 
-    def body(off_ref, limit_ref, x_ref, entry_ref, mid_ref, leave_ref, o_ref, buf, pad_ref):
+    def body(off_ref, limit_ref, x_ref, entry_ref, mid_ref, leave_ref, o_ref, laid_ref, buf, pad_ref):
         pad_ref[:, :length] = jnp.zeros((pad_ref.shape[0], length), jnp.float32)
         for pos in range(subbands):
             for trial in range(trials):
@@ -247,7 +247,10 @@
         tree_in_place(buf, mid_ref, subbands, trials, off_ref[0], TILE, pad_ref)
         table = peaks_of(buf[...], tail_len, length - tail_len, leave_ref[...])[:WIDTHS]
         ids = lax.broadcasted_iota(jnp.int32, table.shape, 1) + off_ref[0] * subbands
-        o_ref[...] = jnp.where(ids < limit_ref[pl.program_id(0)], table, jnp.float32(0.0))
+        masked = jnp.where(ids < limit_ref[pl.program_id(0)], table, jnp.float32(0.0))
+        o_ref[...] = masked
+        for width_bit in range(WIDTHS):
+            laid_ref[width_bit] = masked[width_bit : width_bit + 1, :]
 
     spec = pl.BlockSpec((None, rows, 1, length), lambda b: (b, 0, 0, 0))
     table_spec = pl.BlockSpec((rows, rows), lambda b: (0, 0))
@@ -262,8 +265,14 @@
             table_spec,
             table_spec,
         ],
-        out_specs=pl.BlockSpec((None, WIDTHS, rows), lambda b: (b, 0, 0)),
-        out_shape=jax.ShapeDtypeStruct((beams_dev, WIDTHS, rows), jnp.float32),
+        out_specs=[
+            pl.BlockSpec((None, WIDTHS, rows), lambda b: (b, 0, 0)),
+            pl.BlockSpec((WIDTHS, None, 1, rows), lambda b: (0, b, 0, 0)),
+        ],
+        out_shape=[
+            jax.ShapeDtypeStruct((beams_dev, WIDTHS, rows), jnp.float32),
+            jax.ShapeDtypeStruct((WIDTHS, beams_dev, 1, rows), jnp.float32),
+        ],
         scratch_shapes=[
             pltpu.VMEM((rows, length), jnp.float32),
             pltpu.VMEM((2 * TILE, 2 * length), jnp.float32),
@@ -286,7 +295,7 @@
     position = lax.axis_index("freq")
     series = lax.all_to_all(series, "freq", split_axis=2, concat_axis=1, tiled=True)
     per_dev = series.shape[2]
-    peak_snr = merge_tree(series, position * per_dev, tail_len, dm_limit)
+    peak_snr, laid = merge_tree(series, position * per_dev, tail_len, dm_limit)
     beam_total = jnp.sum(peak_snr, axis=0)
     beam_count = lax.axis_size("beam")
     for level_bit in range(beam_count.bit_length() - 1):
@@ -297,7 +306,8 @@
             pairs = [(i, i ^ span) for i in range(beam_count)]
         beam_total = beam_total + lax.ppermute(beam_total, "beam", pairs)
     excess_snr = peak_snr - beam_total[None] / (beams_dev * lax.axis_size("beam"))
-    return (peak_snr, excess_snr)
+    laid = laid.reshape(WIDTHS, beams_dev, laid.shape[-1]).transpose(1, 0, 2)
+    return (laid, excess_snr)
 
 
 def solution(mesh):

time: 45.1 us -> 45.1 us (level)
  waiting for transfers between devices: 17.4 us -> 18 us
  local copies, waits for them, and re-layouts: 1.99 us -> 1.4 us
    unnamed x6 -> x5, local copies, waits for them, and re-layouts: 1.99 us -> 1.4 us
    ppermute x3, waiting for transfers between devices: 6.29 us -> 6.88 us  [local(): beam_total = beam_total + lax.ppermute(beam_total, 'beam', pairs)]
  transfers between devices with their start and end apart: 4 -> 4, of which waited for: 4 -> 4; matrix products, arithmetic and copies ran while one was open for 1% -> 0% of each run, Pallas kernels for 0% -> 0%
where the time goes in v15:
time: 45.1 us; the launch traced here: 44.8 us
  waiting for transfers between devices  18 us (40%)
  starting transfers between devices  16.2 us (36%)
  Pallas kernels  6.56 us (15%)
  between operations  1.94 us (4%)
  local copies, waits for them, and re-layouts  1.4 us (3%)
  other arithmetic  0.69 us (2%)
    all_to_all x1, waiting for transfers between devices, local(): lax.all_to_all(series, 'freq', split_axis=2, concat_axis=1, tiled=True)  11.2 us
    ppermute x3, starting transfers between devices, local(): beam_total = beam_total + lax.ppermute(beam_total, 'beam', pairs)  8.88 us
    all_to_all x1, starting transfers between devices, local(): lax.all_to_all(series, 'freq', split_axis=2, concat_axis=1, tiled=True)  7.32 us
    ppermute x3, waiting for transfers between devices, local(): beam_total = beam_total + lax.ppermute(beam_total, 'beam', pairs)  6.88 us
    pallas_call x1, Pallas kernels, merge_tree(): pl.pallas_call(body, grid=(beams_dev,), in_specs=[pl.BlockSpec(memory_spa...  3.54 us
    pallas_call x1, Pallas kernels, local_tree(): pl.pallas_call(body, grid=(beams_dev,), in_specs=[pl.BlockSpec(memory_spa...  3.02 us
    unnamed x5, local copies, waits for them, and re-layouts  1.4 us
  transfers between devices with their start and end apart: 4, of which 4 were waited for; matrix products, arithmetic and copies ran while one was open for 0% of the time, Pallas kernels for 0%

profile of v15, /device:TPU:32, one launch (start us, length us, event | category | flops | bytes accessed | tf_op | source)
XLA Modules:
  0.0 44.8 jit_solution(6136704663157347433)
XLA Ops:
  1.3 3.0 %shard_map.113 = f32[1,64,1,2304]{3,2,1,0:T(1,128)} custom-call(s32[1]{0:T(128)S(6)} %copy.15.count_ref, bf16[1,64,2048]{2,1,0:T(8,128)(2,1)} %tail_ref.1, bf16[1,64,256]{2,1,0:T(8,128)(2,1)} %block_ref.1, f32[64,64]{1,0:T(8,128)} %constant.16.clone.entry_ref, f32[64,64]{1,0:T(8,128)} %constant.17.clone.mid_ref.leave_ref, ...), custom_call_target="tpu_custom_call" | custom-call | tf_op jit(solution)/shard_map/pallas_call | solution.py:196
  4.3 7.3 %all-to-all-start = ((f32[1,1,64,2304]{3,0,1,2:T(1,128)}), f32[1,1,64,2304]{3,0,1,2:T(1,128)S(1)}, u32[]{:S(2)}, u32[]{:S(2)}) async-start(f32[1,1,64,2304]{3,0,1,2:T(1,128)} %bitcast.11), calls=%async_computation | async-start | bytes 1179648 | tf_op jit(solution)/shard_map/all_to_all | solution.py:296
  12.3 11.2 %all-to-all-done = f32[1,1,64,2304]{3,0,1,2:T(1,128)S(1)} async-done(((f32[1,1,64,2304]{3,0,1,2:T(1,128)}), f32[1,1,64,2304]{3,0,1,2:T(1,128)S(1)}, u32[]{:S(2)}, u32[]{:S(2)}) %all-to-all-start) | async-done | bytes 589856 | tf_op jit(solution)/shard_map/all_to_all | solution.py:296
  23.4 0.0 copy-start
  23.4 0.8 %copy-done = f32[1,1,64,2304]{3,0,1,2:T(1,128)} copy-done((f32[1,1,64,2304]{3,0,1,2:T(1,128)}, f32[1,1,64,2304]{3,0,1,2:T(1,128)S(1)}, u32[]{:S(2)}) %copy-start) | copy-done | bytes 589848
  24.2 3.5 %shard_map.114 = (f32[1,7,64]{2,1,0:T(8,128)}, f32[7,1,1,64]{3,2,1,0:T(1,128)}) custom-call(s32[1]{0:T(128)} %bitcast.off_ref, s32[1]{0:T(128)S(6)} %copy.16.limit_ref, f32[1,64,1,2304]{3,2,1,0:T(1,128)} %bitcast.10, f32[64,64]{1,0:T(8,128)} %constant.16.clone.entry_ref, f32[64,64]{1,0:T(8,128)} %constant.17.clone.mid_ref.leave_ref, ...), custom_call_target="tpu_custom_call" | custom-call | tf_op jit(solution)/shard_map/pallas_call | solution.py:257
  27.8 0.1 collective-permute-start
  27.9 3.7 %collective-permute-done = f32[7,64]{1,0:T(8,128)S(1)} collective-permute-done((f32[7,64]{1,0:T(8,128)}, f32[7,64]{1,0:T(8,128)S(1)}, u32[]{:S(2)}, u32[]{:S(2)}) %collective-permute-start) | collective-permute-done | bytes 1824 | tf_op jit(solution)/shard_map/ppermute | solution.py:307
  31.6 0.7 %bitcast_add_fusion = f32[7,64]{1,0:T(8,128)S(1)} fusion(f32[7,64]{1,0:T(8,128)S(1)} %collective-permute-done, f32[1,7,64]{2,1,0:T(8,128)} %get-tuple-element.5), kind=kLoop, calls=%fused_computation.1 | loop fusion | flops 448 | bytes 5376 | tf_op jit(solution)/shard_map/add | solution.py:307
  32.3 0.0 copy-start.1
  32.3 3.3 %collective-permute-start.1 = (f32[7,64]{1,0:T(8,128)S(1)}, f32[7,64]{1,0:T(8,128)S(1)}, u32[]{:S(2)}, u32[]{:S(2)}) collective-permute-start(f32[7,64]{1,0:T(8,128)S(1)} %bitcast_add_fusion), channel_id=1, source_target_pairs={{0,2},{1,3},{2,0},{3,1},{4,6},{5,7},{6,4},{7,5},{8,10},{9,11},{10,... | collective-permute-start | bytes 5384 | tf_op jit(solution)/shard_map/ppermute | solution.py:307
  35.6 1.6 %collective-permute-done.1 = f32[7,64]{1,0:T(8,128)S(1)} collective-permute-done((f32[7,64]{1,0:T(8,128)S(1)}, f32[7,64]{1,0:T(8,128)S(1)}, u32[]{:S(2)}, u32[]{:S(2)}) %collective-permute-start.1) | collective-permute-done | bytes 1824 | tf_op jit(solution)/shard_map/ppermute | solution.py:307
  37.1 5.5 %collective-permute-start.2 = (f32[7,64]{1,0:T(8,128)S(1)}, f32[7,64]{1,0:T(8,128)S(1)}, u32[]{:S(2)}, u32[]{:S(2)}) collective-permute-start(f32[7,64]{1,0:T(8,128)S(1)} %add.10), channel_id=1, source_target_pairs={{0,7},{1,6},{2,5},{3,4},{4,3},{5,2},{6,1},{7,0},{8,15},{9,14},{10,... | collective-permute-start | bytes 5384 | tf_op jit(solution)/shard_map/ppermute | solution.py:307
  42.6 1.6 %collective-permute-done.2 = f32[7,64]{1,0:T(8,128)S(1)} collective-permute-done((f32[7,64]{1,0:T(8,128)S(1)}, f32[7,64]{1,0:T(8,128)S(1)}, u32[]{:S(2)}, u32[]{:S(2)}) %collective-permute-start.2) | collective-permute-done | bytes 1824 | tf_op jit(solution)/shard_map/ppermute | solution.py:307
  44.2 0.0 copy-done.1
  44.2 0.6 %copy.14 = f32[1,7,64]{2,0,1:T(1,128)} copy(f32[1,7,64]{2,1,0:T(8,128)S(1)} %bitcast_subtract_fusion) | data formatting | bytes 3584
  (2 shorter events, 0.0 us)
Async XLA Ops:
  4.3 19.1 %all-to-all-start = ((f32[1,1,64,2304]{3,0,1,2:T(1,128)}), f32[1,1,64,2304]{3,0,1,2:T(1,128)S(1)}, u32[]{:S(2)}, u32[]{:S(2)}) async-start(f32[1,1,64,2304]{3,0,1,2:T(1,128)} %bitcast.11), calls=%async_computation | async-start | bytes 1179648 | tf_op jit(solution)/shard_map/all_to_all | solution.py:296
  23.4 0.8 %copy-start = (f32[1,1,64,2304]{3,0,1,2:T(1,128)}, f32[1,1,64,2304]{3,0,1,2:T(1,128)S(1)}, u32[]{:S(2)}) copy-start(f32[1,1,64,2304]{3,0,1,2:T(1,128)S(1)} %all-to-all-done) | copy-start | bytes 1769476
  27.8 3.8 %collective-permute-start = (f32[7,64]{1,0:T(8,128)}, f32[7,64]{1,0:T(8,128)S(1)}, u32[]{:S(2)}, u32[]{:S(2)}) collective-permute-start(f32[7,64]{1,0:T(8,128)} %bitcast.12), channel_id=1, source_target_pairs={{0,1},{1,0},{2,3},{3,2},{4,5},{5,4},{6,7},{7,6},{8,9},{9,8},{10,11... | collective-permute-start | bytes 5384 | tf_op jit(solution)/shard_map/ppermute | solution.py:307
  32.3 11.9 %copy-start.1 = (f32[1,7,64]{2,1,0:T(8,128)S(1)}, f32[1,7,64]{2,1,0:T(8,128)}, u32[]{:S(2)}) copy-start(f32[1,7,64]{2,1,0:T(8,128)} %get-tuple-element.5) | copy-start | bytes 5380
  32.3 4.9 %collective-permute-start.1 = (f32[7,64]{1,0:T(8,128)S(1)}, f32[7,64]{1,0:T(8,128)S(1)}, u32[]{:S(2)}, u32[]{:S(2)}) collective-permute-start(f32[7,64]{1,0:T(8,128)S(1)} %bitcast_add_fusion), channel_id=1, source_target_pairs={{0,2},{1,3},{2,0},{3,1},{4,6},{5,7},{6,4},{7,5},{8,10},{9,11},{10,... | collective-permute-start | bytes 5384 | tf_op jit(solution)/shard_map/ppermute | solution.py:307
  37.1 7.1 %collective-permute-start.2 = (f32[7,64]{1,0:T(8,128)S(1)}, f32[7,64]{1,0:T(8,128)S(1)}, u32[]{:S(2)}, u32[]{:S(2)}) collective-permute-start(f32[7,64]{1,0:T(8,128)S(1)} %add.10), channel_id=1, source_target_pairs={{0,7},{1,6},{2,5},{3,4},{4,3},{5,2},{6,1},{7,0},{8,15},{9,14},{10,... | collective-permute-start | bytes 5384 | tf_op jit(solution)/shard_map/ppermute | solution.py:307

commit v16 on v14

--- a/solution.py
+++ b/solution.py
@@ -289,12 +289,9 @@
     peak_snr = merge_tree(series, position * per_dev, tail_len, dm_limit)
     beam_total = jnp.sum(peak_snr, axis=0)
     beam_count = lax.axis_size("beam")
-    for level_bit in range(beam_count.bit_length() - 1):
-        span = 1 << level_bit
-        if 2 * span == beam_count:
-            pairs = [(i, beam_count - 1 - i) for i in range(beam_count)]
-        else:
-            pairs = [(i, i ^ span) for i in range(beam_count)]
+    spans = [beam_count - 1] + [1 << b for b in range(beam_count.bit_length() - 2)]
+    for span in spans:
+        pairs = [(i, i ^ span) for i in range(beam_count)]
         beam_total = beam_total + lax.ppermute(beam_total, "beam", pairs)
     excess_snr = peak_snr - beam_total[None] / (beams_dev * lax.axis_size("beam"))
     return (peak_snr, excess_snr)

time: 45.1 us -> 45.1 us (level)
  waiting for transfers between devices: 17.4 us -> 19.7 us
  starting transfers between devices: 16.2 us -> 13.9 us
    ppermute x3, starting transfers between devices: 8.88 us -> 6.62 us  [local(): beam_total = beam_total + lax.ppermute(beam_total, 'beam', pairs)]
    ppermute x3, waiting for transfers between devices: 6.29 us -> 8.54 us  [local(): beam_total = beam_total + lax.ppermute(beam_total, 'beam', pairs)]
where the time goes in v16:
time: 45.1 us; the launch traced here: 44.8 us
  waiting for transfers between devices  19.7 us (44%)
  starting transfers between devices  13.9 us (31%)
  Pallas kernels  6.57 us (15%)
  local copies, waits for them, and re-layouts  1.99 us (4%)
  between operations  1.94 us (4%)
  other arithmetic  0.7 us (2%)
    all_to_all x1, waiting for transfers between devices, local(): lax.all_to_all(series, 'freq', split_axis=2, concat_axis=1, tiled=True)  11.2 us
    ppermute x3, waiting for transfers between devices, local(): beam_total = beam_total + lax.ppermute(beam_total, 'beam', pairs)  8.54 us
    all_to_all x1, starting transfers between devices, local(): lax.all_to_all(series, 'freq', split_axis=2, concat_axis=1, tiled=True)  7.32 us
    ppermute x3, starting transfers between devices, local(): beam_total = beam_total + lax.ppermute(beam_total, 'beam', pairs)  6.62 us
    pallas_call x1, Pallas kernels, merge_tree(): pl.pallas_call(body, grid=(beams_dev,), in_specs=[pl.BlockSpec(memory_spa...  3.53 us
    pallas_call x1, Pallas kernels, local_tree(): pl.pallas_call(body, grid=(beams_dev,), in_specs=[pl.BlockSpec(memory_spa...  3.04 us
    unnamed x6, local copies, waits for them, and re-layouts  1.99 us
  transfers between devices with their start and end apart: 4, of which 4 were waited for; matrix products, arithmetic and copies ran while one was open for 1% of the time, Pallas kernels for 0%

profile of v16, /device:TPU:32, one launch (start us, length us, event | category | flops | bytes accessed | tf_op | source)
XLA Modules:
  0.0 44.8 jit_solution(6833047941815036174)
XLA Ops:
  1.3 3.0 %shard_map.113 = f32[1,64,1,2304]{3,2,1,0:T(1,128)} custom-call(s32[1]{0:T(128)S(6)} %copy.17.count_ref, bf16[1,64,2048]{2,1,0:T(8,128)(2,1)} %tail_ref.1, bf16[1,64,256]{2,1,0:T(8,128)(2,1)} %block_ref.1, f32[64,64]{1,0:T(8,128)} %constant.16.clone.entry_ref, f32[64,64]{1,0:T(8,128)} %constant.17.clone.mid_ref.leave_ref, ...), custom_call_target="tpu_custom_call" | custom-call | tf_op jit(solution)/shard_map/pallas_call | solution.py:196
  4.3 7.3 %all-to-all-start = ((f32[1,1,64,2304]{3,0,1,2:T(1,128)}), f32[1,1,64,2304]{3,0,1,2:T(1,128)S(1)}, u32[]{:S(2)}, u32[]{:S(2)}) async-start(f32[1,1,64,2304]{3,0,1,2:T(1,128)} %bitcast.10), calls=%async_computation | async-start | bytes 1179648 | tf_op jit(solution)/shard_map/all_to_all | solution.py:287
  12.3 11.2 %all-to-all-done = f32[1,1,64,2304]{3,0,1,2:T(1,128)S(1)} async-done(((f32[1,1,64,2304]{3,0,1,2:T(1,128)}), f32[1,1,64,2304]{3,0,1,2:T(1,128)S(1)}, u32[]{:S(2)}, u32[]{:S(2)}) %all-to-all-start) | async-done | bytes 589856 | tf_op jit(solution)/shard_map/all_to_all | solution.py:287
  23.4 0.0 copy-start
  23.5 0.8 %copy-done = f32[1,1,64,2304]{3,0,1,2:T(1,128)} copy-done((f32[1,1,64,2304]{3,0,1,2:T(1,128)}, f32[1,1,64,2304]{3,0,1,2:T(1,128)S(1)}, u32[]{:S(2)}) %copy-start) | copy-done | bytes 589848
  24.3 3.5 %shard_map.114 = f32[1,7,64]{2,1,0:T(8,128)} custom-call(s32[1]{0:T(128)} %bitcast.off_ref, s32[1]{0:T(128)S(6)} %copy.18.limit_ref, f32[1,64,1,2304]{3,2,1,0:T(1,128)} %bitcast.9, f32[64,64]{1,0:T(8,128)} %constant.16.clone.entry_ref, f32[64,64]{1,0:T(8,128)} %constant.17.clone.mid_ref.leave_ref, f32[64,64]{1,0:T(8,128)} %constant.17.clone.mid_ref.leave_ref), custom_call_target="tpu_custom_call" | custom-call | tf_op jit(solution)/shard_map/pallas_call | solution.py:254
  27.8 5.8 %collective-permute-start = (f32[7,64]{1,0:T(8,128)}, f32[7,64]{1,0:T(8,128)S(1)}, u32[]{:S(2)}, u32[]{:S(2)}) collective-permute-start(f32[7,64]{1,0:T(8,128)} %bitcast.11), channel_id=1, source_target_pairs={{0,7},{1,6},{2,5},{3,4},{4,3},{5,2},{6,1},{7,0},{8,15},{9,14},{10,... | collective-permute-start | bytes 5384 | tf_op jit(solution)/shard_map/ppermute | solution.py:295
  33.7 1.8 %collective-permute-done = f32[7,64]{1,0:T(8,128)S(1)} collective-permute-done((f32[7,64]{1,0:T(8,128)}, f32[7,64]{1,0:T(8,128)S(1)}, u32[]{:S(2)}, u32[]{:S(2)}) %collective-permute-start) | collective-permute-done | bytes 1824 | tf_op jit(solution)/shard_map/ppermute | solution.py:295
  35.4 0.7 %bitcast_add_fusion = f32[7,64]{1,0:T(8,128)S(1)} fusion(f32[7,64]{1,0:T(8,128)S(1)} %collective-permute-done, f32[1,7,64]{2,1,0:T(8,128)} %shard_map.114), kind=kLoop, calls=%fused_computation.1 | loop fusion | flops 448 | bytes 5376 | tf_op jit(solution)/shard_map/add | solution.py:295
  36.1 0.0 copy-start.1
  36.1 0.1 collective-permute-start.1
  36.3 3.5 %collective-permute-done.1 = f32[7,64]{1,0:T(8,128)S(1)} collective-permute-done((f32[7,64]{1,0:T(8,128)S(1)}, f32[7,64]{1,0:T(8,128)S(1)}, u32[]{:S(2)}, u32[]{:S(2)}) %collective-permute-start.1) | collective-permute-done | bytes 1824 | tf_op jit(solution)/shard_map/ppermute | solution.py:295
  39.7 0.7 %collective-permute-start.2 = (f32[7,64]{1,0:T(8,128)S(1)}, f32[7,64]{1,0:T(8,128)S(1)}, u32[]{:S(2)}, u32[]{:S(2)}) collective-permute-start(f32[7,64]{1,0:T(8,128)S(1)} %add.10), channel_id=1, source_target_pairs={{0,2},{1,3},{2,0},{3,1},{4,6},{5,7},{6,4},{7,5},{8,10},{9,11},{10,... | collective-permute-start | bytes 5384 | tf_op jit(solution)/shard_map/ppermute | solution.py:295
  40.4 0.0 copy-done.1
  40.4 0.6 %copy.15 = f32[1,7,64]{2,0,1:T(1,128)} copy(f32[1,7,64]{2,1,0:T(8,128)S(1)} %copy-done.1) | data formatting | bytes 3584
  41.0 3.3 %collective-permute-done.2 = f32[7,64]{1,0:T(8,128)S(1)} collective-permute-done((f32[7,64]{1,0:T(8,128)S(1)}, f32[7,64]{1,0:T(8,128)S(1)}, u32[]{:S(2)}, u32[]{:S(2)}) %collective-permute-start.2) | collective-permute-done | bytes 1824 | tf_op jit(solution)/shard_map/ppermute | solution.py:295
  44.3 0.6 %copy.16 = f32[1,7,64]{2,0,1:T(1,128)} copy(f32[1,7,64]{2,1,0:T(8,128)S(1)} %bitcast_subtract_fusion) | data formatting | bytes 3584
  (2 shorter events, 0.0 us)
Async XLA Ops:
  4.3 19.1 %all-to-all-start = ((f32[1,1,64,2304]{3,0,1,2:T(1,128)}), f32[1,1,64,2304]{3,0,1,2:T(1,128)S(1)}, u32[]{:S(2)}, u32[]{:S(2)}) async-start(f32[1,1,64,2304]{3,0,1,2:T(1,128)} %bitcast.10), calls=%async_computation | async-start | bytes 1179648 | tf_op jit(solution)/shard_map/all_to_all | solution.py:287
  23.4 0.8 %copy-start = (f32[1,1,64,2304]{3,0,1,2:T(1,128)}, f32[1,1,64,2304]{3,0,1,2:T(1,128)S(1)}, u32[]{:S(2)}) copy-start(f32[1,1,64,2304]{3,0,1,2:T(1,128)S(1)} %all-to-all-done) | copy-start | bytes 1769476
  27.8 7.6 %collective-permute-start = (f32[7,64]{1,0:T(8,128)}, f32[7,64]{1,0:T(8,128)S(1)}, u32[]{:S(2)}, u32[]{:S(2)}) collective-permute-start(f32[7,64]{1,0:T(8,128)} %bitcast.11), channel_id=1, source_target_pairs={{0,7},{1,6},{2,5},{3,4},{4,3},{5,2},{6,1},{7,0},{8,15},{9,14},{10,... | collective-permute-start | bytes 5384 | tf_op jit(solution)/shard_map/ppermute | solution.py:295
  36.1 4.3 %copy-start.1 = (f32[1,7,64]{2,1,0:T(8,128)S(1)}, f32[1,7,64]{2,1,0:T(8,128)}, u32[]{:S(2)}) copy-start(f32[1,7,64]{2,1,0:T(8,128)} %shard_map.114) | copy-start | bytes 5380
  36.1 3.6 %collective-permute-start.1 = (f32[7,64]{1,0:T(8,128)S(1)}, f32[7,64]{1,0:T(8,128)S(1)}, u32[]{:S(2)}, u32[]{:S(2)}) collective-permute-start(f32[7,64]{1,0:T(8,128)S(1)} %bitcast_add_fusion), channel_id=1, source_target_pairs={{0,1},{1,0},{2,3},{3,2},{4,5},{5,4},{6,7},{7,6},{8,9},{9,8},{10,11... | collective-permute-start | bytes 5384 | tf_op jit(solution)/shard_map/ppermute | solution.py:295
  39.7 4.5 %collective-permute-start.2 = (f32[7,64]{1,0:T(8,128)S(1)}, f32[7,64]{1,0:T(8,128)S(1)}, u32[]{:S(2)}, u32[]{:S(2)}) collective-permute-start(f32[7,64]{1,0:T(8,128)S(1)} %add.10), channel_id=1, source_target_pairs={{0,2},{1,3},{2,0},{3,1},{4,6},{5,7},{6,4},{7,5},{8,10},{9,11},{10,... | collective-permute-start | bytes 5384 | tf_op jit(solution)/shard_map/ppermute | solution.py:295

commit v17 on v16

--- a/solution.py
+++ b/solution.py
@@ -228,6 +228,8 @@
         top = jnp.max(boxcar[:, 128:], axis=1, keepdims=True)
         ratio = (top - width_now * average) / (np.sqrt(np.float32(width_now)) * deviation)
         table = jnp.where(lane_ids == width_bit, ratio, table)
+    if trials == TILE * TILE:
+        return swap_blocks(table, TILE).T[:8]
     return permute_rows(leave, table).T[:8]
 
 

time: 45.1 us -> 45.3 us (level)
  no operation moved by 1% of the time
where the time goes in v17:
time: 45.3 us; the launch traced here: 45 us
  waiting for transfers between devices  19.7 us (43%)
  starting transfers between devices  13.9 us (31%)
  Pallas kernels  6.72 us (15%)
  local copies, waits for them, and re-layouts  1.99 us (4%)
  between operations  1.94 us (4%)
  other arithmetic  0.7 us (2%)
    all_to_all x1, waiting for transfers between devices, local(): lax.all_to_all(series, 'freq', split_axis=2, concat_axis=1, tiled=True)  11.2 us
    ppermute x3, waiting for transfers between devices, local(): beam_total = beam_total + lax.ppermute(beam_total, 'beam', pairs)  8.54 us
    all_to_all x1, starting transfers between devices, local(): lax.all_to_all(series, 'freq', split_axis=2, concat_axis=1, tiled=True)  7.32 us
    ppermute x3, starting transfers between devices, local(): beam_total = beam_total + lax.ppermute(beam_total, 'beam', pairs)  6.62 us
    pallas_call x1, Pallas kernels, merge_tree(): pl.pallas_call(body, grid=(beams_dev,), in_specs=[pl.BlockSpec(memory_spa...  3.69 us
    pallas_call x1, Pallas kernels, local_tree(): pl.pallas_call(body, grid=(beams_dev,), in_specs=[pl.BlockSpec(memory_spa...  3.04 us
    unnamed x6, local copies, waits for them, and re-layouts  1.99 us
  transfers between devices with their start and end apart: 4, of which 4 were waited for; matrix products, arithmetic and copies ran while one was open for 1% of the time, Pallas kernels for 0%

profile of v17, /device:TPU:32, one launch (start us, length us, event | category | flops | bytes accessed | tf_op | source)
XLA Modules:
  0.0 45.0 jit_solution(16192371900290426668)
XLA Ops:
  1.3 3.0 %shard_map.113 = f32[1,64,1,2304]{3,2,1,0:T(1,128)} custom-call(s32[1]{0:T(128)S(6)} %copy.17.count_ref, bf16[1,64,2048]{2,1,0:T(8,128)(2,1)} %tail_ref.1, bf16[1,64,256]{2,1,0:T(8,128)(2,1)} %block_ref.1, f32[64,64]{1,0:T(8,128)} %constant.16.clone.entry_ref, f32[64,64]{1,0:T(8,128)} %constant.17.clone.mid_ref.leave_ref, ...), custom_call_target="tpu_custom_call" | custom-call | tf_op jit(solution)/shard_map/pallas_call | solution.py:196
  4.3 7.3 %all-to-all-start = ((f32[1,1,64,2304]{3,0,1,2:T(1,128)}), f32[1,1,64,2304]{3,0,1,2:T(1,128)S(1)}, u32[]{:S(2)}, u32[]{:S(2)}) async-start(f32[1,1,64,2304]{3,0,1,2:T(1,128)} %bitcast.10), calls=%async_computation | async-start | bytes 1179648 | tf_op jit(solution)/shard_map/all_to_all | solution.py:289
  12.3 11.2 %all-to-all-done = f32[1,1,64,2304]{3,0,1,2:T(1,128)S(1)} async-done(((f32[1,1,64,2304]{3,0,1,2:T(1,128)}), f32[1,1,64,2304]{3,0,1,2:T(1,128)S(1)}, u32[]{:S(2)}, u32[]{:S(2)}) %all-to-all-start) | async-done | bytes 589856 | tf_op jit(solution)/shard_map/all_to_all | solution.py:289
  23.4 0.0 copy-start
  23.5 0.8 %copy-done = f32[1,1,64,2304]{3,0,1,2:T(1,128)} copy-done((f32[1,1,64,2304]{3,0,1,2:T(1,128)}, f32[1,1,64,2304]{3,0,1,2:T(1,128)S(1)}, u32[]{:S(2)}) %copy-start) | copy-done | bytes 589848
  24.3 3.7 %shard_map.114 = f32[1,7,64]{2,1,0:T(8,128)} custom-call(s32[1]{0:T(128)} %bitcast.off_ref, s32[1]{0:T(128)S(6)} %copy.18.limit_ref, f32[1,64,1,2304]{3,2,1,0:T(1,128)} %bitcast.9, f32[64,64]{1,0:T(8,128)} %constant.16.clone.entry_ref, f32[64,64]{1,0:T(8,128)} %constant.17.clone.mid_ref.leave_ref, f32[64,64]{1,0:T(8,128)} %constant.17.clone.mid_ref.leave_ref), custom_call_target="tpu_custom_call" | custom-call | tf_op jit(solution)/shard_map/pallas_call | solution.py:256
  28.0 5.8 %collective-permute-start = (f32[7,64]{1,0:T(8,128)}, f32[7,64]{1,0:T(8,128)S(1)}, u32[]{:S(2)}, u32[]{:S(2)}) collective-permute-start(f32[7,64]{1,0:T(8,128)} %bitcast.11), channel_id=1, source_target_pairs={{0,7},{1,6},{2,5},{3,4},{4,3},{5,2},{6,1},{7,0},{8,15},{9,14},{10,... | collective-permute-start | bytes 5384 | tf_op jit(solution)/shard_map/ppermute | solution.py:297
  33.8 1.8 %collective-permute-done = f32[7,64]{1,0:T(8,128)S(1)} collective-permute-done((f32[7,64]{1,0:T(8,128)}, f32[7,64]{1,0:T(8,128)S(1)}, u32[]{:S(2)}, u32[]{:S(2)}) %collective-permute-start) | collective-permute-done | bytes 1824 | tf_op jit(solution)/shard_map/ppermute | solution.py:297
  35.6 0.7 %bitcast_add_fusion = f32[7,64]{1,0:T(8,128)S(1)} fusion(f32[7,64]{1,0:T(8,128)S(1)} %collective-permute-done, f32[1,7,64]{2,1,0:T(8,128)} %shard_map.114), kind=kLoop, calls=%fused_computation.1 | loop fusion | flops 448 | bytes 5376 | tf_op jit(solution)/shard_map/add | solution.py:297
  36.3 0.0 copy-start.1
  36.3 0.1 collective-permute-start.1
  36.4 3.5 %collective-permute-done.1 = f32[7,64]{1,0:T(8,128)S(1)} collective-permute-done((f32[7,64]{1,0:T(8,128)S(1)}, f32[7,64]{1,0:T(8,128)S(1)}, u32[]{:S(2)}, u32[]{:S(2)}) %collective-permute-start.1) | collective-permute-done | bytes 1824 | tf_op jit(solution)/shard_map/ppermute | solution.py:297
  39.9 0.7 %collective-permute-start.2 = (f32[7,64]{1,0:T(8,128)S(1)}, f32[7,64]{1,0:T(8,128)S(1)}, u32[]{:S(2)}, u32[]{:S(2)}) collective-permute-start(f32[7,64]{1,0:T(8,128)S(1)} %add.10), channel_id=1, source_target_pairs={{0,2},{1,3},{2,0},{3,1},{4,6},{5,7},{6,4},{7,5},{8,10},{9,11},{10,... | collective-permute-start | bytes 5384 | tf_op jit(solution)/shard_map/ppermute | solution.py:297
  40.6 0.0 copy-done.1
  40.6 0.6 %copy.15 = f32[1,7,64]{2,0,1:T(1,128)} copy(f32[1,7,64]{2,1,0:T(8,128)S(1)} %copy-done.1) | data formatting | bytes 3584
  41.1 3.3 %collective-permute-done.2 = f32[7,64]{1,0:T(8,128)S(1)} collective-permute-done((f32[7,64]{1,0:T(8,128)S(1)}, f32[7,64]{1,0:T(8,128)S(1)}, u32[]{:S(2)}, u32[]{:S(2)}) %collective-permute-start.2) | collective-permute-done | bytes 1824 | tf_op jit(solution)/shard_map/ppermute | solution.py:297
  44.4 0.6 %copy.16 = f32[1,7,64]{2,0,1:T(1,128)} copy(f32[1,7,64]{2,1,0:T(8,128)S(1)} %bitcast_subtract_fusion) | data formatting | bytes 3584
  (2 shorter events, 0.0 us)
Async XLA Ops:
  4.3 19.1 %all-to-all-start = ((f32[1,1,64,2304]{3,0,1,2:T(1,128)}), f32[1,1,64,2304]{3,0,1,2:T(1,128)S(1)}, u32[]{:S(2)}, u32[]{:S(2)}) async-start(f32[1,1,64,2304]{3,0,1,2:T(1,128)} %bitcast.10), calls=%async_computation | async-start | bytes 1179648 | tf_op jit(solution)/shard_map/all_to_all | solution.py:289
  23.4 0.8 %copy-start = (f32[1,1,64,2304]{3,0,1,2:T(1,128)}, f32[1,1,64,2304]{3,0,1,2:T(1,128)S(1)}, u32[]{:S(2)}) copy-start(f32[1,1,64,2304]{3,0,1,2:T(1,128)S(1)} %all-to-all-done) | copy-start | bytes 1769476
  28.0 7.6 %collective-permute-start = (f32[7,64]{1,0:T(8,128)}, f32[7,64]{1,0:T(8,128)S(1)}, u32[]{:S(2)}, u32[]{:S(2)}) collective-permute-start(f32[7,64]{1,0:T(8,128)} %bitcast.11), channel_id=1, source_target_pairs={{0,7},{1,6},{2,5},{3,4},{4,3},{5,2},{6,1},{7,0},{8,15},{9,14},{10,... | collective-permute-start | bytes 5384 | tf_op jit(solution)/shard_map/ppermute | solution.py:297
  36.3 4.3 %copy-start.1 = (f32[1,7,64]{2,1,0:T(8,128)S(1)}, f32[1,7,64]{2,1,0:T(8,128)}, u32[]{:S(2)}) copy-start(f32[1,7,64]{2,1,0:T(8,128)} %shard_map.114) | copy-start | bytes 5380
  36.3 3.6 %collective-permute-start.1 = (f32[7,64]{1,0:T(8,128)S(1)}, f32[7,64]{1,0:T(8,128)S(1)}, u32[]{:S(2)}, u32[]{:S(2)}) collective-permute-start(f32[7,64]{1,0:T(8,128)S(1)} %bitcast_add_fusion), channel_id=1, source_target_pairs={{0,1},{1,0},{2,3},{3,2},{4,5},{5,4},{6,7},{7,6},{8,9},{9,8},{10,11... | collective-permute-start | bytes 5384 | tf_op jit(solution)/shard_map/ppermute | solution.py:297
  39.9 4.5 %collective-permute-start.2 = (f32[7,64]{1,0:T(8,128)S(1)}, f32[7,64]{1,0:T(8,128)S(1)}, u32[]{:S(2)}, u32[]{:S(2)}) collective-permute-start(f32[7,64]{1,0:T(8,128)S(1)} %add.10), channel_id=1, source_target_pairs={{0,2},{1,3},{2,0},{3,1},{4,6},{5,7},{6,4},{7,5},{8,10},{9,11},{10,... | collective-permute-start | bytes 5384 | tf_op jit(solution)/shard_map/ppermute | solution.py:297
